TPU v7x, 512 devices: a whole 4x4x16 slice. The times are simulated.
512 devices in a mesh: space: 32 (over x, y, z_hi), tm: 16 (over z_lo, core).
Axes of the slice: x: 4, y: 4, z: 16 (z_hi: 2, z_lo: 8; z = z_hi * 8 + z_lo), core: 2. Of those that a mesh axis runs over, the one named last changes fastest.
Arguments:
- lattice_field: float32 [64, 128, 2048], P('tm', 'space'), may hold values from -6 to 6
- parity: int32 [16, 32, 128], P('tm', 'space'), may hold values from 0 to 1
- block_list: int32 [16, 8], replicated, may hold values from 0 to 15, as said below
- w_embed: bfloat16 [256, 768], replicated, may hold values from -0.5 to 0.5
- b_embed: float32 [768], replicated, may hold values from -3 to 3
- gain_in: float32 [768], replicated, may hold values from 0.5 to 1.5
- w_qkv: bfloat16 [768, 2304], replicated, may hold values from -4 to 4
- gain_out: float32 [768], replicated, may hold values from 0.5 to 1.5
- w_head: bfloat16 [768, 512], replicated, may hold values from -0.21875 to 0.21875
- b_head: float32 [512], replicated, may hold values from -3 to 3
Outputs:
- new_field: float32 [64, 128, 2048], P('tm', 'space')
- action_density: float32 [64, 128, 2048], P('tm', 'space')
- time_link: float32 [64, 128, 2048], P('tm', 'space')
- slab_link: float32 [64, 128, 2048], P('tm', 'space')
- totals: float32 [2], replicated
Inputs may be any that keep to these rules, and one draw needn't show every extreme that they name: `block_list`: row b lists 8 different block numbers, b among them.
All inputs are finite; a program needn't handle non-finite values.
Results may differ from a plain program's by a relative error of at most 0.006.
Values may be sent and summed in bfloat16 or wider, within the bound.
No kernel may reach another device: no remote copies, remote signals or barrier semaphores. Data moves between devices by JAX's collectives and lax.ppermute only.
A program may use at most 64 MiB of HBM per device.

v0:
```python
import math

import jax
import jax.numpy as jnp
from jax import lax
from jax.sharding import PartitionSpec as P

P_SIZE = 4
D = 768
HEADS = 12
HS = 64
LY = 32
LZ = 64
BLK = 128


hopping = 0.2
quartic = 0.5
epsilon = 1e-05
log_two_pi = math.log(2.0 * math.pi)
floor_score = -1e30


def shifted(x, axis, by):
    length = lax.axis_size(axis)
    return lax.ppermute(x, axis, [(i, (i + by) % length) for i in range(length)])


def layer_norm(values, gain_vec):
    centre = values - jnp.mean(values, axis=-1, keepdims=True)
    spread = jnp.mean(centre * centre, axis=-1, keepdims=True)
    return centre * lax.rsqrt(spread + epsilon) * gain_vec


def site_parity(patch_side):
    positions = jnp.arange(patch_side**4, dtype=jnp.int32)
    return (
        positions // patch_side**3
        + positions // patch_side**2 % patch_side
        + positions // patch_side % patch_side
        + positions % patch_side
    ) % 2


def embed_rows(frozen_in, w_embed, b_embed, gain_in):
    embedded = jnp.dot(frozen_in, w_embed, preferred_element_type=jnp.float32) + b_embed
    return (embedded, layer_norm(embedded, gain_in).astype(jnp.bfloat16))


def attend(carry_in, queries, key_part, value_part, first_key, block_rows):
    running_max, running_sum, running_out = carry_in
    key_rows = key_part.shape[0]
    key_block = (first_key + jnp.arange(key_rows, dtype=jnp.int32)) // BLK
    listed = jnp.any(block_rows[:, :, None] == key_block[None, None, :], axis=1)
    allowed = jnp.repeat(listed, BLK, axis=0)[None]
    query_heads = queries.reshape(queries.shape[0], HEADS, HS)
    scores = jnp.einsum(
        "qhd,khd->hqk",
        query_heads,
        key_part.reshape(key_rows, HEADS, HS),
        preferred_element_type=jnp.float32,
    ) * HS ** (-0.5)
    masked = jnp.where(allowed, scores, floor_score)
    new_max = jnp.maximum(running_max, jnp.max(masked, axis=2))
    exp_scores = jnp.where(allowed, jnp.exp(scores - new_max[:, :, None]), 0.0)
    factor = jnp.exp(running_max - new_max)
    running_sum = running_sum * factor + jnp.sum(exp_scores, axis=2)
    product = jnp.einsum(
        "hqk,khd->hqd",
        exp_scores.astype(jnp.bfloat16),
        value_part.reshape(key_rows, HEADS, HS),
        preferred_element_type=jnp.float32,
    )
    running_out = running_out * factor[:, :, None] + product
    return (new_max, running_sum, running_out)


def fold_rows(carry_in, pieces_in, make_pair, queries, block_rows):
    row_total = pieces_in[0].shape[0]
    pieces_split = tuple(
        (
            piece_arr.reshape((row_total // BLK, BLK) + piece_arr.shape[1:])
            for piece_arr in pieces_in
        )
    )

    def visit_block(carry_now, item_pair):
        position, block_parts = item_pair
        first_key = position * BLK
        block_id = first_key // BLK
        needed = jnp.any(block_rows == block_id)

        def compute_block(carry_here):
            key_part, value_part = make_pair(block_parts)
            return attend(carry_here, queries, key_part, value_part, first_key, block_rows)

        def skip_block(carry_here):
            return carry_here

        return (lax.cond(needed, compute_block, skip_block, carry_now), None)

    carry_out, _ = lax.scan(
        visit_block, carry_in, (jnp.arange(row_total // BLK, dtype=jnp.int32), pieces_split)
    )
    return carry_out


def shards(
    lattice_field, parity, block_list, w_embed, b_embed, gain_in, w_qkv, gain_out, w_head, b_head
):
    tokens_dev = LY // P_SIZE * (LZ // P_SIZE)
    patch_len = P_SIZE**4
    lattice_grid = lattice_field.reshape(
        P_SIZE, P_SIZE, LY // P_SIZE, P_SIZE, LZ // P_SIZE, P_SIZE
    ).transpose(2, 4, 0, 1, 3, 5)
    site_rows = lattice_grid.reshape(tokens_dev, patch_len)
    frozen = site_parity(P_SIZE)[None, :] == parity.reshape(tokens_dev)[:, None]
    frozen_in = jnp.where(frozen, site_rows, 0.0).astype(jnp.bfloat16)
    embedded, normed = embed_rows(frozen_in, w_embed, b_embed, gain_in)
    blocks_dev = tokens_dev // BLK
    block_rows = lax.dynamic_slice_in_dim(
        block_list, lax.axis_index("tm") * blocks_dev, blocks_dev, 0
    )
    start_state = (
        jnp.full((HEADS, tokens_dev), floor_score, jnp.float32),
        jnp.zeros((HEADS, tokens_dev), jnp.float32),
        jnp.zeros((HEADS, tokens_dev, HS), jnp.float32),
    )
    qkv_rows = jnp.dot(normed, w_qkv, preferred_element_type=jnp.float32).astype(jnp.bfloat16)
    queries = qkv_rows[:, :D]

    def from_pair(block_parts):
        return (block_parts[0], block_parts[1])

    result = fold_rows(
        start_state,
        (
            lax.all_gather(qkv_rows[:, D : 2 * D], "tm", axis=0, tiled=True),
            lax.all_gather(qkv_rows[:, 2 * D :], "tm", axis=0, tiled=True),
        ),
        from_pair,
        queries,
        block_rows,
    )
    _, running_sum, running_out = result
    mixed = (running_out / running_sum[:, :, None]).transpose(1, 0, 2).reshape(tokens_dev, D)
    hidden = embedded + mixed
    normed_out = layer_norm(hidden, gain_out).astype(jnp.bfloat16)
    affine = jnp.dot(normed_out, w_head, preferred_element_type=jnp.float32) + b_head
    scale_log = jnp.tanh(affine[:, :patch_len])
    shift_val = affine[:, patch_len:]
    moved = jnp.where(frozen, site_rows, site_rows * jnp.exp(scale_log) + shift_val)
    log_det = jnp.sum(jnp.where(frozen, 0.0, scale_log))
    new_field = (
        moved.reshape(LY // P_SIZE, LZ // P_SIZE, P_SIZE, P_SIZE, P_SIZE, P_SIZE)
        .transpose(2, 3, 0, 4, 1, 5)
        .reshape(P_SIZE, P_SIZE, LY * LZ)
    )
    ahead_time = shifted(new_field[0:1].astype(jnp.bfloat16), "tm", -1).astype(jnp.float32)
    ahead_slab = shifted(new_field[:, 0:1].astype(jnp.bfloat16), "space", -1).astype(jnp.float32)
    next_time_field = jnp.concatenate([new_field[1:], ahead_time], axis=0)
    next_slab_field = jnp.concatenate([new_field[:, 1:], ahead_slab], axis=1)
    cube = new_field.reshape(P_SIZE, P_SIZE, LY, LZ)
    next_y_field = jnp.roll(cube, -1, 2).reshape(P_SIZE, P_SIZE, LY * LZ)
    next_z_field = jnp.roll(cube, -1, 3).reshape(P_SIZE, P_SIZE, LY * LZ)
    neighbours = next_time_field + next_slab_field
    neighbours = neighbours + next_y_field
    neighbours = neighbours + next_z_field
    squared = new_field * new_field
    density = (
        -2.0 * hopping * new_field * neighbours
        + squared
        + quartic * (squared - 1.0) * (squared - 1.0)
    )
    time_link = new_field * next_time_field
    slab_link = new_field * next_slab_field
    local_log = -0.5 * jnp.sum(lattice_field * lattice_field) - log_det
    local_act = jnp.sum(density)
    sum_log, sum_act = lax.psum((local_log, local_act), ("space", "tm"))
    site_count = lattice_field.size * lax.axis_size("space") * lax.axis_size("tm")
    totals = jnp.stack([sum_log / site_count - 0.5 * log_two_pi, sum_act / site_count]).astype(
        jnp.float32
    )
    return (new_field, density, time_link, slab_link, totals)


def solution(mesh):
    in_specs = (
        P("tm", "space", None),
        P("tm", "space", None),
        P(),
        P(),
        P(),
        P(),
        P(),
        P(),
        P(),
        P(),
    )
    out_specs = (
        P("tm", "space", None),
        P("tm", "space", None),
        P("tm", "space", None),
        P("tm", "space", None),
        P(),
    )
    return jax.shard_map(shards, mesh=mesh, in_specs=in_specs, out_specs=out_specs, check_vma=False)
```

profile of v0, /device:TPU:1, one launch (start us, length us, event | category | flops | bytes accessed | tf_op | source)
XLA Modules:
  0.0 584.1 jit_solution(14701347401462404792)
XLA Ops:
  7.3 6.7 %reshape.277 = f32[4,4,8,4,16,4]{5,4,3,2,1,0:T(8,128)} reshape(f32[4,4,2048]{2,1,0:T(4,128)} %param.14) | data formatting | bytes 262144 | tf_op jit(solution)/shard_map/reshape | solution.py:113
  14.0 5.7 copy.50
  32.6 102.8 %all-gather.3.cloned.1.call-done = bf16[2048,768]{1,0:T(8,128)(2,1)} async-done(((bf16[128,768]{1,0:T(8,128)(2,1)}), bf16[2048,768]{1,0:T(8,128)(2,1)}) %all-gather.3.cloned.1.call-update) | async-done | bytes 3145744 | tf_op jit(solution)/shard_map/all_gather | solution.py:138
  135.4 4.6 copy.53
  140.0 101.0 %all-gather.5.cloned.1.call-done = bf16[2048,768]{1,0:T(8,128)(2,1)} async-done(((bf16[128,768]{1,0:T(8,128)(2,1)}), bf16[2048,768]{1,0:T(8,128)(2,1)}) %all-gather.5.cloned.1.call-update) | async-done | bytes 3145744 | tf_op jit(solution)/shard_map/all_gather | solution.py:139
  241.0 4.7 copy.55
  247.1 100.4 %while.16 = (s32[]{:T(128)}, f32[12,128]{1,0:T(8,128)S(1)}, f32[12,128]{1,0:T(8,128)S(1)}, f32[12,128,64]{1,2,0:T(8,128)}, s32[16]{0:T(128)}, /*index=5*/s32[1,8...) while((s32[]{:T(128)}, f32[12,128]{1,0:T(8,128)S(1)}, ...), condition=%wide.region_9.10_spmd, body=%wide.region_2.9_spmd.sunk | while | flops 52304800 | bytes 7768141 | solution.py:102
  268.1 4.5 conditional.2
  301.3 4.5 conditional.2
  309.8 4.5 conditional.2
  322.3 4.5 conditional.2
  334.9 4.5 conditional.2
  360.2 5.4 copy.60
  365.7 5.6 reshape.283
  383.6 9.5 %collective-permute-start.1 = (bf16[4,1,2048]{2,1,0:T(2,128)(2,1)}, bf16[4,1,2048]{2,1,0:T(2,128)(2,1)}, u32[]{:S(2)}, u32[]{:S(2)}) collective-permute-start(bf16[4,1,2048]{2,1,0:T(2,128)(2,1)} %slice.87), channel_id=1, source_target_pairs={{0,496},{16,0},{32,16},{48,32},{64,48},{80,64},{96,80},{112,96},{1... | collective-permute-start | bytes 49160 | tf_op jit(solution)/shard_map/ppermute | solution.py:26
  398.0 9.9 %collective-permute-start = (bf16[1,4,2048]{2,1,0:T(4,128)(2,1)}, bf16[1,4,2048]{2,1,0:T(4,128)(2,1)S(1)}, u32[]{:S(2)}, u32[]{:S(2)}) collective-permute-start(bf16[1,4,2048]{2,1,0:T(4,128)(2,1)} %convert_element_type.46), channel_id=1, source_target_pairs={{0,15},{1,0},{2,1},{3,2},{4,3},{5,4},{6,5},{7,6},{8,7},{9,8},{10,9... | collective-permute-start | bytes 49160 | tf_op jit(solution)/shard_map/ppermute | solution.py:26
  423.1 4.5 reshape.286
  427.6 4.6 copy.61
  432.2 5.7 copy.69
  437.8 5.6 copy.68
  443.5 5.1 reshape.288
  448.6 4.6 copy.66
  469.5 4.6 slice.55
  474.1 98.3 %all-reduce = (f32[]{:T(128)}, f32[]{:T(128)}) all-reduce(f32[]{:T(128)} %fusion.5, f32[]{:T(128)S(6)} %sub.78), channel_id=1, replica_groups=mesh['space'=32,'tm'=16] {'space','tm'}, use_global_device_ids=true, to_apply=%region_16.17 | all-reduce | flops 2 | bytes 16 | tf_op jit(solution)/shard_map/psum | solution.py:179
  (225 shorter events, 169.1 us)
Async XLA Ops:
  7.2 18.5 %copy-start = (bf16[768,2304]{1,0:T(8,128)(2,1)S(1)}, bf16[768,2304]{1,0:T(8,128)(2,1)}, u32[]{:S(2)}) copy-start(bf16[768,2304]{1,0:T(8,128)(2,1)} %param.20) | copy-start | bytes 10616836
  7.2 128.2 %all-gather.3.cloned.1.call-start = ((), (), s32[]{:S(2)}) async-start(), calls=%async_computation | async-start | bytes 3342336 | tf_op jit(solution)/shard_map/all_gather | solution.py:138
  7.2 16.2 %copy-start.6 = (s32[256]{0:T(256)}, s32[256]{0:T(256)S(1)}, u32[]{:S(2)}) copy-start(s32[256]{0:T(256)S(1)} %and_select_fusion.1) | copy-start | bytes 3076
  14.0 9.5 %copy-start.4 = (f32[768]{0:T(1024)S(1)}, f32[768]{0:T(1024)}, u32[]{:S(2)}) copy-start(f32[768]{0:T(1024)} %param.18) | copy-start | bytes 9220
  14.0 9.5 %copy-start.10 = (s32[1,1,128]{2,1,0:T(1,128)S(1)}, s32[1,1,128]{2,1,0:T(1,128)}, u32[]{:S(2)}) copy-start(s32[1,1,128]{2,1,0:T(1,128)} %param.15) | copy-start | bytes 1540
  14.0 11.7 %copy-start.9 = (f32[768]{0:T(1024)S(1)}, f32[768]{0:T(1024)}, u32[]{:S(2)}) copy-start(f32[768]{0:T(1024)} %param.19) | copy-start | bytes 9220
  25.1 2.9 copy-start.8
  27.2 213.8 %all-gather.5.cloned.1.call-start = ((), (), s32[]{:S(2)}) async-start(), calls=%async_computation.1 | async-start | bytes 3342336 | tf_op jit(solution)/shard_map/all_gather | solution.py:139
  251.1 3.3 copy-start.1
  259.6 3.3 copy-start.1
  268.1 3.3 copy-start.1
  271.8 0.8 copy-start.2
  284.7 3.3 copy-start.1
  301.3 3.3 copy-start.1
  305.0 0.8 copy-start.2
  309.8 3.3 copy-start.1
  313.5 0.8 copy-start.2
  322.3 3.4 copy-start.1
  334.9 3.4 copy-start.1
  347.5 5.2 copy-start.5
  347.5 6.6 %copy-start.7 = (s32[256]{0:T(256)S(1)}, s32[256]{0:T(256)}, u32[]{:S(2)}) copy-start(s32[256]{0:T(256)} %copy-done.6) | copy-start | bytes 3076
  349.3 4.9 copy-start.11
  383.6 75.1 %collective-permute-start.1 = (bf16[4,1,2048]{2,1,0:T(2,128)(2,1)}, bf16[4,1,2048]{2,1,0:T(2,128)(2,1)}, u32[]{:S(2)}, u32[]{:S(2)}) collective-permute-start(bf16[4,1,2048]{2,1,0:T(2,128)(2,1)} %slice.87), channel_id=1, source_target_pairs={{0,496},{16,0},{32,16},{48,32},{64,48},{80,64},{96,80},{112,96},{1... | collective-permute-start | bytes 49160 | tf_op jit(solution)/shard_map/ppermute | solution.py:26
  398.0 55.8 %collective-permute-start = (bf16[1,4,2048]{2,1,0:T(4,128)(2,1)}, bf16[1,4,2048]{2,1,0:T(4,128)(2,1)S(1)}, u32[]{:S(2)}, u32[]{:S(2)}) collective-permute-start(bf16[1,4,2048]{2,1,0:T(4,128)(2,1)} %convert_element_type.46), channel_id=1, source_target_pairs={{0,15},{1,0},{2,1},{3,2},{4,3},{5,4},{6,5},{7,6},{8,7},{9,8},{10,9... | collective-permute-start | bytes 49160 | tf_op jit(solution)/shard_map/ppermute | solution.py:26
  (6 other events, 4.6 us)
Sparse Core Ops, SparseCore 0:
  27.3 107.9 all-gather.2
  137.5 103.5 all-gather.4
where the time goes:
time: 587 us; the launch traced here: 584 us
  waiting for transfers between devices  205 us (35%)
  local copies, waits for them, and re-layouts  157 us (27%)
  blocking collectives  98.3 us (17%)
  other arithmetic  49 us (8%)
  loops' own time  22.6 us (4%)
  starting transfers between devices  19.5 us (3%)
  between operations  16.9 us (3%)
  matrix products  16.2 us (3%)
    all_gather x1, waiting for transfers between devices, shards(): lax.all_gather(qkv_rows[:, D:2 * D], 'tm', axis=0, tiled=True)  103 us
    all_gather x1, waiting for transfers between devices, shards(): lax.all_gather(qkv_rows[:, 2 * D:], 'tm', axis=0, tiled=True)  101 us
    psum x1, blocking collectives, shards(): sum_log, sum_act = lax.psum((local_log, local_act), ('space', 'tm'))  98.3 us
    dynamic_slice x24, local copies, waits for them, and re-layouts, fold_rows(): lax.scan(visit_block, carry_in, (jnp.arange(row_total // BLK, dtype=jnp.i...  29.4 us
    another operation x1, loops' own time, fold_rows(): lax.scan(visit_block, carry_in, (jnp.arange(row_total // BLK, dtype=jnp.i...  21.8 us
    reduce_or x16, other arithmetic, visit_block(): needed = jnp.any(block_rows == block_id)  21.6 us
    ppermute x2, starting transfers between devices, shifted(): lax.ppermute(x, axis, [(i, (i + by) % length) for i in range(length)])  19.4 us
    concatenate x4, local copies, waits for them, and re-layouts, shards(): next_slab_field = jnp.concatenate([new_field[:, 1:], ahead_slab], axis=1)  15.3 us
  transfers between devices with their start and end apart: 4, of which 2 were waited for; matrix products, arithmetic and copies ran while one was open for 11% of the time, Pallas kernels for 0%

commit v1 on v0

v1 whole, which is shorter than its diff:
```python
import math

import numpy as np
import jax
import jax.numpy as jnp
from jax import lax
from jax.sharding import PartitionSpec as P

P_SIZE = 4
D = 768
HEADS = 12
HS = 64
LY = 32
LZ = 64
BLK = 128


hopping = 0.2
quartic = 0.5
epsilon = 1e-05
log_two_pi = math.log(2.0 * math.pi)


def shifted(x, axis, by):
    length = lax.axis_size(axis)
    return lax.ppermute(x, axis, [(i, (i + by) % length) for i in range(length)])


def layer_norm(values, gain_vec):
    centre = values - jnp.mean(values, axis=-1, keepdims=True)
    spread = jnp.mean(centre * centre, axis=-1, keepdims=True)
    return centre * lax.rsqrt(spread + epsilon) * gain_vec


def site_parity(patch_side):
    positions = np.arange(patch_side**4, dtype=np.int32)
    return (
        positions // patch_side**3
        + positions // patch_side**2 % patch_side
        + positions // patch_side % patch_side
        + positions % patch_side
    ) % 2


def packed_rows(p_bit):
    th, x4, y4, z4 = np.meshgrid(np.arange(2), np.arange(4), np.arange(4), np.arange(4), indexing="ij")
    t4 = 2 * th + (p_bit + x4 + y4 + z4) % 2
    return (((t4 * 4 + x4) * 4 + y4) * 4 + z4).reshape(-1)


def embed_packed(tokens, bits, w_pair, b_embed):
    both = jnp.dot(tokens, w_pair, preferred_element_type=jnp.float32)
    half = both.shape[-1] // 2
    return jnp.where(bits[..., None] > 0.5, both[..., half:], both[..., :half]) + b_embed


def shards(
    lattice_field, parity, block_list, w_embed, b_embed, gain_in, w_qkv, gain_out, w_head, b_head
):
    n_y = LY // P_SIZE
    n_z = LZ // P_SIZE
    tokens_dev = n_y * n_z
    patch_len = P_SIZE**4
    u = lattice_field
    bits = parity.reshape(n_y, n_z)

    lane = lax.broadcasted_iota(jnp.int32, u.shape, 2)
    t_pos = lax.broadcasted_iota(jnp.int32, u.shape, 0)
    x_pos = lax.broadcasted_iota(jnp.int32, u.shape, 1)
    site_bit = (t_pos + x_pos + lane // LZ + lane % LZ) % 2
    bits_lat = jnp.repeat(jnp.repeat(bits, P_SIZE, axis=0), P_SIZE, axis=1).reshape(LY * LZ)
    frozen = site_bit == bits_lat[None, None, :]
    frozen_in = jnp.where(frozen, u, 0.0).astype(jnp.bfloat16)

    packed = frozen_in[0::2] + frozen_in[1::2]
    tokens = (
        packed.reshape(2, P_SIZE, n_y, P_SIZE, n_z, P_SIZE)
        .transpose(2, 4, 0, 1, 3, 5)
        .reshape(tokens_dev, patch_len // 2)
    )
    bits_f = bits.reshape(1, tokens_dev).astype(jnp.bfloat16)
    send = jnp.concatenate([tokens, bits_f], axis=0)
    gathered = lax.all_gather(send, "tm", axis=0, tiled=True).reshape(-1, tokens_dev + 1, patch_len // 2)

    w_pair = jnp.concatenate(
        [w_embed[packed_rows(0)], w_embed[packed_rows(1)]], axis=1
    )
    bits_own = bits.reshape(tokens_dev).astype(jnp.float32)
    embedded = embed_packed(tokens, bits_own, w_pair, b_embed)
    normed = layer_norm(embedded, gain_in).astype(jnp.bfloat16)
    queries = jnp.dot(normed, w_qkv[:, :D], preferred_element_type=jnp.float32).astype(
        jnp.bfloat16
    )

    block_rows = lax.dynamic_index_in_dim(block_list, lax.axis_index("tm"), 0, keepdims=False)
    chosen = jnp.take(gathered, block_rows, axis=0)
    n_sel = chosen.shape[0]
    sel_tokens = chosen[:, :tokens_dev, :].reshape(n_sel * tokens_dev, patch_len // 2)
    sel_bits = chosen[:, tokens_dev, :].reshape(n_sel * tokens_dev).astype(jnp.float32)
    sel_embedded = embed_packed(sel_tokens, sel_bits, w_pair, b_embed)
    sel_normed = layer_norm(sel_embedded, gain_in).astype(jnp.bfloat16)
    kv = jnp.dot(sel_normed, w_qkv[:, D:], preferred_element_type=jnp.float32).astype(
        jnp.bfloat16
    )
    keys = kv[:, :D].reshape(n_sel * tokens_dev, HEADS, HS)
    values = kv[:, D:].reshape(n_sel * tokens_dev, HEADS, HS)

    scores = jnp.einsum(
        "qhd,khd->hqk",
        queries.reshape(tokens_dev, HEADS, HS),
        keys,
        preferred_element_type=jnp.float32,
    ) * HS ** (-0.5)
    row_top = jnp.max(scores, axis=-1, keepdims=True)
    exp_scores = jnp.exp(scores - row_top)
    row_total = jnp.sum(exp_scores, axis=-1)
    product = jnp.einsum(
        "hqk,khd->qhd",
        exp_scores.astype(jnp.bfloat16),
        values,
        preferred_element_type=jnp.float32,
    )
    mixed = (product / row_total.T[:, :, None]).reshape(tokens_dev, D)
    hidden = embedded + mixed
    normed_out = layer_norm(hidden, gain_out).astype(jnp.bfloat16)
    affine = jnp.dot(normed_out, w_head, preferred_element_type=jnp.float32) + b_head
    scale_log = jnp.tanh(affine[:, :patch_len])
    frozen_tok = jnp.asarray(site_parity(P_SIZE))[None, :] == bits.reshape(tokens_dev)[:, None]
    log_det = jnp.sum(jnp.where(frozen_tok, 0.0, scale_log))

    coupling = jnp.concatenate([scale_log, affine[:, patch_len:]], axis=1)
    coupling_lat = (
        coupling.reshape(n_y, n_z, 2, P_SIZE, P_SIZE, P_SIZE, P_SIZE)
        .transpose(2, 3, 4, 0, 5, 1, 6)
        .reshape(2, P_SIZE, P_SIZE, LY * LZ)
    )
    scale_lat = coupling_lat[0]
    shift_lat = coupling_lat[1]
    new_field = jnp.where(frozen, u, u * jnp.exp(scale_lat) + shift_lat)

    ahead_time = shifted(new_field[0:1].astype(jnp.bfloat16), "tm", -1).astype(jnp.float32)
    ahead_slab = shifted(new_field[:, 0:1].astype(jnp.bfloat16), "space", -1).astype(jnp.float32)
    next_time_field = jnp.concatenate([new_field[1:], ahead_time], axis=0)
    next_slab_field = jnp.concatenate([new_field[:, 1:], ahead_slab], axis=1)
    next_y_field = jnp.roll(new_field, -LZ, axis=2)
    next_z_field = jnp.where(
        lane % LZ == LZ - 1, jnp.roll(new_field, LZ - 1, axis=2), jnp.roll(new_field, -1, axis=2)
    )
    neighbours = next_time_field + next_slab_field
    neighbours = neighbours + next_y_field
    neighbours = neighbours + next_z_field
    squared = new_field * new_field
    density = (
        -2.0 * hopping * new_field * neighbours
        + squared
        + quartic * (squared - 1.0) * (squared - 1.0)
    )
    time_link = new_field * next_time_field
    slab_link = new_field * next_slab_field
    local_log = -0.5 * jnp.sum(u * u) - log_det
    local_act = jnp.sum(density)
    sum_log, sum_act = lax.psum(lax.psum((local_log, local_act), "tm"), "space")
    site_count = u.size * lax.axis_size("space") * lax.axis_size("tm")
    totals = jnp.stack([sum_log / site_count - 0.5 * log_two_pi, sum_act / site_count]).astype(
        jnp.float32
    )
    return (new_field, density, time_link, slab_link, totals)


def solution(mesh):
    in_specs = (
        P("tm", "space", None),
        P("tm", "space", None),
        P(),
        P(),
        P(),
        P(),
        P(),
        P(),
        P(),
        P(),
    )
    out_specs = (
        P("tm", "space", None),
        P("tm", "space", None),
        P("tm", "space", None),
        P("tm", "space", None),
        P(),
    )
    return jax.shard_map(shards, mesh=mesh, in_specs=in_specs, out_specs=out_specs, check_vma=False)
```

time: 587 us -> 320 us (0.55)
  the two profiles are of different devices: /device:TPU:1 before, /device:TPU:8 now
where the time goes in v1:
time: 320 us; the launch traced here: 319 us
  blocking collectives  243 us (76%)
  local copies, waits for them, and re-layouts  38.7 us (12%)
  other arithmetic  10.2 us (3%)
  starting transfers between devices  9.85 us (3%)
  matrix products  9.01 us (3%)
  waiting for transfers between devices  4.84 us (2%)
  between operations  3.69 us (1%)
    psum x2, blocking collectives, shards(): sum_log, sum_act = lax.psum(lax.psum((local_log, local_act), 'tm'), 'space')  204 us
    all_gather x1, blocking collectives, shards(): lax.all_gather(send, 'tm', axis=0, tiled=True)  38.9 us
    exp x3, local copies, waits for them, and re-layouts, shards(): new_field = jnp.where(frozen, u, u * jnp.exp(scale_lat) + shift_lat)  12 us
    ppermute x2, starting transfers between devices, shifted(): lax.ppermute(x, axis, [(i, (i + by) % length) for i in range(length)])  9.85 us
  transfers between devices with their start and end apart: 2, of which 1 were waited for; matrix products, arithmetic and copies ran while one was open for 0% of the time, Pallas kernels for 0%

profile of v1, /device:TPU:8, one launch (start us, length us, event | category | flops | bytes accessed | tf_op | source)
XLA Modules:
  0.0 319.3 jit_solution(7519041615641170280)
XLA Ops:
  2.9 1.4 convert_bitcast_fusion
  4.8 1.1 select_convert_fusion
  5.9 2.2 reshape.160
  8.1 1.7 copy.56
  10.1 38.9 %all-gather = bf16[16,129,128]{2,1,0:T(8,128)(2,1)S(1)} all-gather(bf16[1,129,128]{2,1,0:T(8,128)(2,1)S(1)} %copy.58), channel_id=1, replica_groups=mesh['space'=32,'tm'=16] {'tm'}, dimensions={0}, use_global_device_ids=true | all-gather | bytes 561408 | tf_op jit(solution)/shard_map/all_gather | solution.py:83
  52.3 1.6 fusion.16
  57.1 3.1 convolution_convert_fusion
  60.2 1.9 fusion.53
  62.1 1.7 copy.61
  63.8 2.6 copy.59
  66.4 1.1 multiply_reduce_fusion
  67.5 1.3 fusion
  68.9 1.6 fusion.19
  72.9 1.6 slice_exponential_fusion
  74.4 5.4 %copy.64 = f32[1,4,4,8,4,16,4]{6,5,4,3,2,1,0:T(8,128)} copy(f32[1,4,4,8,4,16,4]{5,3,6,4,2,1,0:T(8,128)} %get-tuple-element.21) | data formatting | bytes 262144 | tf_op jit(solution)/shard_map/exp | solution.py:139
  79.9 5.0 %exp.11 = f32[4,4,2048]{2,1,0:T(4,128)S(1)} reshape(f32[1,4,4,8,4,16,4]{6,5,4,3,2,1,0:T(8,128)} %copy.64) | data formatting | bytes 262144 | tf_op jit(solution)/shard_map/exp | solution.py:139
  85.0 4.5 %copy.65 = f32[1,4,4,8,4,16,4]{6,5,4,3,2,1,0:T(8,128)} copy(f32[1,4,4,8,4,16,4]{5,3,6,4,2,1,0:T(8,128)S(1)} %copy-done.4) | data formatting | bytes 262144 | tf_op jit(solution)/shard_map/slice | solution.py:138
  89.4 5.0 %squeeze.12 = f32[4,4,2048]{2,1,0:T(4,128)S(1)} reshape(f32[1,4,4,8,4,16,4]{6,5,4,3,2,1,0:T(8,128)} %copy.65) | data formatting | bytes 262144 | tf_op jit(solution)/shard_map/squeeze | solution.py:138
  95.3 1.9 collective-permute-start
  97.2 7.9 %collective-permute-start.1 = (bf16[4,1,2048]{2,1,0:T(2,128)(2,1)S(1)}, bf16[4,1,2048]{2,1,0:T(2,128)(2,1)S(1)}, u32[]{:S(2)}, u32[]{:S(2)}) collective-permute-start(bf16[4,1,2048]{2,1,0:T(2,128)(2,1)S(1)} %slice.135), channel_id=1, source_target_pairs={{0,496},{16,0},{32,16},{48,32},{64,48},{80,64},{96,80},{112,96},{1... | collective-permute-start | bytes 49160 | tf_op jit(solution)/shard_map/ppermute | solution.py:26
  106.9 4.8 %collective-permute-done.1 = bf16[4,1,2048]{2,1,0:T(2,128)(2,1)S(1)} collective-permute-done((bf16[4,1,2048]{2,1,0:T(2,128)(2,1)S(1)}, bf16[4,1,2048]{2,1,0:T(2,128)(2,1)S(1)}, u32[]{:S(2)}, u32[]{:S(2)}) %collective-permute-start.1) | collective-permute-done | bytes 16416 | tf_op jit(solution)/shard_map/ppermute | solution.py:26
  111.8 1.6 fusion.45
  113.4 45.9 %all-reduce.1 = (f32[]{:T(128)}, f32[]{:T(128)}) all-reduce(f32[]{:T(128)} %get-tuple-element.9, f32[]{:T(128)S(6)} %sub.59), channel_id=1, replica_groups=mesh['space'=32,'tm'=16] {'tm'}, use_global_device_ids=true, to_apply=%region_13.14 | all-reduce | flops 2 | bytes 16 | tf_op jit(solution)/shard_map/psum | solution.py:162
  159.3 158.2 %all-reduce = (f32[]{:T(128)}, f32[]{:T(128)}) all-reduce(f32[]{:T(128)} %get-tuple-element.7, f32[]{:T(128)} %get-tuple-element.8), channel_id=1, replica_groups=mesh['space'=32,'tm'=16] {'space'}, use_global_device_ids=true, to_apply=%region_14.15 | all-reduce | flops 2 | bytes 16 | tf_op jit(solution)/shard_map/psum | solution.py:162
  (92 shorter events, 13.6 us)
Async XLA Ops:
  0.6 70.4 %copy-start = (bf16[768,512]{1,0:T(8,128)(2,1)S(1)}, bf16[768,512]{1,0:T(8,128)(2,1)}, u32[]{:S(2)}) copy-start(bf16[768,512]{1,0:T(8,128)(2,1)} %param.23) | copy-start | bytes 2359300
  0.6 49.1 %copy-start.11 = (s32[128]{0:T(128)S(1)}, s32[128]{0:T(128)}, u32[]{:S(2)}) copy-start(s32[128]{0:T(128)} %constant.125) | copy-start | bytes 1540
  0.7 49.1 %copy-start.12 = (s32[128]{0:T(128)S(1)}, s32[128]{0:T(128)}, u32[]{:S(2)}) copy-start(s32[128]{0:T(128)} %constant.124) | copy-start | bytes 1540
  0.7 49.1 %copy-start.1 = (bf16[256,768]{1,0:T(8,128)(2,1)S(1)}, bf16[256,768]{1,0:T(8,128)(2,1)}, u32[]{:S(2)}) copy-start(bf16[256,768]{1,0:T(8,128)(2,1)} %param.18) | copy-start | bytes 1179652
  49.7 2.2 copy-start.6
  49.8 2.5 copy-start.14
  55.1 2.0 copy-start.13
  67.5 1.4 copy-start.3
  68.9 2.1 copy-start.7
  68.9 2.1 copy-start.8
  70.5 0.9 copy-start.9
  70.5 0.9 copy-start.10
  79.9 5.1 %copy-start.4 = (f32[1,4,4,8,4,16,4]{5,3,6,4,2,1,0:T(8,128)S(1)}, f32[1,4,4,8,4,16,4]{5,3,6,4,2,1,0:T(8,128)}, u32[]{:S(2)}) copy-start(f32[1,4,4,8,4,16,4]{5,3,6,4,2,1,0:T(8,128)} %get-tuple-element.22) | copy-start | bytes 393220
  89.4 5.0 %copy-start.5 = (f32[4,4,2048]{2,1,0:T(4,128)S(1)}, f32[4,4,2048]{2,1,0:T(4,128)}, u32[]{:S(2)}) copy-start(f32[4,4,2048]{2,1,0:T(4,128)} %param.15) | copy-start | bytes 393220
  95.2 224.0 %copy-start.2 = (f32[4,4,2048]{2,1,0:T(4,128)}, f32[4,4,2048]{2,1,0:T(4,128)S(1)}, u32[]{:S(2)}) copy-start(f32[4,4,2048]{2,1,0:T(4,128)S(1)} %get-tuple-element.12) | copy-start | bytes 393220
  95.3 11.6 %collective-permute-start = (bf16[1,4,2048]{2,1,0:T(4,128)(2,1)S(1)}, bf16[1,4,2048]{2,1,0:T(4,128)(2,1)S(1)}, u32[]{:S(2)}, u32[]{:S(2)}) collective-permute-start(bf16[1,4,2048]{2,1,0:T(4,128)(2,1)S(1)} %slice.133), channel_id=1, source_target_pairs={{0,15},{1,0},{2,1},{3,2},{4,3},{5,4},{6,5},{7,6},{8,7},{9,8},{10,9... | collective-permute-start | bytes 49160 | tf_op jit(solution)/shard_map/ppermute | solution.py:26
  97.2 14.5 %collective-permute-start.1 = (bf16[4,1,2048]{2,1,0:T(2,128)(2,1)S(1)}, bf16[4,1,2048]{2,1,0:T(2,128)(2,1)S(1)}, u32[]{:S(2)}, u32[]{:S(2)}) collective-permute-start(bf16[4,1,2048]{2,1,0:T(2,128)(2,1)S(1)} %slice.135), channel_id=1, source_target_pairs={{0,496},{16,0},{32,16},{48,32},{64,48},{80,64},{96,80},{112,96},{1... | collective-permute-start | bytes 49160 | tf_op jit(solution)/shard_map/ppermute | solution.py:26

commit v2 on v1

--- a/solution.py
+++ b/solution.py
@@ -19,6 +19,32 @@
 quartic = 0.5
 epsilon = 1e-05
 log_two_pi = math.log(2.0 * math.pi)
+
+
+def exchange(x, axis, bit):
+    length = lax.axis_size(axis)
+    return lax.ppermute(x, axis, [(i, i ^ bit) for i in range(length)])
+
+
+def doubling_sum(x, axis):
+    bit = 1
+    while bit < lax.axis_size(axis):
+        x = x + exchange(x, axis, bit)
+        bit *= 2
+    return x
+
+
+def doubling_gather(x, axis):
+    bits = []
+    bit = 1
+    while bit < lax.axis_size(axis):
+        bits.append(bit)
+        bit *= 2
+    offsets = [0]
+    for bit in reversed(bits):
+        x = jnp.concatenate([x, exchange(x, axis, bit)], axis=0)
+        offsets = offsets + [o ^ bit for o in offsets]
+    return x, offsets
 
 
 def shifted(x, axis, by):
@@ -80,7 +106,8 @@
     )
     bits_f = bits.reshape(1, tokens_dev).astype(jnp.bfloat16)
     send = jnp.concatenate([tokens, bits_f], axis=0)
-    gathered = lax.all_gather(send, "tm", axis=0, tiled=True).reshape(-1, tokens_dev + 1, patch_len // 2)
+    gathered, offsets = doubling_gather(send[None], "tm")
+    slot_of = np.argsort(np.asarray(offsets)).astype(np.int32)
 
     w_pair = jnp.concatenate(
         [w_embed[packed_rows(0)], w_embed[packed_rows(1)]], axis=1
@@ -93,7 +120,8 @@
     )
 
     block_rows = lax.dynamic_index_in_dim(block_list, lax.axis_index("tm"), 0, keepdims=False)
-    chosen = jnp.take(gathered, block_rows, axis=0)
+    own = lax.axis_index("tm")
+    chosen = jnp.take(gathered, jnp.asarray(slot_of)[block_rows ^ own], axis=0)
     n_sel = chosen.shape[0]
     sel_tokens = chosen[:, :tokens_dev, :].reshape(n_sel * tokens_dev, patch_len // 2)
     sel_bits = chosen[:, tokens_dev, :].reshape(n_sel * tokens_dev).astype(jnp.float32)
@@ -159,7 +187,8 @@
     slab_link = new_field * next_slab_field
     local_log = -0.5 * jnp.sum(u * u) - log_det
     local_act = jnp.sum(density)
-    sum_log, sum_act = lax.psum(lax.psum((local_log, local_act), "tm"), "space")
+    sums = doubling_sum(doubling_sum(jnp.stack([local_log, local_act]), "tm"), "space")
+    sum_log, sum_act = sums[0], sums[1]
     site_count = u.size * lax.axis_size("space") * lax.axis_size("tm")
     totals = jnp.stack([sum_log / site_count - 0.5 * log_two_pi, sum_act / site_count]).astype(
         jnp.float32

time: 320 us -> 188 us (0.59)
  the two profiles are of different devices: /device:TPU:8 before, /device:TPU:30 now
where the time goes in v2:
time: 188 us; the launch traced here: 187 us
  starting transfers between devices  68.5 us (36%)
  waiting for transfers between devices  49.7 us (26%)
  local copies, waits for them, and re-layouts  43 us (23%)
  other arithmetic  13 us (7%)
  matrix products  9.03 us (5%)
  between operations  3.88 us (2%)
    ppermute x13, starting transfers between devices, exchange(): return lax.ppermute(x, axis, [(i, i ^ bit) for i in range(length)])  47.8 us
    ppermute x13, waiting for transfers between devices, exchange(): return lax.ppermute(x, axis, [(i, i ^ bit) for i in range(length)])  46.1 us
    ppermute x2, starting transfers between devices, shifted(): lax.ppermute(x, axis, [(i, (i + by) % length) for i in range(length)])  20.7 us
    exp x3, local copies, waits for them, and re-layouts, shards(): new_field = jnp.where(frozen, u, u * jnp.exp(scale_lat) + shift_lat)  12 us
    squeeze x1, local copies, waits for them, and re-layouts, shards(): shift_lat = coupling_lat[1]  4.98 us
    slice x1, local copies, waits for them, and re-layouts, shards(): shift_lat = coupling_lat[1]  4.5 us
  transfers between devices with their start and end apart: 15, of which 13 were waited for; matrix products, arithmetic and copies ran while one was open for 4% of the time, Pallas kernels for 0%

profile of v2, /device:TPU:30, one launch (start us, length us, event | category | flops | bytes accessed | tf_op | source)
XLA Modules:
  0.0 187.2 jit_solution(16856910658973537207)
XLA Ops:
  8.4 9.1 %collective-permute-start = (bf16[1,129,128]{1,2,0:T(8,128)(2,1)S(1)}, bf16[1,129,128]{1,2,0:T(8,128)(2,1)S(1)}, u32[]{:S(2)}, u32[]{:S(2)}) collective-permute-start(bf16[1,129,128]{1,2,0:T(8,128)(2,1)S(1)} %maximum_bitcast_fusion), channel_id=1, source_target_pairs={{0,8},{1,9},{2,10},{3,11},{4,12},{5,13},{6,14},{7,15},{8,0},{9,1},... | collective-permute-start | bytes 99080 | tf_op jit(solution)/shard_map/ppermute | solution.py:26
  24.0 3.9 %collective-permute-start.1 = (bf16[2,129,128]{1,2,0:T(8,128)(2,1)S(1)}, bf16[2,129,128]{1,2,0:T(8,128)(2,1)S(1)}, u32[]{:S(2)}, u32[]{:S(2)}) collective-permute-start(bf16[2,129,128]{1,2,0:T(8,128)(2,1)S(1)} %pad_maximum_fusion.3), channel_id=1, source_target_pairs={{0,4},{1,5},{2,6},{3,7},{4,0},{5,1},{6,2},{7,3},{8,12},{9,13},{10,... | collective-permute-start | bytes 198152 | tf_op jit(solution)/shard_map/ppermute | solution.py:26
  27.9 6.0 %collective-permute-done.1 = bf16[2,129,128]{1,2,0:T(8,128)(2,1)S(1)} collective-permute-done((bf16[2,129,128]{1,2,0:T(8,128)(2,1)S(1)}, bf16[2,129,128]{1,2,0:T(8,128)(2,1)S(1)}, u32[]{:S(2)}, u32[]{:S(2)}) %collective-permute-start.1) | collective-permute-done | bytes 66080 | tf_op jit(solution)/shard_map/ppermute | solution.py:26
  33.9 2.6 %collective-permute-start.2 = (bf16[4,129,128]{1,2,0:T(8,128)(2,1)S(1)}, bf16[4,129,128]{1,2,0:T(8,128)(2,1)S(1)}, u32[]{:S(2)}, u32[]{:S(2)}) collective-permute-start(bf16[4,129,128]{1,2,0:T(8,128)(2,1)S(1)} %pad_maximum_fusion.1), channel_id=1, source_target_pairs={{0,2},{1,3},{2,0},{3,1},{4,6},{5,7},{6,4},{7,5},{8,10},{9,11},{10,... | collective-permute-start | bytes 396296 | tf_op jit(solution)/shard_map/ppermute | solution.py:26
  37.4 5.7 %collective-permute-done.2 = bf16[4,129,128]{1,2,0:T(8,128)(2,1)S(1)} collective-permute-done((bf16[4,129,128]{1,2,0:T(8,128)(2,1)S(1)}, bf16[4,129,128]{1,2,0:T(8,128)(2,1)S(1)}, u32[]{:S(2)}, u32[]{:S(2)}) %collective-permute-start.2) | collective-permute-done | bytes 132128 | tf_op jit(solution)/shard_map/ppermute | solution.py:26
  53.3 3.1 %convolution_convert_fusion = bf16[1024,1536]{1,0:T(8,128)(2,1)S(1)} fusion(bf16[768,2304]{1,0:T(8,128)(2,1)S(1)} %copy-done.15, f32[1024,768]{1,0:T(8,128)S(1)} %get-tuple-element.14, f32[768]{0:T(1024)S(1)} %copy-done.16, f32[1024]{0:T(1024)S(1)} %add_rsqrt_fusion, f32[1024]{0:T(1024)S(1)} %broadcast_multiply_fusion), kind=kOutput, calls=%fused_computation.8 | convolution fusion | flops 2420637696 | bytes 8663040 | tf_op jit(solution)/shard_map/dot_general | solution.py:130
  60.0 2.6 %copy.39 = bf16[1024,768]{0,1:T(8,128)(2,1)} copy(bf16[1024,768]{1,0:T(8,128)(2,1)} %get-tuple-element.16) | data formatting | bytes 3145728 | tf_op jit(solution)/shard_map/slice | solution.py:134
  70.5 5.5 %copy.44 = f32[1,4,4,8,4,16,4]{6,5,4,3,2,1,0:T(8,128)} copy(f32[1,4,4,8,4,16,4]{5,3,6,4,2,1,0:T(8,128)} %get-tuple-element.17) | data formatting | bytes 262144 | tf_op jit(solution)/shard_map/exp | solution.py:167
  76.0 5.0 %exp.11 = f32[4,4,2048]{2,1,0:T(4,128)S(1)} reshape(f32[1,4,4,8,4,16,4]{6,5,4,3,2,1,0:T(8,128)} %copy.44) | data formatting | bytes 262144 | tf_op jit(solution)/shard_map/exp | solution.py:167
  81.1 4.5 %copy.45 = f32[1,4,4,8,4,16,4]{6,5,4,3,2,1,0:T(8,128)} copy(f32[1,4,4,8,4,16,4]{5,3,6,4,2,1,0:T(8,128)S(1)} %copy-done.5) | data formatting | bytes 262144 | tf_op jit(solution)/shard_map/slice | solution.py:166
  85.6 5.0 %squeeze.4 = f32[4,4,2048]{2,1,0:T(4,128)S(1)} reshape(f32[1,4,4,8,4,16,4]{6,5,4,3,2,1,0:T(8,128)} %copy.45) | data formatting | bytes 262144 | tf_op jit(solution)/shard_map/squeeze | solution.py:166
  91.4 11.0 %collective-permute-start.4 = (bf16[1,4,2048]{2,1,0:T(4,128)(2,1)S(1)}, bf16[1,4,2048]{2,1,0:T(4,128)(2,1)S(1)}, u32[]{:S(2)}, u32[]{:S(2)}) collective-permute-start(bf16[1,4,2048]{2,1,0:T(4,128)(2,1)S(1)} %slice.143), channel_id=1, source_target_pairs={{0,15},{1,0},{2,1},{3,2},{4,3},{5,4},{6,5},{7,6},{8,7},{9,8},{10,9... | collective-permute-start | bytes 49160 | tf_op jit(solution)/shard_map/ppermute | solution.py:52
  102.4 9.7 %collective-permute-start.5 = (bf16[4,1,2048]{2,1,0:T(2,128)(2,1)S(1)}, bf16[4,1,2048]{2,1,0:T(2,128)(2,1)S(1)}, u32[]{:S(2)}, u32[]{:S(2)}) collective-permute-start(bf16[4,1,2048]{2,1,0:T(2,128)(2,1)S(1)} %slice.145), channel_id=1, source_target_pairs={{0,496},{16,0},{32,16},{48,32},{64,48},{80,64},{96,80},{112,96},{1... | collective-permute-start | bytes 49160 | tf_op jit(solution)/shard_map/ppermute | solution.py:52
  113.9 3.6 %collective-permute-done.5 = bf16[4,1,2048]{2,1,0:T(2,128)(2,1)S(1)} collective-permute-done((bf16[4,1,2048]{2,1,0:T(2,128)(2,1)S(1)}, bf16[4,1,2048]{2,1,0:T(2,128)(2,1)S(1)}, u32[]{:S(2)}, u32[]{:S(2)}) %collective-permute-start.5) | collective-permute-done | bytes 16416 | tf_op jit(solution)/shard_map/ppermute | solution.py:52
  125.5 3.5 %collective-permute-done.7 = f32[2]{0:T(128)S(1)} collective-permute-done((f32[2]{0:T(128)S(1)}, f32[2]{0:T(128)S(1)}, u32[]{:S(2)}, u32[]{:S(2)}) %collective-permute-start.7) | collective-permute-done | bytes 40 | tf_op jit(solution)/shard_map/ppermute | solution.py:26
  131.7 4.4 %collective-permute-done.8 = f32[2]{0:T(128)S(1)} collective-permute-done((f32[2]{0:T(128)S(1)}, f32[2]{0:T(128)S(1)}, u32[]{:S(2)}, u32[]{:S(2)}) %collective-permute-start.8) | collective-permute-done | bytes 40 | tf_op jit(solution)/shard_map/ppermute | solution.py:26
  138.0 7.4 %collective-permute-done.9 = f32[2]{0:T(128)S(1)} collective-permute-done((f32[2]{0:T(128)S(1)}, f32[2]{0:T(128)S(1)}, u32[]{:S(2)}, u32[]{:S(2)}) %collective-permute-start.9) | collective-permute-done | bytes 40 | tf_op jit(solution)/shard_map/ppermute | solution.py:26
  145.4 13.2 %collective-permute-start.10 = (f32[2]{0:T(128)S(1)}, f32[2]{0:T(128)S(1)}, u32[]{:S(2)}, u32[]{:S(2)}) collective-permute-start(f32[2]{0:T(128)S(1)} %add.198), channel_id=1, source_target_pairs={{0,16},{16,0},{32,48},{48,32},{64,80},{80,64},{96,112},{112,96},{1... | collective-permute-start | bytes 32 | tf_op jit(solution)/shard_map/ppermute | solution.py:26
  162.1 3.4 %collective-permute-done.11 = f32[2]{0:T(128)S(1)} collective-permute-done((f32[2]{0:T(128)S(1)}, f32[2]{0:T(128)S(1)}, u32[]{:S(2)}, u32[]{:S(2)}) %collective-permute-start.11) | collective-permute-done | bytes 40 | tf_op jit(solution)/shard_map/ppermute | solution.py:26
  165.5 2.5 %collective-permute-start.12 = (f32[2]{0:T(128)S(1)}, f32[2]{0:T(128)S(1)}, u32[]{:S(2)}, u32[]{:S(2)}) collective-permute-start(f32[2]{0:T(128)S(1)} %add.200), channel_id=1, source_target_pairs={{0,64},{16,80},{32,96},{48,112},{64,0},{80,16},{96,32},{112,48},{1... | collective-permute-start | bytes 32 | tf_op jit(solution)/shard_map/ppermute | solution.py:26
  168.0 4.4 %collective-permute-done.12 = f32[2]{0:T(128)S(1)} collective-permute-done((f32[2]{0:T(128)S(1)}, f32[2]{0:T(128)S(1)}, u32[]{:S(2)}, u32[]{:S(2)}) %collective-permute-start.12) | collective-permute-done | bytes 40 | tf_op jit(solution)/shard_map/ppermute | solution.py:26
  174.7 3.2 %collective-permute-done.13 = f32[2]{0:T(128)S(1)} collective-permute-done((f32[2]{0:T(128)S(1)}, f32[2]{0:T(128)S(1)}, u32[]{:S(2)}, u32[]{:S(2)}) %collective-permute-start.13) | collective-permute-done | bytes 40 | tf_op jit(solution)/shard_map/ppermute | solution.py:26
  177.9 2.8 %collective-permute-start.14 = (f32[2]{0:T(128)S(1)}, f32[2]{0:T(128)S(1)}, u32[]{:S(2)}, u32[]{:S(2)}) collective-permute-start(f32[2]{0:T(128)S(1)} %add.202), channel_id=1, source_target_pairs={{0,256},{16,272},{32,288},{48,304},{64,320},{80,336},{96,352},{112... | collective-permute-start | bytes 32 | tf_op jit(solution)/shard_map/ppermute | solution.py:26
  180.7 4.1 %collective-permute-done.14 = f32[2]{0:T(128)S(1)} collective-permute-done((f32[2]{0:T(128)S(1)}, f32[2]{0:T(128)S(1)}, u32[]{:S(2)}, u32[]{:S(2)}) %collective-permute-start.14) | collective-permute-done | bytes 40 | tf_op jit(solution)/shard_map/ppermute | solution.py:26
  (141 shorter events, 57.0 us)
Async XLA Ops:
  0.6 66.5 %copy-start = (bf16[768,512]{1,0:T(8,128)(2,1)S(1)}, bf16[768,512]{1,0:T(8,128)(2,1)}, u32[]{:S(2)}) copy-start(bf16[768,512]{1,0:T(8,128)(2,1)} %param.24) | copy-start | bytes 2359300
  0.6 17.1 %copy-start.14 = (s32[128]{0:T(128)S(1)}, s32[128]{0:T(128)}, u32[]{:S(2)}) copy-start(s32[128]{0:T(128)} %constant.132) | copy-start | bytes 1540
  0.7 17.1 %copy-start.13 = (s32[128]{0:T(128)S(1)}, s32[128]{0:T(128)}, u32[]{:S(2)}) copy-start(s32[128]{0:T(128)} %constant.133) | copy-start | bytes 1540
  0.7 16.8 %copy-start.11 = (s32[1,1,128]{2,1,0:T(1,128)S(1)}, s32[1,1,128]{2,1,0:T(1,128)}, u32[]{:S(2)}) copy-start(s32[1,1,128]{2,1,0:T(1,128)} %param.17) | copy-start | bytes 1540
  0.7 16.8 %copy-start.9 = (s32[16,8]{0,1:T(8,128)S(1)}, s32[16,8]{0,1:T(8,128)}, u32[]{:S(2)}) copy-start(s32[16,8]{0,1:T(8,128)} %param.18) | copy-start | bytes 1540
  0.7 17.1 %copy-start.2 = (bf16[256,768]{1,0:T(8,128)(2,1)S(1)}, bf16[256,768]{1,0:T(8,128)(2,1)}, u32[]{:S(2)}) copy-start(bf16[256,768]{1,0:T(8,128)(2,1)} %param.19) | copy-start | bytes 1179652
  8.2 11.7 %copy-start.7 = (f32[768]{0:T(1024)S(1)}, f32[768]{0:T(1024)}, u32[]{:S(2)}) copy-start(f32[768]{0:T(1024)} %param.20) | copy-start | bytes 9220
  8.4 15.5 %collective-permute-start = (bf16[1,129,128]{1,2,0:T(8,128)(2,1)S(1)}, bf16[1,129,128]{1,2,0:T(8,128)(2,1)S(1)}, u32[]{:S(2)}, u32[]{:S(2)}) collective-permute-start(bf16[1,129,128]{1,2,0:T(8,128)(2,1)S(1)} %maximum_bitcast_fusion), channel_id=1, source_target_pairs={{0,8},{1,9},{2,10},{3,11},{4,12},{5,13},{6,14},{7,15},{8,0},{9,1},... | collective-permute-start | bytes 99080 | tf_op jit(solution)/shard_map/ppermute | solution.py:26
  24.0 9.9 %collective-permute-start.1 = (bf16[2,129,128]{1,2,0:T(8,128)(2,1)S(1)}, bf16[2,129,128]{1,2,0:T(8,128)(2,1)S(1)}, u32[]{:S(2)}, u32[]{:S(2)}) collective-permute-start(bf16[2,129,128]{1,2,0:T(8,128)(2,1)S(1)} %pad_maximum_fusion.3), channel_id=1, source_target_pairs={{0,4},{1,5},{2,6},{3,7},{4,0},{5,1},{6,2},{7,3},{8,12},{9,13},{10,... | collective-permute-start | bytes 198152 | tf_op jit(solution)/shard_map/ppermute | solution.py:26
  33.9 9.1 %collective-permute-start.2 = (bf16[4,129,128]{1,2,0:T(8,128)(2,1)S(1)}, bf16[4,129,128]{1,2,0:T(8,128)(2,1)S(1)}, u32[]{:S(2)}, u32[]{:S(2)}) collective-permute-start(bf16[4,129,128]{1,2,0:T(8,128)(2,1)S(1)} %pad_maximum_fusion.1), channel_id=1, source_target_pairs={{0,2},{1,3},{2,0},{3,1},{4,6},{5,7},{6,4},{7,5},{8,10},{9,11},{10,... | collective-permute-start | bytes 396296 | tf_op jit(solution)/shard_map/ppermute | solution.py:26
  43.1 3.9 %collective-permute-start.3 = (bf16[8,129,128]{1,2,0:T(8,128)(2,1)S(1)}, bf16[8,129,128]{1,2,0:T(8,128)(2,1)S(1)}, u32[]{:S(2)}, u32[]{:S(2)}) collective-permute-start(bf16[8,129,128]{1,2,0:T(8,128)(2,1)S(1)} %pad_maximum_fusion), channel_id=1, source_target_pairs={{0,1},{1,0},{2,3},{3,2},{4,5},{5,4},{6,7},{7,6},{8,9},{9,8},{10,11... | collective-permute-start | bytes 792584 | tf_op jit(solution)/shard_map/ppermute | solution.py:26
  76.0 5.1 %copy-start.5 = (f32[1,4,4,8,4,16,4]{5,3,6,4,2,1,0:T(8,128)S(1)}, f32[1,4,4,8,4,16,4]{5,3,6,4,2,1,0:T(8,128)}, u32[]{:S(2)}) copy-start(f32[1,4,4,8,4,16,4]{5,3,6,4,2,1,0:T(8,128)} %get-tuple-element.18) | copy-start | bytes 393220
  91.4 95.8 %copy-start.3 = (f32[4,4,2048]{2,1,0:T(4,128)}, f32[4,4,2048]{2,1,0:T(4,128)S(1)}, u32[]{:S(2)}) copy-start(f32[4,4,2048]{2,1,0:T(4,128)S(1)} %get-tuple-element.8) | copy-start | bytes 393220
  91.4 22.5 %collective-permute-start.4 = (bf16[1,4,2048]{2,1,0:T(4,128)(2,1)S(1)}, bf16[1,4,2048]{2,1,0:T(4,128)(2,1)S(1)}, u32[]{:S(2)}, u32[]{:S(2)}) collective-permute-start(bf16[1,4,2048]{2,1,0:T(4,128)(2,1)S(1)} %slice.143), channel_id=1, source_target_pairs={{0,15},{1,0},{2,1},{3,2},{4,3},{5,4},{6,5},{7,6},{8,7},{9,8},{10,9... | collective-permute-start | bytes 49160 | tf_op jit(solution)/shard_map/ppermute | solution.py:52
  102.4 15.1 %collective-permute-start.5 = (bf16[4,1,2048]{2,1,0:T(2,128)(2,1)S(1)}, bf16[4,1,2048]{2,1,0:T(2,128)(2,1)S(1)}, u32[]{:S(2)}, u32[]{:S(2)}) collective-permute-start(bf16[4,1,2048]{2,1,0:T(2,128)(2,1)S(1)} %slice.145), channel_id=1, source_target_pairs={{0,496},{16,0},{32,16},{48,32},{64,48},{80,64},{96,80},{112,96},{1... | collective-permute-start | bytes 49160 | tf_op jit(solution)/shard_map/ppermute | solution.py:52
  119.9 3.0 %collective-permute-start.6 = (f32[2]{0:T(128)S(1)}, f32[2]{0:T(128)S(1)}, u32[]{:S(2)}, u32[]{:S(2)}) collective-permute-start(f32[2]{0:T(128)S(1)} %pad_maximum_fusion.6), channel_id=1, source_target_pairs={{0,1},{1,0},{2,3},{3,2},{4,5},{5,4},{6,7},{7,6},{8,9},{9,8},{10,11... | collective-permute-start | bytes 32 | tf_op jit(solution)/shard_map/ppermute | solution.py:26
  123.6 5.4 %collective-permute-start.7 = (f32[2]{0:T(128)S(1)}, f32[2]{0:T(128)S(1)}, u32[]{:S(2)}, u32[]{:S(2)}) collective-permute-start(f32[2]{0:T(128)S(1)} %fusion.67), channel_id=1, source_target_pairs={{0,2},{1,3},{2,0},{3,1},{4,6},{5,7},{6,4},{7,5},{8,10},{9,11},{10,... | collective-permute-start | bytes 32 | tf_op jit(solution)/shard_map/ppermute | solution.py:26
  129.7 6.3 %collective-permute-start.8 = (f32[2]{0:T(128)S(1)}, f32[2]{0:T(128)S(1)}, u32[]{:S(2)}, u32[]{:S(2)}) collective-permute-start(f32[2]{0:T(128)S(1)} %fusion.68), channel_id=1, source_target_pairs={{0,4},{1,5},{2,6},{3,7},{4,0},{5,1},{6,2},{7,3},{8,12},{9,13},{10,... | collective-permute-start | bytes 32 | tf_op jit(solution)/shard_map/ppermute | solution.py:26
  136.1 9.3 %collective-permute-start.9 = (f32[2]{0:T(128)S(1)}, f32[2]{0:T(128)S(1)}, u32[]{:S(2)}, u32[]{:S(2)}) collective-permute-start(f32[2]{0:T(128)S(1)} %add.197), channel_id=1, source_target_pairs={{0,8},{1,9},{2,10},{3,11},{4,12},{5,13},{6,14},{7,15},{8,0},{9,1},... | collective-permute-start | bytes 32 | tf_op jit(solution)/shard_map/ppermute | solution.py:26
  145.4 14.7 %collective-permute-start.10 = (f32[2]{0:T(128)S(1)}, f32[2]{0:T(128)S(1)}, u32[]{:S(2)}, u32[]{:S(2)}) collective-permute-start(f32[2]{0:T(128)S(1)} %add.198), channel_id=1, source_target_pairs={{0,16},{16,0},{32,48},{48,32},{64,80},{80,64},{96,112},{112,96},{1... | collective-permute-start | bytes 32 | tf_op jit(solution)/shard_map/ppermute | solution.py:26
  160.1 5.4 %collective-permute-start.11 = (f32[2]{0:T(128)S(1)}, f32[2]{0:T(128)S(1)}, u32[]{:S(2)}, u32[]{:S(2)}) collective-permute-start(f32[2]{0:T(128)S(1)} %add.199), channel_id=1, source_target_pairs={{0,32},{16,48},{32,0},{48,16},{64,96},{80,112},{96,64},{112,80},{1... | collective-permute-start | bytes 32 | tf_op jit(solution)/shard_map/ppermute | solution.py:26
  165.5 6.9 %collective-permute-start.12 = (f32[2]{0:T(128)S(1)}, f32[2]{0:T(128)S(1)}, u32[]{:S(2)}, u32[]{:S(2)}) collective-permute-start(f32[2]{0:T(128)S(1)} %add.200), channel_id=1, source_target_pairs={{0,64},{16,80},{32,96},{48,112},{64,0},{80,16},{96,32},{112,48},{1... | collective-permute-start | bytes 32 | tf_op jit(solution)/shard_map/ppermute | solution.py:26
  172.4 5.4 %collective-permute-start.13 = (f32[2]{0:T(128)S(1)}, f32[2]{0:T(128)S(1)}, u32[]{:S(2)}, u32[]{:S(2)}) collective-permute-start(f32[2]{0:T(128)S(1)} %add.201), channel_id=1, source_target_pairs={{0,128},{16,144},{32,160},{48,176},{64,192},{80,208},{96,224},{112... | collective-permute-start | bytes 32 | tf_op jit(solution)/shard_map/ppermute | solution.py:26
  177.9 6.9 %collective-permute-start.14 = (f32[2]{0:T(128)S(1)}, f32[2]{0:T(128)S(1)}, u32[]{:S(2)}, u32[]{:S(2)}) collective-permute-start(f32[2]{0:T(128)S(1)} %add.202), channel_id=1, source_target_pairs={{0,256},{16,272},{32,288},{48,304},{64,320},{80,336},{96,352},{112... | collective-permute-start | bytes 32 | tf_op jit(solution)/shard_map/ppermute | solution.py:26
  (8 other events, 18.3 us)

commit v3 on v2

--- a/solution.py
+++ b/solution.py
@@ -151,19 +151,28 @@
     mixed = (product / row_total.T[:, :, None]).reshape(tokens_dev, D)
     hidden = embedded + mixed
     normed_out = layer_norm(hidden, gain_out).astype(jnp.bfloat16)
-    affine = jnp.dot(normed_out, w_head, preferred_element_type=jnp.float32) + b_head
-    scale_log = jnp.tanh(affine[:, :patch_len])
-    frozen_tok = jnp.asarray(site_parity(P_SIZE))[None, :] == bits.reshape(tokens_dev)[:, None]
-    log_det = jnp.sum(jnp.where(frozen_tok, 0.0, scale_log))
-
-    coupling = jnp.concatenate([scale_log, affine[:, patch_len:]], axis=1)
-    coupling_lat = (
-        coupling.reshape(n_y, n_z, 2, P_SIZE, P_SIZE, P_SIZE, P_SIZE)
-        .transpose(2, 3, 4, 0, 5, 1, 6)
-        .reshape(2, P_SIZE, P_SIZE, LY * LZ)
-    )
+    tok_ids = lax.broadcasted_iota(jnp.int32, (tokens_dev, LY * LZ), 0)
+    lane_ids = lax.broadcasted_iota(jnp.int32, (tokens_dev, LY * LZ), 1)
+    tok_lane = tok_ids // n_z * (P_SIZE * LZ) + tok_ids % n_z * P_SIZE
+    spread_tok = (lane_ids == tok_lane).astype(jnp.bfloat16)
+    normed_lanes = jnp.einsum(
+        "tc,tl->cl", normed_out, spread_tok, preferred_element_type=jnp.float32
+    ).astype(jnp.bfloat16)
+    affine_lanes = jnp.einsum(
+        "cj,cl->jl", w_head, normed_lanes, preferred_element_type=jnp.float32
+    )
+    base_lane = (lane[0, 0] % P_SIZE == 0) & (lane[0, 0] // LZ % P_SIZE == 0)
+    affine_lanes = affine_lanes + jnp.where(base_lane[None, :], b_head[:, None], 0.0)
+    coupling_rows = jnp.concatenate(
+        [jnp.tanh(affine_lanes[:patch_len]), affine_lanes[patch_len:]], axis=0
+    ).reshape(2, P_SIZE, P_SIZE, P_SIZE * P_SIZE, LY * LZ)
+    coupling_lat = coupling_rows[:, :, :, 0]
+    for k in range(1, P_SIZE * P_SIZE):
+        offset = k // P_SIZE * LZ + k % P_SIZE
+        coupling_lat = coupling_lat + jnp.roll(coupling_rows[:, :, :, k], offset, axis=-1)
     scale_lat = coupling_lat[0]
     shift_lat = coupling_lat[1]
+    log_det = jnp.sum(jnp.where(frozen, 0.0, scale_lat))
     new_field = jnp.where(frozen, u, u * jnp.exp(scale_lat) + shift_lat)
 
     ahead_time = shifted(new_field[0:1].astype(jnp.bfloat16), "tm", -1).astype(jnp.float32)
@@ -187,7 +196,9 @@
     slab_link = new_field * next_slab_field
     local_log = -0.5 * jnp.sum(u * u) - log_det
     local_act = jnp.sum(density)
-    sums = doubling_sum(doubling_sum(jnp.stack([local_log, local_act]), "tm"), "space")
+    members = lax.axis_size("space") * lax.axis_size("tm")
+    partials = jnp.broadcast_to(jnp.stack([local_log, local_act])[None], (members, 2))
+    sums = jnp.sum(lax.all_to_all(partials, ("space", "tm"), 0, 0, tiled=True), axis=0)
     sum_log, sum_act = sums[0], sums[1]
     site_count = u.size * lax.axis_size("space") * lax.axis_size("tm")
     totals = jnp.stack([sum_log / site_count - 0.5 * log_two_pi, sum_act / site_count]).astype(

time: 188 us -> 158 us (0.84)
  the two profiles are of different devices: /device:TPU:30 before, /device:TPU:1 now
where the time goes in v3:
time: 158 us; the launch traced here: 157 us
  starting transfers between devices  46.6 us (29%)
  blocking collectives  40.3 us (26%)
  local copies, waits for them, and re-layouts  31 us (20%)
  other arithmetic  13.7 us (9%)
  matrix products  13.5 us (9%)
  waiting for transfers between devices  7.79 us (5%)
  between operations  4.1 us (3%)
    all_to_all x1, blocking collectives, shards(): lax.all_to_all(partials, ('space', 'tm'), 0, 0, tiled=True)  40.3 us
    ppermute x4, starting transfers between devices, exchange(): return lax.ppermute(x, axis, [(i, i ^ bit) for i in range(length)])  25.3 us
    ppermute x2, starting transfers between devices, shifted(): lax.ppermute(x, axis, [(i, (i + by) % length) for i in range(length)])  21.3 us
    ppermute x4, waiting for transfers between devices, exchange(): return lax.ppermute(x, axis, [(i, i ^ bit) for i in range(length)])  6.7 us
    unnamed x50, local copies, waits for them, and re-layouts  5.1 us
    dot_general x1, matrix products, shards(): jnp.einsum('cj,cl->jl', w_head, normed_lanes, preferred_element_type=jnp....  4.77 us
    slice x1, local copies, waits for them, and re-layouts, shards(): coupling_lat = coupling_rows[:, :, :, 0]  4.48 us
    slice x2, local copies, waits for them, and re-layouts, shards(): keys = kv[:, :D].reshape(n_sel * tokens_dev, HEADS, HS)  3.56 us
  transfers between devices with their start and end apart: 6, of which 3 were waited for; matrix products, arithmetic and copies ran while one was open for 5% of the time, Pallas kernels for 0%

profile of v3, /device:TPU:1, one launch (start us, length us, event | category | flops | bytes accessed | tf_op | source)
XLA Modules:
  0.0 156.9 jit_solution(9768524440884454405)
XLA Ops:
  1.3 1.4 convert_bitcast_fusion
  4.1 2.2 %reshape.205 = bf16[2,4,8,4,16,4]{5,4,3,2,1,0:T(8,128)(2,1)S(1)} reshape(bf16[2,4,2048]{2,1,0:T(4,128)(2,1)S(1)} %slice_add_fusion) | data formatting | bytes 65536 | tf_op jit(solution)/shard_map/reshape | solution.py:103
  6.4 1.7 %copy.108 = bf16[8,16,2,4,4,4]{1,0,5,4,3,2:T(8,128)(2,1)S(1)} copy(bf16[8,16,2,4,4,4]{5,1,4,0,3,2:T(8,128)(2,1)S(1)} %bitcast.123) | data formatting | bytes 65536 | tf_op jit(solution)/shard_map/transpose | solution.py:104
  8.4 9.6 %collective-permute-start = (bf16[1,129,128]{1,2,0:T(8,128)(2,1)S(1)}, bf16[1,129,128]{1,2,0:T(8,128)(2,1)S(1)}, u32[]{:S(2)}, u32[]{:S(2)}) collective-permute-start(bf16[1,129,128]{1,2,0:T(8,128)(2,1)S(1)} %maximum_bitcast_fusion), channel_id=1, source_target_pairs={{0,8},{1,9},{2,10},{3,11},{4,12},{5,13},{6,14},{7,15},{8,0},{9,1},... | collective-permute-start | bytes 99080 | tf_op jit(solution)/shard_map/ppermute | solution.py:26
  21.5 1.6 %fusion.16 = bf16[128,768]{1,0:T(8,128)(2,1)S(1)} fusion(bf16[768,2304]{1,0:T(8,128)(2,1)} %param.21, f32[128,768]{1,0:T(8,128)S(1)} %get-tuple-element.12, f32[768]{0:T(1024)S(1)} %copy-done.12, f32[128]{0:T(128)S(1)} %add_rsqrt_fusion.2, f32[128]{0:T(128)S(1)} %broadcast_multiply_fusion.2), kind=kOutput, calls=%fused_computation.27 | convolution fusion | flops 151486464 | bytes 1773568 | tf_op jit(solution)/shard_map/dot_general | solution.py:118
  23.3 4.9 %collective-permute-start.1 = (bf16[2,129,128]{1,2,0:T(8,128)(2,1)S(1)}, bf16[2,129,128]{1,2,0:T(8,128)(2,1)S(1)}, u32[]{:S(2)}, u32[]{:S(2)}) collective-permute-start(bf16[2,129,128]{1,2,0:T(8,128)(2,1)S(1)} %pad_maximum_fusion.3), channel_id=1, source_target_pairs={{0,4},{1,5},{2,6},{3,7},{4,0},{5,1},{6,2},{7,3},{8,12},{9,13},{10,... | collective-permute-start | bytes 198152 | tf_op jit(solution)/shard_map/ppermute | solution.py:26
  28.2 2.3 %collective-permute-done.1 = bf16[2,129,128]{1,2,0:T(8,128)(2,1)S(1)} collective-permute-done((bf16[2,129,128]{1,2,0:T(8,128)(2,1)S(1)}, bf16[2,129,128]{1,2,0:T(8,128)(2,1)S(1)}, u32[]{:S(2)}, u32[]{:S(2)}) %collective-permute-start.1) | collective-permute-done | bytes 66080 | tf_op jit(solution)/shard_map/ppermute | solution.py:26
  30.6 6.7 %collective-permute-start.2 = (bf16[4,129,128]{1,2,0:T(8,128)(2,1)S(1)}, bf16[4,129,128]{1,2,0:T(8,128)(2,1)S(1)}, u32[]{:S(2)}, u32[]{:S(2)}) collective-permute-start(bf16[4,129,128]{1,2,0:T(8,128)(2,1)S(1)} %pad_maximum_fusion.2), channel_id=1, source_target_pairs={{0,2},{1,3},{2,0},{3,1},{4,6},{5,7},{6,4},{7,5},{8,10},{9,11},{10,... | collective-permute-start | bytes 396296 | tf_op jit(solution)/shard_map/ppermute | solution.py:26
  38.1 4.3 %collective-permute-done.2 = bf16[4,129,128]{1,2,0:T(8,128)(2,1)S(1)} collective-permute-done((bf16[4,129,128]{1,2,0:T(8,128)(2,1)S(1)}, bf16[4,129,128]{1,2,0:T(8,128)(2,1)S(1)}, u32[]{:S(2)}, u32[]{:S(2)}) %collective-permute-start.2) | collective-permute-done | bytes 132128 | tf_op jit(solution)/shard_map/ppermute | solution.py:26
  42.6 4.0 %collective-permute-start.3 = (bf16[8,129,128]{1,2,0:T(8,128)(2,1)S(1)}, bf16[8,129,128]{1,2,0:T(8,128)(2,1)S(1)}, u32[]{:S(2)}, u32[]{:S(2)}) collective-permute-start(bf16[8,129,128]{1,2,0:T(8,128)(2,1)S(1)} %pad_maximum_fusion.1), channel_id=1, source_target_pairs={{0,1},{1,0},{2,3},{3,2},{4,5},{5,4},{6,7},{7,6},{8,9},{9,8},{10,11... | collective-permute-start | bytes 792584 | tf_op jit(solution)/shard_map/ppermute | solution.py:26
  49.4 1.8 %gather_fusion.3 = bf16[8,129,128]{1,2,0:T(8,128)(2,1)S(1)} fusion(bf16[16,129,128]{1,2,0:T(8,128)(2,1)} %constant_dynamic-update-slice_fusion.2, s32[1024]{0:T(1024)S(1)} %pad_clamp_fusion), kind=kCustom, calls=%fused_computation.3 | custom fusion | bytes 528416 | tf_op jit(solution)/shard_map/jit(_take)/gather | solution.py:124
  54.8 3.1 %convolution_convert_fusion = bf16[1024,1536]{1,0:T(8,128)(2,1)S(1)} fusion(bf16[768,2304]{1,0:T(8,128)(2,1)S(1)} %copy-done.11, f32[1024,768]{1,0:T(8,128)S(1)} %get-tuple-element.14, f32[768]{0:T(1024)S(1)} %copy-done.12, f32[1024]{0:T(1024)S(1)} %add_rsqrt_fusion, f32[1024]{0:T(1024)S(1)} %broadcast_multiply_fusion), kind=kOutput, calls=%fused_computation.10 | convolution fusion | flops 2420637696 | bytes 8663040 | tf_op jit(solution)/shard_map/dot_general | solution.py:130
  57.9 1.9 %fusion.103 = (bf16[1024,768]{1,0:T(8,128)(2,1)}, bf16[1024,768]{1,0:T(8,128)(2,1)}) fusion(bf16[1024,1536]{1,0:T(8,128)(2,1)S(1)} %convolution_convert_fusion), kind=kLoop, calls=%fused_computation.180 | loop fusion | bytes 6291456 | tf_op jit(solution)/shard_map/slice | solution.py:133
  59.8 1.7 %copy.113 = bf16[1024,768]{0,1:T(8,128)(2,1)S(1)} copy(bf16[1024,768]{1,0:T(8,128)(2,1)} %get-tuple-element.33) | data formatting | bytes 3145728 | tf_op jit(solution)/shard_map/slice | solution.py:133
  61.5 2.6 %copy.111 = bf16[1024,768]{0,1:T(8,128)(2,1)} copy(bf16[1024,768]{1,0:T(8,128)(2,1)} %get-tuple-element.34) | data formatting | bytes 3145728 | tf_op jit(solution)/shard_map/slice | solution.py:134
  66.6 1.6 %fusion.19 = f32[128,12,64]{0,2,1:T(8,128)S(1)} fusion(bf16[1024,12,64]{0,2,1:T(8,128)(2,1)S(1)} %bitcast.122, f32[12,128,1024]{2,1,0:T(8,128)S(1)} %get-tuple-element.44, f32[12,128]{1,0:T(8,128)S(1)} %get-tuple-element.43, f32[128,12]{0,1:T(8,128)S(1)} %bitcast.158), kind=kOutput, calls=%fused_computation.29 | convolution fusion | flops 206143488 | bytes 8269824 | tf_op jit(solution)/shard_map/hqk,khd->qhd/dot_general | solution.py:145
  68.8 4.8 %bitcast_add_fusion = f32[512,2048]{1,0:T(8,128)} fusion(bf16[768,512]{1,0:T(8,128)(2,1)S(1)} %copy-done, f32[512]{0:T(512)S(1)} %copy-done.14, pred[2048]{0:T(1024)(128)(4,1)S(1)} %fusion.84, s32[128]{0:T(128)S(1)} %get-tuple-element.56, s32[128]{0:T(128)S(1)} %get-tuple-element.57, s32[128]{0:T(128)S(1)} %get-tuple-element.55, ...), kind=kOutput, calls=%fused_computation.9 | convolution fusion | flops 2018902016 | bytes 5384448 | tf_op jit(solution)/shard_map/cj,cl->jl/dot_general | solution.py:161
  73.5 2.7 %slice_tanh_fusion = (f32[256,2048]{1,0:T(8,128)S(1)}, f32[256,2048]{1,0:T(8,128)S(1)}) fusion(f32[512,2048]{1,0:T(8,128)} %bitcast_add_fusion), kind=kLoop, calls=%fused_computation.20 | loop fusion | bytes 8388608 | tf_op jit(solution)/shard_map/tanh | solution.py:167
  76.5 4.5 %fusion.102 = (f32[2,4,4,1,2048]{4,3,2,1,0:T(1,128)S(1)}, f32[2,4,4,1,2048]{4,3,2,1,0:T(1,128)S(1)}, f32[2,4,4,1,2048]{4,3,2,1,0:T(1,128)S(1)}, f32[2,4,4,1,2048...) fusion(f32[2,4,4,16,2048]{4,3,2,1,0:T(8,128)S(1)} %bitcast.119), kind=kLoop, calls=%fused_computation.179 | loop fusion | bytes 8388608 | tf_op jit(solution)/shard_map/slice | solution.py:169
  84.0 2.0 %fusion.52 = f32[2,4,4,2048]{3,2,1,0:T(4,128)S(1)} fusion(f32[2,4,4,1855]{3,2,1,0:T(4,128)S(1)} %slice.393, f32[2,4,4,193]{3,2,1,0:T(4,128)S(1)} %slice.392, f32[2,4,4,1854]{3,2,1,0:T(4,128)S(1)} %slice.396, f32[2,4,4,194]{3,2,1,0:T(4,128)S(1)} %slice.395, f32[2,4,4,1853]{3,2,1,0:T(4,128)S(1)} %slice.399, f32[2,4,4,195]{3,2,1,0:T(4,128)S(1)} %slice.398, ...), kind=kLoop, calls=%fused_computation.63 | loop fusion | flops 1966080 | bytes 4456448 | tf_op jit(solution)/shard_map/add | solution.py:172
  86.8 19.1 %collective-permute-start.5 = (bf16[4,1,2048]{2,1,0:T(2,128)(2,1)S(1)}, bf16[4,1,2048]{2,1,0:T(2,128)(2,1)S(1)}, u32[]{:S(2)}, u32[]{:S(2)}) collective-permute-start(bf16[4,1,2048]{2,1,0:T(2,128)(2,1)S(1)} %slice.405), channel_id=1, source_target_pairs={{0,496},{16,0},{32,16},{48,32},{64,48},{80,64},{96,80},{112,96},{1... | collective-permute-start | bytes 49160 | tf_op jit(solution)/shard_map/ppermute | solution.py:52
  105.9 2.2 %collective-permute-start.4 = (bf16[1,4,2048]{2,1,0:T(4,128)(2,1)S(1)}, bf16[1,4,2048]{2,1,0:T(4,128)(2,1)S(1)}, u32[]{:S(2)}, u32[]{:S(2)}) collective-permute-start(bf16[1,4,2048]{2,1,0:T(4,128)(2,1)S(1)} %slice.403), channel_id=1, source_target_pairs={{0,15},{1,0},{2,1},{3,2},{4,3},{5,4},{6,5},{7,6},{8,7},{9,8},{10,9... | collective-permute-start | bytes 49160 | tf_op jit(solution)/shard_map/ppermute | solution.py:52
  111.0 1.6 %fusion.93 = (f32[]{:T(128)}, f32[4,4,2048]{2,1,0:T(4,128)}, f32[4,4,2048]{2,1,0:T(4,128)}, f32[4,4,2048]{2,1,0:T(4,128)}) fusion(f32[4,4,2048]{2,1,0:T(4,128)S(1)} %get-tuple-element.8, f32[4,4,1]{2,1,0:T(4,128)S(1)} %slice.411, f32[4,4,2047]{2,1,0:T(4,128)S(1)} %slice.410, f32[4,4,1985]{2,1,0:T(4,128)S(1)} %bitcast.120, f32[4,4,63]{2,1,0:T(4,128)S(1)} %slice.408, ...), kind=kLoop, calls=%fused_computation.174 | loop fusion | flops 720895 | bytes 1198084 | tf_op jit(solution)/shard_map/reduce_sum | solution.py:198
  113.5 40.3 %all_to_all.6 = f32[512,1,2]{2,1,0:T(1,128)S(1)} all-to-all(f32[512,1,2]{2,1,0:T(1,128)S(1)} %broadcast_in_dim.104), channel_id=1, replica_groups=mesh['space'=32,'tm'=16] {'space','tm'}, dimensions={0} | all-to-all | bytes 8192 | tf_op jit(solution)/shard_map/all_to_all | solution.py:201
  (150 shorter events, 24.2 us)
Async XLA Ops:
  0.6 68.1 %copy-start = (bf16[768,512]{1,0:T(8,128)(2,1)S(1)}, bf16[768,512]{1,0:T(8,128)(2,1)}, u32[]{:S(2)}) copy-start(bf16[768,512]{1,0:T(8,128)(2,1)} %param.23) | copy-start | bytes 2359300
  0.6 17.6 %copy-start.9 = (s32[128]{0:T(128)S(1)}, s32[128]{0:T(128)}, u32[]{:S(2)}) copy-start(s32[128]{0:T(128)} %constant.191) | copy-start | bytes 1540
  0.7 17.6 %copy-start.1 = (s32[16]{0:T(128)S(1)}, s32[16]{0:T(128)}, u32[]{:S(2)}) copy-start(s32[16]{0:T(128)} %constant.185.clone) | copy-start | bytes 196
  0.7 18.3 %copy-start.8 = (s32[128]{0:T(128)S(1)}, s32[128]{0:T(128)}, u32[]{:S(2)}) copy-start(s32[128]{0:T(128)} %constant.190) | copy-start | bytes 1540
  0.7 18.3 %copy-start.10 = (s32[1,1,128]{2,1,0:T(1,128)S(1)}, s32[1,1,128]{2,1,0:T(1,128)}, u32[]{:S(2)}) copy-start(s32[1,1,128]{2,1,0:T(1,128)} %param.16) | copy-start | bytes 1540
  0.7 17.4 %copy-start.7 = (s32[16,8]{0,1:T(8,128)S(1)}, s32[16,8]{0,1:T(8,128)}, u32[]{:S(2)}) copy-start(s32[16,8]{0,1:T(8,128)} %param.17) | copy-start | bytes 1540
  0.7 18.3 %copy-start.2 = (bf16[256,768]{1,0:T(8,128)(2,1)S(1)}, bf16[256,768]{1,0:T(8,128)(2,1)}, u32[]{:S(2)}) copy-start(bf16[256,768]{1,0:T(8,128)(2,1)} %param.18) | copy-start | bytes 1179652
  8.2 12.9 %copy-start.6 = (f32[768]{0:T(1024)S(1)}, f32[768]{0:T(1024)}, u32[]{:S(2)}) copy-start(f32[768]{0:T(1024)} %param.19) | copy-start | bytes 9220
  8.4 14.8 %collective-permute-start = (bf16[1,129,128]{1,2,0:T(8,128)(2,1)S(1)}, bf16[1,129,128]{1,2,0:T(8,128)(2,1)S(1)}, u32[]{:S(2)}, u32[]{:S(2)}) collective-permute-start(bf16[1,129,128]{1,2,0:T(8,128)(2,1)S(1)} %maximum_bitcast_fusion), channel_id=1, source_target_pairs={{0,8},{1,9},{2,10},{3,11},{4,12},{5,13},{6,14},{7,15},{8,0},{9,1},... | collective-permute-start | bytes 99080 | tf_op jit(solution)/shard_map/ppermute | solution.py:26
  19.0 2.5 %copy-start.12 = (f32[768]{0:T(1024)S(1)}, f32[768]{0:T(1024)}, u32[]{:S(2)}) copy-start(f32[768]{0:T(1024)} %param.20) | copy-start | bytes 9220
  23.3 7.3 %collective-permute-start.1 = (bf16[2,129,128]{1,2,0:T(8,128)(2,1)S(1)}, bf16[2,129,128]{1,2,0:T(8,128)(2,1)S(1)}, u32[]{:S(2)}, u32[]{:S(2)}) collective-permute-start(bf16[2,129,128]{1,2,0:T(8,128)(2,1)S(1)} %pad_maximum_fusion.3), channel_id=1, source_target_pairs={{0,4},{1,5},{2,6},{3,7},{4,0},{5,1},{6,2},{7,3},{8,12},{9,13},{10,... | collective-permute-start | bytes 198152 | tf_op jit(solution)/shard_map/ppermute | solution.py:26
  30.6 11.9 %collective-permute-start.2 = (bf16[4,129,128]{1,2,0:T(8,128)(2,1)S(1)}, bf16[4,129,128]{1,2,0:T(8,128)(2,1)S(1)}, u32[]{:S(2)}, u32[]{:S(2)}) collective-permute-start(bf16[4,129,128]{1,2,0:T(8,128)(2,1)S(1)} %pad_maximum_fusion.2), channel_id=1, source_target_pairs={{0,2},{1,3},{2,0},{3,1},{4,6},{5,7},{6,4},{7,5},{8,10},{9,11},{10,... | collective-permute-start | bytes 396296 | tf_op jit(solution)/shard_map/ppermute | solution.py:26
  42.6 6.0 %collective-permute-start.3 = (bf16[8,129,128]{1,2,0:T(8,128)(2,1)S(1)}, bf16[8,129,128]{1,2,0:T(8,128)(2,1)S(1)}, u32[]{:S(2)}, u32[]{:S(2)}) collective-permute-start(bf16[8,129,128]{1,2,0:T(8,128)(2,1)S(1)} %pad_maximum_fusion.1), channel_id=1, source_target_pairs={{0,1},{1,0},{2,3},{3,2},{4,5},{5,4},{6,7},{7,6},{8,9},{9,8},{10,11... | collective-permute-start | bytes 792584 | tf_op jit(solution)/shard_map/ppermute | solution.py:26
  52.8 2.0 %copy-start.11 = (bf16[768,2304]{1,0:T(8,128)(2,1)S(1)}, bf16[768,2304]{1,0:T(8,128)(2,1)}, u32[]{:S(2)}) copy-start(bf16[768,2304]{1,0:T(8,128)(2,1)} %param.21) | copy-start | bytes 10616836
  65.2 1.4 copy-start.4
  66.6 2.1 %copy-start.13 = (f32[768]{0:T(1024)S(1)}, f32[768]{0:T(1024)}, u32[]{:S(2)}) copy-start(f32[768]{0:T(1024)} %param.22) | copy-start | bytes 9220
  66.6 2.1 %copy-start.14 = (f32[512]{0:T(512)S(1)}, f32[512]{0:T(512)}, u32[]{:S(2)}) copy-start(f32[512]{0:T(512)} %param.24) | copy-start | bytes 6148
  83.4 2.5 %copy-start.5 = (f32[4,4,2048]{2,1,0:T(4,128)S(1)}, f32[4,4,2048]{2,1,0:T(4,128)}, u32[]{:S(2)}) copy-start(f32[4,4,2048]{2,1,0:T(4,128)} %param.15) | copy-start | bytes 393220
  86.8 70.1 %copy-start.3 = (f32[4,4,2048]{2,1,0:T(4,128)}, f32[4,4,2048]{2,1,0:T(4,128)S(1)}, u32[]{:S(2)}) copy-start(f32[4,4,2048]{2,1,0:T(4,128)S(1)} %get-tuple-element.8) | copy-start | bytes 393220
  86.8 23.1 %collective-permute-start.5 = (bf16[4,1,2048]{2,1,0:T(2,128)(2,1)S(1)}, bf16[4,1,2048]{2,1,0:T(2,128)(2,1)S(1)}, u32[]{:S(2)}, u32[]{:S(2)}) collective-permute-start(bf16[4,1,2048]{2,1,0:T(2,128)(2,1)S(1)} %slice.405), channel_id=1, source_target_pairs={{0,496},{16,0},{32,16},{48,32},{64,48},{80,64},{96,80},{112,96},{1... | collective-permute-start | bytes 49160 | tf_op jit(solution)/shard_map/ppermute | solution.py:52
  105.9 5.1 %collective-permute-start.4 = (bf16[1,4,2048]{2,1,0:T(4,128)(2,1)S(1)}, bf16[1,4,2048]{2,1,0:T(4,128)(2,1)S(1)}, u32[]{:S(2)}, u32[]{:S(2)}) collective-permute-start(bf16[1,4,2048]{2,1,0:T(4,128)(2,1)S(1)} %slice.403), channel_id=1, source_target_pairs={{0,15},{1,0},{2,1},{3,2},{4,3},{5,4},{6,5},{7,6},{8,7},{9,8},{10,9... | collective-permute-start | bytes 49160 | tf_op jit(solution)/shard_map/ppermute | solution.py:52

commit v4 on v3

--- a/solution.py
+++ b/solution.py
@@ -115,9 +115,6 @@
     bits_own = bits.reshape(tokens_dev).astype(jnp.float32)
     embedded = embed_packed(tokens, bits_own, w_pair, b_embed)
     normed = layer_norm(embedded, gain_in).astype(jnp.bfloat16)
-    queries = jnp.dot(normed, w_qkv[:, :D], preferred_element_type=jnp.float32).astype(
-        jnp.bfloat16
-    )
 
     block_rows = lax.dynamic_index_in_dim(block_list, lax.axis_index("tm"), 0, keepdims=False)
     own = lax.axis_index("tm")
@@ -127,23 +124,25 @@
     sel_bits = chosen[:, tokens_dev, :].reshape(n_sel * tokens_dev).astype(jnp.float32)
     sel_embedded = embed_packed(sel_tokens, sel_bits, w_pair, b_embed)
     sel_normed = layer_norm(sel_embedded, gain_in).astype(jnp.bfloat16)
-    kv = jnp.dot(sel_normed, w_qkv[:, D:], preferred_element_type=jnp.float32).astype(
-        jnp.bfloat16
-    )
-    keys = kv[:, :D].reshape(n_sel * tokens_dev, HEADS, HS)
-    values = kv[:, D:].reshape(n_sel * tokens_dev, HEADS, HS)
+    w_heads = w_qkv.reshape(D, 3, HEADS, HS)
+    queries = jnp.einsum(
+        "tc,chd->htd", normed, w_heads[:, 0], preferred_element_type=jnp.float32
+    ).astype(jnp.bfloat16)
+    keys_t = jnp.einsum(
+        "tc,chd->hdt", sel_normed, w_heads[:, 1], preferred_element_type=jnp.float32
+    ).astype(jnp.bfloat16)
+    values = jnp.einsum(
+        "tc,chd->htd", sel_normed, w_heads[:, 2], preferred_element_type=jnp.float32
+    ).astype(jnp.bfloat16)
 
     scores = jnp.einsum(
-        "qhd,khd->hqk",
-        queries.reshape(tokens_dev, HEADS, HS),
-        keys,
-        preferred_element_type=jnp.float32,
+        "hqd,hdk->hqk", queries, keys_t, preferred_element_type=jnp.float32
     ) * HS ** (-0.5)
     row_top = jnp.max(scores, axis=-1, keepdims=True)
     exp_scores = jnp.exp(scores - row_top)
     row_total = jnp.sum(exp_scores, axis=-1)
     product = jnp.einsum(
-        "hqk,khd->qhd",
+        "hqk,hkd->qhd",
         exp_scores.astype(jnp.bfloat16),
         values,
         preferred_element_type=jnp.float32,
@@ -158,18 +157,23 @@
     normed_lanes = jnp.einsum(
         "tc,tl->cl", normed_out, spread_tok, preferred_element_type=jnp.float32
     ).astype(jnp.bfloat16)
+    n_off = P_SIZE * P_SIZE
+    w_rows = w_head.reshape(D, 2 * P_SIZE * P_SIZE, n_off)
     affine_lanes = jnp.einsum(
-        "cj,cl->jl", w_head, normed_lanes, preferred_element_type=jnp.float32
+        "crk,cl->krl", w_rows, normed_lanes, preferred_element_type=jnp.float32
     )
     base_lane = (lane[0, 0] % P_SIZE == 0) & (lane[0, 0] // LZ % P_SIZE == 0)
-    affine_lanes = affine_lanes + jnp.where(base_lane[None, :], b_head[:, None], 0.0)
+    bias_rows = b_head.reshape(2 * P_SIZE * P_SIZE, n_off).T
+    affine_lanes = affine_lanes + jnp.where(base_lane[None, None, :], bias_rows[:, :, None], 0.0)
+    half_rows = P_SIZE * P_SIZE
     coupling_rows = jnp.concatenate(
-        [jnp.tanh(affine_lanes[:patch_len]), affine_lanes[patch_len:]], axis=0
-    ).reshape(2, P_SIZE, P_SIZE, P_SIZE * P_SIZE, LY * LZ)
-    coupling_lat = coupling_rows[:, :, :, 0]
-    for k in range(1, P_SIZE * P_SIZE):
+        [jnp.tanh(affine_lanes[:, :half_rows]), affine_lanes[:, half_rows:]], axis=1
+    )
+    coupling_lat = coupling_rows[0]
+    for k in range(1, n_off):
         offset = k // P_SIZE * LZ + k % P_SIZE
-        coupling_lat = coupling_lat + jnp.roll(coupling_rows[:, :, :, k], offset, axis=-1)
+        coupling_lat = coupling_lat + jnp.roll(coupling_rows[k], offset, axis=-1)
+    coupling_lat = coupling_lat.reshape(2, P_SIZE, P_SIZE, LY * LZ)
     scale_lat = coupling_lat[0]
     shift_lat = coupling_lat[1]
     log_det = jnp.sum(jnp.where(frozen, 0.0, scale_lat))

time: 158 us -> 157 us (level)
  blocking collectives: 40.3 us -> 48.6 us
  starting transfers between devices: 46.6 us -> 39.1 us
    all_to_all x1, blocking collectives: 40.3 us -> 48.6 us  [shards(): lax.all_to_all(partials, ('space', 'tm'), 0, 0, tiled=True)]
    slice x27 -> x24, local copies, waits for them, and re-layouts: 11.9 us -> 4.47 us  [the longest x1 3.3 us: shards(): w_heads[:, 2]]
    unnamed x50 -> x35, local copies, waits for them, and re-layouts: 5.1 us -> 11.4 us
    dot_general x5 -> x3, matrix products: 12.2 us -> 7.68 us  [the longest x1 4.77 us: shards(): jnp.einsum('crk,cl->krl', w_rows, normed_lanes, preferred_element_type=jn...]
    ppermute x2, starting transfers between devices: 21.3 us -> 17.1 us  [shifted(): lax.ppermute(x, axis, [(i, (i + by) % length) for i in range(length)])]
    unnamed x0 -> x3, matrix products: none -> 3.8 us
    ppermute x4, starting transfers between devices: 25.3 us -> 22 us  [exchange(): return lax.ppermute(x, axis, [(i, i ^ bit) for i in range(length)])]
  transfers between devices with their start and end apart: 6 -> 6, of which waited for: 3 -> 2; matrix products, arithmetic and copies ran while one was open for 5% -> 12% of each run, Pallas kernels for 0% -> 0%
where the time goes in v4:
time: 157 us
  blocking collectives  48.6 us (31%)
  starting transfers between devices  39.1 us (25%)
  local copies, waits for them, and re-layouts  30.1 us (19%)
  other arithmetic  14.1 us (9%)
  matrix products  12.7 us (8%)
  waiting for transfers between devices  7.95 us (5%)
  between operations  4.01 us (3%)
    all_to_all x1, blocking collectives, shards(): lax.all_to_all(partials, ('space', 'tm'), 0, 0, tiled=True)  48.6 us
    ppermute x4, starting transfers between devices, exchange(): return lax.ppermute(x, axis, [(i, i ^ bit) for i in range(length)])  22 us
    ppermute x2, starting transfers between devices, shifted(): lax.ppermute(x, axis, [(i, (i + by) % length) for i in range(length)])  17.1 us
    unnamed x35, local copies, waits for them, and re-layouts  11.4 us
    ppermute x4, waiting for transfers between devices, exchange(): return lax.ppermute(x, axis, [(i, i ^ bit) for i in range(length)])  7.95 us
    dot_general x1, matrix products, shards(): jnp.einsum('crk,cl->krl', w_rows, normed_lanes, preferred_element_type=jn...  4.77 us
    unnamed x3, matrix products  3.8 us
    slice x1, local copies, waits for them, and re-layouts, shards(): w_heads[:, 2]  3.3 us
  transfers between devices with their start and end apart: 6, of which 2 were waited for; matrix products, arithmetic and copies ran while one was open for 12% of the time, Pallas kernels for 0%

profile of v4, /device:TPU:1, one launch (start us, length us, event | category | flops | bytes accessed | tf_op | source)
XLA Modules:
  0.0 156.5 jit_solution(6456723720120408473)
XLA Ops:
  1.3 1.4 convert_bitcast_fusion
  4.3 2.2 %reshape.211 = bf16[2,4,8,4,16,4]{5,4,3,2,1,0:T(8,128)(2,1)S(1)} reshape(bf16[2,4,2048]{2,1,0:T(4,128)(2,1)S(1)} %slice_add_fusion) | data formatting | bytes 65536 | tf_op jit(solution)/shard_map/reshape | solution.py:103
  6.5 1.7 %copy.45 = bf16[8,16,2,4,4,4]{1,0,5,4,3,2:T(8,128)(2,1)S(1)} copy(bf16[8,16,2,4,4,4]{5,1,4,0,3,2:T(8,128)(2,1)S(1)} %bitcast.119) | data formatting | bytes 65536 | tf_op jit(solution)/shard_map/transpose | solution.py:104
  8.4 9.6 %collective-permute-start = (bf16[1,129,128]{1,2,0:T(8,128)(2,1)S(1)}, bf16[1,129,128]{1,2,0:T(8,128)(2,1)S(1)}, u32[]{:S(2)}, u32[]{:S(2)}) collective-permute-start(bf16[1,129,128]{1,2,0:T(8,128)(2,1)S(1)} %maximum_bitcast_fusion), channel_id=1, source_target_pairs={{0,8},{1,9},{2,10},{3,11},{4,12},{5,13},{6,14},{7,15},{8,0},{9,1},... | collective-permute-start | bytes 99080 | tf_op jit(solution)/shard_map/ppermute | solution.py:26
  21.5 5.8 %copy.48 = bf16[768,2304]{0,1:T(8,128)(2,1)} copy(bf16[768,2304]{1,0:T(8,128)(2,1)} %param.21) | data formatting | bytes 7077888 | tf_op args[6]
  27.3 3.3 %fusion.139 = (bf16[768,1,12,64]{0,3,2,1:T(8,128)(2,1)S(1)}, bf16[768,1,12,64]{0,3,2,1:T(8,128)(2,1)}, bf16[768,1,12,64]{0,3,2,1:T(8,128)(2,1)S(1)}) fusion(bf16[768,3,12,64]{0,3,2,1:T(8,128)(2,1)} %bitcast.116), kind=kLoop, calls=%fused_computation.231 | loop fusion | bytes 7077888 | tf_op jit(solution)/shard_map/slice | solution.py:135
  31.2 4.9 %collective-permute-start.1 = (bf16[2,129,128]{1,2,0:T(8,128)(2,1)S(1)}, bf16[2,129,128]{1,2,0:T(8,128)(2,1)S(1)}, u32[]{:S(2)}, u32[]{:S(2)}) collective-permute-start(bf16[2,129,128]{1,2,0:T(8,128)(2,1)S(1)} %pad_maximum_fusion.3), channel_id=1, source_target_pairs={{0,4},{1,5},{2,6},{3,7},{4,0},{5,1},{6,2},{7,3},{8,12},{9,13},{10,... | collective-permute-start | bytes 198152 | tf_op jit(solution)/shard_map/ppermute | solution.py:26
  36.1 5.7 %collective-permute-done.1 = bf16[2,129,128]{1,2,0:T(8,128)(2,1)S(1)} collective-permute-done((bf16[2,129,128]{1,2,0:T(8,128)(2,1)S(1)}, bf16[2,129,128]{1,2,0:T(8,128)(2,1)S(1)}, u32[]{:S(2)}, u32[]{:S(2)}) %collective-permute-start.1) | collective-permute-done | bytes 66080 | tf_op jit(solution)/shard_map/ppermute | solution.py:26
  42.6 3.4 %collective-permute-start.2 = (bf16[4,129,128]{1,2,0:T(8,128)(2,1)}, bf16[4,129,128]{1,2,0:T(8,128)(2,1)S(1)}, u32[]{:S(2)}, u32[]{:S(2)}) collective-permute-start(bf16[4,129,128]{1,2,0:T(8,128)(2,1)} %pad_maximum_fusion.2), channel_id=1, source_target_pairs={{0,2},{1,3},{2,0},{3,1},{4,6},{5,7},{6,4},{7,5},{8,10},{9,11},{10,... | collective-permute-start | bytes 396296 | tf_op jit(solution)/shard_map/ppermute | solution.py:26
  46.2 2.3 %copy.50 = bf16[768,512]{0,1:T(8,128)(2,1)} copy(bf16[768,512]{1,0:T(8,128)(2,1)} %param.23) | data formatting | bytes 1572864 | tf_op args[8]
  49.2 2.3 %collective-permute-done.2 = bf16[4,129,128]{1,2,0:T(8,128)(2,1)S(1)} collective-permute-done((bf16[4,129,128]{1,2,0:T(8,128)(2,1)}, bf16[4,129,128]{1,2,0:T(8,128)(2,1)S(1)}, u32[]{:S(2)}, u32[]{:S(2)}) %collective-permute-start.2) | collective-permute-done | bytes 132128 | tf_op jit(solution)/shard_map/ppermute | solution.py:26
  51.5 4.1 %collective-permute-start.3 = (bf16[8,129,128]{1,2,0:T(8,128)(2,1)S(1)}, bf16[8,129,128]{1,2,0:T(8,128)(2,1)S(1)}, u32[]{:S(2)}, u32[]{:S(2)}) collective-permute-start(bf16[8,129,128]{1,2,0:T(8,128)(2,1)S(1)} %pad_maximum_fusion), channel_id=1, source_target_pairs={{0,1},{1,0},{2,3},{3,2},{4,5},{5,4},{6,7},{7,6},{8,9},{9,8},{10,11... | collective-permute-start | bytes 792584 | tf_op jit(solution)/shard_map/ppermute | solution.py:26
  58.5 1.8 %gather_fusion.3 = bf16[8,129,128]{1,2,0:T(8,128)(2,1)S(1)} fusion(bf16[16,129,128]{1,2,0:T(8,128)(2,1)} %constant_dynamic-update-slice_fusion.2, s32[1024]{0:T(1024)S(1)} %pad_clamp_fusion), kind=kCustom, calls=%fused_computation.3 | custom fusion | bytes 528416 | tf_op jit(solution)/shard_map/jit(_take)/gather | solution.py:121
  63.7 1.6 %fusion.129 = f32[1024,768]{0,1:S(1)} fusion(bf16[768,768]{0,1:T(8,128)(2,1)S(1)} %bitcast.126, f32[1024,768]{1,0:T(8,128)S(1)} %get-tuple-element.14, f32[768]{0:T(1024)S(1)} %copy-done.7, f32[1024]{0:T(1024)S(1)} %add_rsqrt_fusion, f32[1024]{0:T(1024)S(1)} %broadcast_multiply_fusion), kind=kOutput, calls=%fused_computation.224 | convolution fusion | flops 1211105280 | bytes 7482368
  65.4 1.6 %fusion.130 = f32[1024,768]{0,1:S(1)} fusion(bf16[768,768]{0,1:T(8,128)(2,1)S(1)} %bitcast.125, f32[1024,768]{1,0:T(8,128)S(1)} %get-tuple-element.14, f32[768]{0:T(1024)S(1)} %copy-done.7, f32[1024]{0:T(1024)S(1)} %add_rsqrt_fusion, f32[1024]{0:T(1024)S(1)} %broadcast_multiply_fusion), kind=kOutput, calls=%fused_computation.225 | convolution fusion | flops 1211105280 | bytes 7482368
  67.0 1.1 multiply_reduce_fusion
  68.1 1.3 fusion
  69.5 1.8 %fusion.18 = f32[128,12,64]{0,2,1:T(8,128)S(1)} fusion(f32[12,128,1024]{2,1,0:T(8,128)S(1)} %get-tuple-element.46, f32[12,128]{1,0:T(8,128)S(1)} %get-tuple-element.45, f32[1024,12,64]{0,2,1:T(8,128)S(1)} %bitcast.120, f32[128,12]{0,1:T(8,128)S(1)} %bitcast.137), kind=kOutput, calls=%fused_computation.56 | convolution fusion | flops 206929920 | bytes 9842688 | tf_op jit(solution)/shard_map/hqk,hkd->qhd/dot_general | solution.py:144
  71.8 4.8 %bitcast_add_fusion = f32[16,32,2048]{2,1,0:T(8,128)} fusion(f32[16,32]{1,0:T(8,128)S(1)} %copy.52, pred[2048]{0:T(1024)(128)(4,1)S(1)} %fusion.120, bf16[768,32,16]{0,2,1:T(8,128)(2,1)S(1)} %bitcast.134, s32[128]{0:T(128)S(1)} %get-tuple-element.58, s32[128]{0:T(128)S(1)} %get-tuple-element.59, s32[128]{0:T(128)S(1)} %get-tuple-element.57, ...), kind=kOutput, calls=%fused_computation.38 | convolution fusion | flops 2018902016 | bytes 5384448 | tf_op jit(solution)/shard_map/crk,cl->krl/dot_general | solution.py:162
  76.6 2.7 %slice_tanh_fusion = (f32[16,16,2048]{2,1,0:T(8,128)S(1)}, f32[16,16,2048]{2,1,0:T(8,128)S(1)}) fusion(f32[16,32,2048]{2,1,0:T(8,128)} %bitcast_add_fusion), kind=kLoop, calls=%fused_computation.48 | loop fusion | bytes 8388608 | tf_op jit(solution)/shard_map/tanh | solution.py:170
  83.4 1.9 %collective-permute-start.4 = (bf16[1,4,2048]{2,1,0:T(4,128)(2,1)S(1)}, bf16[1,4,2048]{2,1,0:T(4,128)(2,1)S(1)}, u32[]{:S(2)}, u32[]{:S(2)}) collective-permute-start(bf16[1,4,2048]{2,1,0:T(4,128)(2,1)S(1)} %slice.416), channel_id=1, source_target_pairs={{0,15},{1,0},{2,1},{3,2},{4,3},{5,4},{6,5},{7,6},{8,7},{9,8},{10,9... | collective-permute-start | bytes 49160 | tf_op jit(solution)/shard_map/ppermute | solution.py:52
  85.4 15.1 %collective-permute-start.5 = (bf16[4,1,2048]{2,1,0:T(2,128)(2,1)S(1)}, bf16[4,1,2048]{2,1,0:T(2,128)(2,1)S(1)}, u32[]{:S(2)}, u32[]{:S(2)}) collective-permute-start(bf16[4,1,2048]{2,1,0:T(2,128)(2,1)S(1)} %slice.418), channel_id=1, source_target_pairs={{0,496},{16,0},{32,16},{48,32},{64,48},{80,64},{96,80},{112,96},{1... | collective-permute-start | bytes 49160 | tf_op jit(solution)/shard_map/ppermute | solution.py:52
  102.3 1.6 %fusion.131 = (f32[]{:T(128)}, f32[4,4,2048]{2,1,0:T(4,128)}, f32[4,4,2048]{2,1,0:T(4,128)}, f32[4,4,2048]{2,1,0:T(4,128)}) fusion(f32[4,4,2048]{2,1,0:T(4,128)S(1)} %get-tuple-element.8, f32[4,4,1]{2,1,0:T(4,128)S(1)} %slice.424, f32[4,4,2047]{2,1,0:T(4,128)S(1)} %slice.423, f32[4,4,1985]{2,1,0:T(4,128)S(1)} %bitcast.117, f32[4,4,63]{2,1,0:T(4,128)S(1)} %slice.421, ...), kind=kLoop, calls=%fused_computation.226 | loop fusion | flops 720895 | bytes 1198084 | tf_op jit(solution)/shard_map/reduce_sum | solution.py:202
  104.8 48.6 %all_to_all.6 = f32[512,1,2]{2,1,0:T(1,128)S(1)} all-to-all(f32[512,1,2]{2,1,0:T(1,128)S(1)} %broadcast_in_dim.107), channel_id=1, replica_groups=mesh['space'=32,'tm'=16] {'space','tm'}, dimensions={0} | all-to-all | bytes 8192 | tf_op jit(solution)/shard_map/all_to_all | solution.py:205
  (140 shorter events, 22.0 us)
Async XLA Ops:
  0.6 18.4 %copy-start = (bf16[256,768]{1,0:T(8,128)(2,1)S(1)}, bf16[256,768]{1,0:T(8,128)(2,1)}, u32[]{:S(2)}) copy-start(bf16[256,768]{1,0:T(8,128)(2,1)} %param.18) | copy-start | bytes 1179652
  0.6 17.7 %copy-start.11 = (s32[128]{0:T(128)S(1)}, s32[128]{0:T(128)}, u32[]{:S(2)}) copy-start(s32[128]{0:T(128)} %constant.193) | copy-start | bytes 1540
  0.7 17.7 %copy-start.1 = (s32[16]{0:T(128)S(1)}, s32[16]{0:T(128)}, u32[]{:S(2)}) copy-start(s32[16]{0:T(128)} %constant.187.clone) | copy-start | bytes 196
  0.7 18.3 %copy-start.10 = (s32[128]{0:T(128)S(1)}, s32[128]{0:T(128)}, u32[]{:S(2)}) copy-start(s32[128]{0:T(128)} %constant.192) | copy-start | bytes 1540
  0.7 17.4 %copy-start.12 = (s32[1,1,128]{2,1,0:T(1,128)S(1)}, s32[1,1,128]{2,1,0:T(1,128)}, u32[]{:S(2)}) copy-start(s32[1,1,128]{2,1,0:T(1,128)} %param.16) | copy-start | bytes 1540
  0.7 17.4 %copy-start.8 = (s32[16,8]{0,1:T(8,128)S(1)}, s32[16,8]{0,1:T(8,128)}, u32[]{:S(2)}) copy-start(s32[16,8]{0,1:T(8,128)} %param.17) | copy-start | bytes 1540
  8.3 12.8 %copy-start.6 = (f32[768]{0:T(1024)S(1)}, f32[768]{0:T(1024)}, u32[]{:S(2)}) copy-start(f32[768]{0:T(1024)} %param.19) | copy-start | bytes 9220
  8.4 22.8 %collective-permute-start = (bf16[1,129,128]{1,2,0:T(8,128)(2,1)S(1)}, bf16[1,129,128]{1,2,0:T(8,128)(2,1)S(1)}, u32[]{:S(2)}, u32[]{:S(2)}) collective-permute-start(bf16[1,129,128]{1,2,0:T(8,128)(2,1)S(1)} %maximum_bitcast_fusion), channel_id=1, source_target_pairs={{0,8},{1,9},{2,10},{3,11},{4,12},{5,13},{6,14},{7,15},{8,0},{9,1},... | collective-permute-start | bytes 99080 | tf_op jit(solution)/shard_map/ppermute | solution.py:26
  27.3 3.3 %copy-start.7 = (f32[768]{0:T(1024)S(1)}, f32[768]{0:T(1024)}, u32[]{:S(2)}) copy-start(f32[768]{0:T(1024)} %param.20) | copy-start | bytes 9220
  27.3 18.8 %copy-start.9 = (f32[512]{0:T(512)S(1)}, f32[512]{0:T(512)}, u32[]{:S(2)}) copy-start(f32[512]{0:T(512)} %param.24) | copy-start | bytes 6148
  31.2 10.6 %collective-permute-start.1 = (bf16[2,129,128]{1,2,0:T(8,128)(2,1)S(1)}, bf16[2,129,128]{1,2,0:T(8,128)(2,1)S(1)}, u32[]{:S(2)}, u32[]{:S(2)}) collective-permute-start(bf16[2,129,128]{1,2,0:T(8,128)(2,1)S(1)} %pad_maximum_fusion.3), channel_id=1, source_target_pairs={{0,4},{1,5},{2,6},{3,7},{4,0},{5,1},{6,2},{7,3},{8,12},{9,13},{10,... | collective-permute-start | bytes 198152 | tf_op jit(solution)/shard_map/ppermute | solution.py:26
  42.6 8.9 %collective-permute-start.2 = (bf16[4,129,128]{1,2,0:T(8,128)(2,1)}, bf16[4,129,128]{1,2,0:T(8,128)(2,1)S(1)}, u32[]{:S(2)}, u32[]{:S(2)}) collective-permute-start(bf16[4,129,128]{1,2,0:T(8,128)(2,1)} %pad_maximum_fusion.2), channel_id=1, source_target_pairs={{0,2},{1,3},{2,0},{3,1},{4,6},{5,7},{6,4},{7,5},{8,10},{9,11},{10,... | collective-permute-start | bytes 396296 | tf_op jit(solution)/shard_map/ppermute | solution.py:26
  51.5 6.1 %collective-permute-start.3 = (bf16[8,129,128]{1,2,0:T(8,128)(2,1)S(1)}, bf16[8,129,128]{1,2,0:T(8,128)(2,1)S(1)}, u32[]{:S(2)}, u32[]{:S(2)}) collective-permute-start(bf16[8,129,128]{1,2,0:T(8,128)(2,1)S(1)} %pad_maximum_fusion), channel_id=1, source_target_pairs={{0,1},{1,0},{2,3},{3,2},{4,5},{5,4},{6,7},{7,6},{8,9},{9,8},{10,11... | collective-permute-start | bytes 792584 | tf_op jit(solution)/shard_map/ppermute | solution.py:26
  62.5 1.3 copy-start.3
  69.4 2.3 %copy-start.4 = (bf16[768,512]{0,1:T(8,128)(2,1)S(1)}, bf16[768,512]{0,1:T(8,128)(2,1)}, u32[]{:S(2)}) copy-start(bf16[768,512]{0,1:T(8,128)(2,1)} %copy.50) | copy-start | bytes 2359300
  69.4 2.3 %copy-start.13 = (f32[768]{0:T(1024)S(1)}, f32[768]{0:T(1024)}, u32[]{:S(2)}) copy-start(f32[768]{0:T(1024)} %param.22) | copy-start | bytes 9220
  80.8 1.8 %copy-start.5 = (f32[4,4,2048]{2,1,0:T(4,128)S(1)}, f32[4,4,2048]{2,1,0:T(4,128)}, u32[]{:S(2)}) copy-start(f32[4,4,2048]{2,1,0:T(4,128)} %param.15) | copy-start | bytes 393220
  83.4 73.1 %copy-start.2 = (f32[4,4,2048]{2,1,0:T(4,128)}, f32[4,4,2048]{2,1,0:T(4,128)S(1)}, u32[]{:S(2)}) copy-start(f32[4,4,2048]{2,1,0:T(4,128)S(1)} %get-tuple-element.8) | copy-start | bytes 393220
  83.4 18.8 %collective-permute-start.4 = (bf16[1,4,2048]{2,1,0:T(4,128)(2,1)S(1)}, bf16[1,4,2048]{2,1,0:T(4,128)(2,1)S(1)}, u32[]{:S(2)}, u32[]{:S(2)}) collective-permute-start(bf16[1,4,2048]{2,1,0:T(4,128)(2,1)S(1)} %slice.416), channel_id=1, source_target_pairs={{0,15},{1,0},{2,1},{3,2},{4,3},{5,4},{6,5},{7,6},{8,7},{9,8},{10,9... | collective-permute-start | bytes 49160 | tf_op jit(solution)/shard_map/ppermute | solution.py:52
  85.4 16.9 %collective-permute-start.5 = (bf16[4,1,2048]{2,1,0:T(2,128)(2,1)S(1)}, bf16[4,1,2048]{2,1,0:T(2,128)(2,1)S(1)}, u32[]{:S(2)}, u32[]{:S(2)}) collective-permute-start(bf16[4,1,2048]{2,1,0:T(2,128)(2,1)S(1)} %slice.418), channel_id=1, source_target_pairs={{0,496},{16,0},{32,16},{48,32},{64,48},{80,64},{96,80},{112,96},{1... | collective-permute-start | bytes 49160 | tf_op jit(solution)/shard_map/ppermute | solution.py:52

commit v5 on v4

--- a/solution.py
+++ b/solution.py
@@ -124,25 +124,26 @@
     sel_bits = chosen[:, tokens_dev, :].reshape(n_sel * tokens_dev).astype(jnp.float32)
     sel_embedded = embed_packed(sel_tokens, sel_bits, w_pair, b_embed)
     sel_normed = layer_norm(sel_embedded, gain_in).astype(jnp.bfloat16)
-    w_heads = w_qkv.reshape(D, 3, HEADS, HS)
-    queries = jnp.einsum(
-        "tc,chd->htd", normed, w_heads[:, 0], preferred_element_type=jnp.float32
-    ).astype(jnp.bfloat16)
-    keys_t = jnp.einsum(
-        "tc,chd->hdt", sel_normed, w_heads[:, 1], preferred_element_type=jnp.float32
-    ).astype(jnp.bfloat16)
-    values = jnp.einsum(
-        "tc,chd->htd", sel_normed, w_heads[:, 2], preferred_element_type=jnp.float32
-    ).astype(jnp.bfloat16)
+    queries = jnp.dot(normed, w_qkv[:, :D], preferred_element_type=jnp.float32).astype(
+        jnp.bfloat16
+    )
+    kv = jnp.dot(sel_normed, w_qkv[:, D:], preferred_element_type=jnp.float32).astype(
+        jnp.bfloat16
+    )
+    keys = kv[:, :D].reshape(n_sel * tokens_dev, HEADS, HS)
+    values = kv[:, D:].reshape(n_sel * tokens_dev, HEADS, HS)
 
     scores = jnp.einsum(
-        "hqd,hdk->hqk", queries, keys_t, preferred_element_type=jnp.float32
+        "qhd,khd->hqk",
+        queries.reshape(tokens_dev, HEADS, HS),
+        keys,
+        preferred_element_type=jnp.float32,
     ) * HS ** (-0.5)
     row_top = jnp.max(scores, axis=-1, keepdims=True)
     exp_scores = jnp.exp(scores - row_top)
     row_total = jnp.sum(exp_scores, axis=-1)
     product = jnp.einsum(
-        "hqk,hkd->qhd",
+        "hqk,khd->qhd",
         exp_scores.astype(jnp.bfloat16),
         values,
         preferred_element_type=jnp.float32,

time: 157 us -> 149 us (0.949)
  blocking collectives: 48.6 us -> 40.7 us
  local copies, waits for them, and re-layouts: 30.1 us -> 23.4 us
  other arithmetic: 14.1 us -> 16.3 us
  matrix products: 12.7 us -> 14.5 us
    unnamed x35 -> x76, local copies, waits for them, and re-layouts: 11.4 us -> 3.36 us
    all_to_all x1, blocking collectives: 48.6 us -> 40.7 us  [shards(): lax.all_to_all(partials, ('space', 'tm'), 0, 0, tiled=True)]
    dot_general x2 -> x4, matrix products: 2.91 us -> 8.43 us  [the longest x1 3.14 us: shards(): jnp.dot(sel_normed, w_qkv[:, D:], preferred_element_type=jnp.float32)]
    unnamed x3 -> x0, matrix products: 3.8 us -> none
    ppermute x2, starting transfers between devices: 17.1 us -> 18.7 us  [shifted(): lax.ppermute(x, axis, [(i, (i + by) % length) for i in range(length)])]
    slice x1 -> x3, local copies, waits for them, and re-layouts: 3.3 us -> 4.76 us  [the longest x2 3.09 us: shards(): keys = kv[:, :D].reshape(n_sel * tokens_dev, HEADS, HS)]
  transfers between devices with their start and end apart: 6 -> 6, of which waited for: 2 -> 4; matrix products, arithmetic and copies ran while one was open for 12% -> 8% of each run, Pallas kernels for 0% -> 0%
where the time goes in v5:
time: 149 us; the launch traced here: 148 us
  blocking collectives  40.7 us (27%)
  starting transfers between devices  40.6 us (27%)
  local copies, waits for them, and re-layouts  23.4 us (16%)
  other arithmetic  16.3 us (11%)
  matrix products  14.5 us (10%)
  waiting for transfers between devices  8.54 us (6%)
  between operations  4.19 us (3%)
    all_to_all x1, blocking collectives, shards(): lax.all_to_all(partials, ('space', 'tm'), 0, 0, tiled=True)  40.7 us
    ppermute x4, starting transfers between devices, exchange(): return lax.ppermute(x, axis, [(i, i ^ bit) for i in range(length)])  21.9 us
    ppermute x2, starting transfers between devices, shifted(): lax.ppermute(x, axis, [(i, (i + by) % length) for i in range(length)])  18.7 us
    ppermute x4, waiting for transfers between devices, exchange(): return lax.ppermute(x, axis, [(i, i ^ bit) for i in range(length)])  7.82 us
    dot_general x1, matrix products, shards(): jnp.einsum('crk,cl->krl', w_rows, normed_lanes, preferred_element_type=jn...  4.81 us
    unnamed x76, local copies, waits for them, and re-layouts  3.36 us
    dot_general x1, matrix products, shards(): jnp.dot(sel_normed, w_qkv[:, D:], preferred_element_type=jnp.float32)  3.14 us
    slice x2, local copies, waits for them, and re-layouts, shards(): keys = kv[:, :D].reshape(n_sel * tokens_dev, HEADS, HS)  3.09 us
  transfers between devices with their start and end apart: 6, of which 4 were waited for; matrix products, arithmetic and copies ran while one was open for 8% of the time, Pallas kernels for 0%

profile of v5, /device:TPU:1, one launch (start us, length us, event | category | flops | bytes accessed | tf_op | source)
XLA Modules:
  0.0 148.2 jit_solution(12728182599624673797)
XLA Ops:
  1.3 1.4 convert_bitcast_fusion
  4.2 2.2 %reshape.217 = bf16[2,4,8,4,16,4]{5,4,3,2,1,0:T(8,128)(2,1)S(1)} reshape(bf16[2,4,2048]{2,1,0:T(4,128)(2,1)S(1)} %slice_add_fusion) | data formatting | bytes 65536 | tf_op jit(solution)/shard_map/reshape | solution.py:103
  6.5 1.7 %copy.54 = bf16[8,16,2,4,4,4]{1,0,5,4,3,2:T(8,128)(2,1)S(1)} copy(bf16[8,16,2,4,4,4]{5,1,4,0,3,2:T(8,128)(2,1)S(1)} %bitcast.92) | data formatting | bytes 65536 | tf_op jit(solution)/shard_map/transpose | solution.py:104
  8.5 9.6 %collective-permute-start = (bf16[1,129,128]{1,2,0:T(8,128)(2,1)S(1)}, bf16[1,129,128]{1,2,0:T(8,128)(2,1)S(1)}, u32[]{:S(2)}, u32[]{:S(2)}) collective-permute-start(bf16[1,129,128]{1,2,0:T(8,128)(2,1)S(1)} %maximum_bitcast_fusion), channel_id=1, source_target_pairs={{0,8},{1,9},{2,10},{3,11},{4,12},{5,13},{6,14},{7,15},{8,0},{9,1},... | collective-permute-start | bytes 99080 | tf_op jit(solution)/shard_map/ppermute | solution.py:26
  24.1 1.6 %fusion.17 = bf16[128,768]{1,0:T(8,128)(2,1)S(1)} fusion(bf16[768,2304]{1,0:T(8,128)(2,1)} %param.21, f32[128,768]{1,0:T(8,128)S(1)} %get-tuple-element.12, f32[768]{0:T(1024)S(1)} %copy-done.27, f32[128]{0:T(128)S(1)} %add_rsqrt_fusion.2, f32[128]{0:T(128)S(1)} %broadcast_multiply_fusion.2), kind=kOutput, calls=%fused_computation.57 | convolution fusion | flops 151486464 | bytes 1773568 | tf_op jit(solution)/shard_map/dot_general | solution.py:127
  26.3 4.9 %collective-permute-start.1 = (bf16[2,129,128]{1,2,0:T(8,128)(2,1)S(1)}, bf16[2,129,128]{1,2,0:T(8,128)(2,1)S(1)}, u32[]{:S(2)}, u32[]{:S(2)}) collective-permute-start(bf16[2,129,128]{1,2,0:T(8,128)(2,1)S(1)} %pad_maximum_fusion.3), channel_id=1, source_target_pairs={{0,4},{1,5},{2,6},{3,7},{4,0},{5,1},{6,2},{7,3},{8,12},{9,13},{10,... | collective-permute-start | bytes 198152 | tf_op jit(solution)/shard_map/ppermute | solution.py:26
  31.8 5.1 %collective-permute-done.1 = bf16[2,129,128]{1,2,0:T(8,128)(2,1)S(1)} collective-permute-done((bf16[2,129,128]{1,2,0:T(8,128)(2,1)S(1)}, bf16[2,129,128]{1,2,0:T(8,128)(2,1)S(1)}, u32[]{:S(2)}, u32[]{:S(2)}) %collective-permute-start.1) | collective-permute-done | bytes 66080 | tf_op jit(solution)/shard_map/ppermute | solution.py:26
  37.0 3.4 %collective-permute-start.2 = (bf16[4,129,128]{1,2,0:T(8,128)(2,1)S(1)}, bf16[4,129,128]{1,2,0:T(8,128)(2,1)S(1)}, u32[]{:S(2)}, u32[]{:S(2)}) collective-permute-start(bf16[4,129,128]{1,2,0:T(8,128)(2,1)S(1)} %pad_maximum_fusion.2), channel_id=1, source_target_pairs={{0,2},{1,3},{2,0},{3,1},{4,6},{5,7},{6,4},{7,5},{8,10},{9,11},{10,... | collective-permute-start | bytes 396296 | tf_op jit(solution)/shard_map/ppermute | solution.py:26
  44.3 1.3 collective-permute-done.2
  45.6 4.0 %collective-permute-start.3 = (bf16[8,129,128]{1,2,0:T(8,128)(2,1)S(1)}, bf16[8,129,128]{1,2,0:T(8,128)(2,1)S(1)}, u32[]{:S(2)}, u32[]{:S(2)}) collective-permute-start(bf16[8,129,128]{1,2,0:T(8,128)(2,1)S(1)} %pad_maximum_fusion), channel_id=1, source_target_pairs={{0,1},{1,0},{2,3},{3,2},{4,5},{5,4},{6,7},{7,6},{8,9},{9,8},{10,11... | collective-permute-start | bytes 792584 | tf_op jit(solution)/shard_map/ppermute | solution.py:26
  49.7 1.5 collective-permute-done.3
  55.3 3.1 %convolution_convert_fusion = bf16[1024,1536]{1,0:T(8,128)(2,1)S(1)} fusion(bf16[768,2304]{1,0:T(8,128)(2,1)S(1)} %copy-done.26, f32[1024,768]{1,0:T(8,128)S(1)} %get-tuple-element.14, f32[768]{0:T(1024)S(1)} %copy-done.27, f32[1024]{0:T(1024)S(1)} %add_rsqrt_fusion, f32[1024]{0:T(1024)S(1)} %broadcast_multiply_fusion), kind=kOutput, calls=%fused_computation.39 | convolution fusion | flops 2420637696 | bytes 8663040 | tf_op jit(solution)/shard_map/dot_general | solution.py:130
  58.5 1.4 fusion.134
  59.9 1.7 %copy.59 = bf16[1024,768]{0,1:T(8,128)(2,1)S(1)} copy(bf16[1024,768]{1,0:T(8,128)(2,1)} %get-tuple-element.32) | data formatting | bytes 3145728 | tf_op jit(solution)/shard_map/slice | solution.py:133
  61.6 1.7 %copy.57 = bf16[1024,768]{0,1:T(8,128)(2,1)} copy(bf16[1024,768]{1,0:T(8,128)(2,1)S(1)} %get-tuple-element.33) | data formatting | bytes 3145728 | tf_op jit(solution)/shard_map/slice | solution.py:134
  63.2 2.0 %multiply_reduce_fusion = (f32[12,128]{1,0:T(8,128)S(1)}, f32[12,128,1024]{2,1,0:T(8,128)S(1)}) fusion(bf16[128,12,64]{0,2,1:T(8,128)(2,1)} %bitcast.103, bf16[1024,12,64]{0,2,1:T(8,128)(2,1)S(1)} %bitcast.90), kind=kOutput, calls=%fused_computation.35 | convolution fusion | flops 204470784 | bytes 8067072 | tf_op jit(solution)/shard_map/qhd,khd->hqk/dot_general | solution.py:136
  65.3 1.3 fusion
  66.8 1.6 %fusion.20 = f32[128,12,64]{0,2,1:T(8,128)S(1)} fusion(bf16[1024,12,64]{0,2,1:T(8,128)(2,1)S(1)} %bitcast.91, f32[12,128,1024]{2,1,0:T(8,128)S(1)} %get-tuple-element.45, f32[12,128]{1,0:T(8,128)S(1)} %get-tuple-element.44, f32[128,12]{0,1:T(8,128)S(1)} %bitcast.106), kind=kOutput, calls=%fused_computation.59 | convolution fusion | flops 206143488 | bytes 8269824 | tf_op jit(solution)/shard_map/hqk,khd->qhd/dot_general | solution.py:145
  69.0 4.8 %bitcast_add_fusion = f32[16,32,2048]{2,1,0:T(8,128)} fusion(f32[16,32]{1,0:T(8,128)S(1)} %copy-done.20, pred[2048]{0:T(1024)(128)(4,1)S(1)} %copy-done.23, bf16[768,32,16]{0,2,1:T(8,128)(2,1)S(1)} %bitcast.102, s32[128]{0:T(128)S(1)} %copy-done.32, s32[128]{0:T(128)S(1)} %copy-done.33, s32[128]{0:T(128)S(1)} %copy-done.31, s32[128]{0:T(128)S(1)} %copy-done.34, ...), kind=kOutput, calls=%fused_computation.38 | convolution fusion | flops 2018902016 | bytes 5384448 | tf_op jit(solution)/shard_map/crk,cl->krl/dot_general | solution.py:163
  73.8 2.7 %slice_tanh_fusion = (f32[16,16,2048]{2,1,0:T(8,128)S(1)}, f32[16,16,2048]{2,1,0:T(8,128)S(1)}) fusion(f32[16,32,2048]{2,1,0:T(8,128)} %bitcast_add_fusion), kind=kLoop, calls=%fused_computation.50 | loop fusion | bytes 8388608 | tf_op jit(solution)/shard_map/tanh | solution.py:171
  80.8 16.2 %collective-permute-start.5 = (bf16[4,1,2048]{2,1,0:T(2,128)(2,1)S(1)}, bf16[4,1,2048]{2,1,0:T(2,128)(2,1)S(1)}, u32[]{:S(2)}, u32[]{:S(2)}) collective-permute-start(bf16[4,1,2048]{2,1,0:T(2,128)(2,1)S(1)} %slice.421), channel_id=1, source_target_pairs={{0,496},{16,0},{32,16},{48,32},{64,48},{80,64},{96,80},{112,96},{1... | collective-permute-start | bytes 49160 | tf_op jit(solution)/shard_map/ppermute | solution.py:52
  97.0 2.6 %collective-permute-start.4 = (bf16[1,4,2048]{2,1,0:T(4,128)(2,1)S(1)}, bf16[1,4,2048]{2,1,0:T(4,128)(2,1)S(1)}, u32[]{:S(2)}, u32[]{:S(2)}) collective-permute-start(bf16[1,4,2048]{2,1,0:T(4,128)(2,1)S(1)} %slice.419), channel_id=1, source_target_pairs={{0,15},{1,0},{2,1},{3,2},{4,3},{5,4},{6,5},{7,6},{8,7},{9,8},{10,9... | collective-permute-start | bytes 49160 | tf_op jit(solution)/shard_map/ppermute | solution.py:52
  102.1 1.6 %fusion.126 = (f32[]{:T(128)}, f32[4,4,2048]{2,1,0:T(4,128)}, f32[4,4,2048]{2,1,0:T(4,128)}, f32[4,4,2048]{2,1,0:T(4,128)}) fusion(f32[4,4,2048]{2,1,0:T(4,128)S(1)} %get-tuple-element.8, f32[4,4,1]{2,1,0:T(4,128)S(1)} %slice.427, f32[4,4,2047]{2,1,0:T(4,128)S(1)} %slice.426, f32[4,4,1985]{2,1,0:T(4,128)S(1)} %bitcast.89, f32[4,4,63]{2,1,0:T(4,128)S(1)} %slice.424, ...), kind=kLoop, calls=%fused_computation.224 | loop fusion | flops 720895 | bytes 1198084 | tf_op jit(solution)/shard_map/reduce_sum | solution.py:203
  104.5 40.7 %all_to_all.6 = f32[512,1,2]{2,1,0:T(1,128)S(1)} all-to-all(f32[512,1,2]{2,1,0:T(1,128)S(1)} %broadcast_in_dim.107), channel_id=1, replica_groups=mesh['space'=32,'tm'=16] {'space','tm'}, dimensions={0} | all-to-all | bytes 8192 | tf_op jit(solution)/shard_map/all_to_all | solution.py:206
  (183 shorter events, 26.1 us)
Async XLA Ops:
  0.6 20.4 %copy-start = (bf16[256,768]{1,0:T(8,128)(2,1)S(1)}, bf16[256,768]{1,0:T(8,128)(2,1)}, u32[]{:S(2)}) copy-start(bf16[256,768]{1,0:T(8,128)(2,1)} %param.18) | copy-start | bytes 1179652
  0.6 19.0 %copy-start.1 = (s32[16]{0:T(128)S(1)}, s32[16]{0:T(128)}, u32[]{:S(2)}) copy-start(s32[16]{0:T(128)} %constant.187.clone) | copy-start | bytes 196
  0.7 20.3 %copy-start.24 = (s32[128]{0:T(128)S(1)}, s32[128]{0:T(128)}, u32[]{:S(2)}) copy-start(s32[128]{0:T(128)} %constant.192) | copy-start | bytes 1540
  0.7 19.7 %copy-start.25 = (s32[1,1,128]{2,1,0:T(1,128)S(1)}, s32[1,1,128]{2,1,0:T(1,128)}, u32[]{:S(2)}) copy-start(s32[1,1,128]{2,1,0:T(1,128)} %param.16) | copy-start | bytes 1540
  0.7 3.4 %copy-start.11 = (s32[2048]{0:T(1024)}, s32[2048]{0:T(1024)S(1)}, u32[]{:S(2)}) copy-start(s32[2048]{0:T(1024)S(1)} %get-tuple-element.46) | copy-start | bytes 24580
  0.7 3.4 %copy-start.13 = (s32[2048]{0:T(1024)}, s32[2048]{0:T(1024)S(1)}, u32[]{:S(2)}) copy-start(s32[2048]{0:T(1024)S(1)} %get-tuple-element.49) | copy-start | bytes 24580
  0.7 3.4 %copy-start.15 = (pred[2048]{0:T(1024)(128)(4,1)}, pred[2048]{0:T(1024)(128)(4,1)S(1)}, u32[]{:S(2)}) copy-start(pred[2048]{0:T(1024)(128)(4,1)S(1)} %get-tuple-element.50) | copy-start | bytes 6148
  0.8 3.4 %copy-start.17 = (pred[2048]{0:T(1024)(128)(4,1)}, pred[2048]{0:T(1024)(128)(4,1)S(1)}, u32[]{:S(2)}) copy-start(pred[2048]{0:T(1024)(128)(4,1)S(1)} %get-tuple-element.51) | copy-start | bytes 6148
  6.4 16.6 %copy-start.19 = (f32[768]{0:T(1024)S(1)}, f32[768]{0:T(1024)}, u32[]{:S(2)}) copy-start(f32[768]{0:T(1024)} %param.19) | copy-start | bytes 9220
  8.1 15.9 %copy-start.27 = (f32[768]{0:T(1024)S(1)}, f32[768]{0:T(1024)}, u32[]{:S(2)}) copy-start(f32[768]{0:T(1024)} %param.20) | copy-start | bytes 9220
  8.5 17.8 %collective-permute-start = (bf16[1,129,128]{1,2,0:T(8,128)(2,1)S(1)}, bf16[1,129,128]{1,2,0:T(8,128)(2,1)S(1)}, u32[]{:S(2)}, u32[]{:S(2)}) collective-permute-start(bf16[1,129,128]{1,2,0:T(8,128)(2,1)S(1)} %maximum_bitcast_fusion), channel_id=1, source_target_pairs={{0,8},{1,9},{2,10},{3,11},{4,12},{5,13},{6,14},{7,15},{8,0},{9,1},... | collective-permute-start | bytes 99080 | tf_op jit(solution)/shard_map/ppermute | solution.py:26
  21.9 19.9 %copy-start.6 = (bf16[768,512]{1,0:T(8,128)(2,1)S(1)}, bf16[768,512]{1,0:T(8,128)(2,1)}, u32[]{:S(2)}) copy-start(bf16[768,512]{1,0:T(8,128)(2,1)} %param.23) | copy-start | bytes 2359300
  22.7 20.2 %copy-start.22 = (f32[512]{0:T(512)S(1)}, f32[512]{0:T(512)}, u32[]{:S(2)}) copy-start(f32[512]{0:T(512)} %param.24) | copy-start | bytes 6148
  26.3 10.6 %collective-permute-start.1 = (bf16[2,129,128]{1,2,0:T(8,128)(2,1)S(1)}, bf16[2,129,128]{1,2,0:T(8,128)(2,1)S(1)}, u32[]{:S(2)}, u32[]{:S(2)}) collective-permute-start(bf16[2,129,128]{1,2,0:T(8,128)(2,1)S(1)} %pad_maximum_fusion.3), channel_id=1, source_target_pairs={{0,4},{1,5},{2,6},{3,7},{4,0},{5,1},{6,2},{7,3},{8,12},{9,13},{10,... | collective-permute-start | bytes 198152 | tf_op jit(solution)/shard_map/ppermute | solution.py:26
  37.0 8.6 %collective-permute-start.2 = (bf16[4,129,128]{1,2,0:T(8,128)(2,1)S(1)}, bf16[4,129,128]{1,2,0:T(8,128)(2,1)S(1)}, u32[]{:S(2)}, u32[]{:S(2)}) collective-permute-start(bf16[4,129,128]{1,2,0:T(8,128)(2,1)S(1)} %pad_maximum_fusion.2), channel_id=1, source_target_pairs={{0,2},{1,3},{2,0},{3,1},{4,6},{5,7},{6,4},{7,5},{8,10},{9,11},{10,... | collective-permute-start | bytes 396296 | tf_op jit(solution)/shard_map/ppermute | solution.py:26
  45.6 5.5 %collective-permute-start.3 = (bf16[8,129,128]{1,2,0:T(8,128)(2,1)S(1)}, bf16[8,129,128]{1,2,0:T(8,128)(2,1)S(1)}, u32[]{:S(2)}, u32[]{:S(2)}) collective-permute-start(bf16[8,129,128]{1,2,0:T(8,128)(2,1)S(1)} %pad_maximum_fusion), channel_id=1, source_target_pairs={{0,1},{1,0},{2,3},{3,2},{4,5},{5,4},{6,7},{7,6},{8,9},{9,8},{10,11... | collective-permute-start | bytes 792584 | tf_op jit(solution)/shard_map/ppermute | solution.py:26
  66.7 2.2 %copy-start.28 = (f32[768]{0:T(1024)S(1)}, f32[768]{0:T(1024)}, u32[]{:S(2)}) copy-start(f32[768]{0:T(1024)} %param.22) | copy-start | bytes 9220
  66.7 2.2 %copy-start.29 = (pred[128]{0:T(512)(128)(4,1)S(1)}, pred[128]{0:T(512)(128)(4,1)}, u32[]{:S(2)}) copy-start(pred[128]{0:T(512)(128)(4,1)} %get-tuple-element.54) | copy-start | bytes 388
  66.7 2.2 %copy-start.30 = (pred[128]{0:T(512)(128)(4,1)S(1)}, pred[128]{0:T(512)(128)(4,1)}, u32[]{:S(2)}) copy-start(pred[128]{0:T(512)(128)(4,1)} %get-tuple-element.55) | copy-start | bytes 388
  66.7 2.2 %copy-start.31 = (s32[128]{0:T(128)S(1)}, s32[128]{0:T(128)}, u32[]{:S(2)}) copy-start(s32[128]{0:T(128)} %get-tuple-element.56) | copy-start | bytes 1540
  66.7 2.2 %copy-start.32 = (s32[128]{0:T(128)S(1)}, s32[128]{0:T(128)}, u32[]{:S(2)}) copy-start(s32[128]{0:T(128)} %get-tuple-element.57) | copy-start | bytes 1540
  80.8 67.4 %copy-start.2 = (f32[4,4,2048]{2,1,0:T(4,128)}, f32[4,4,2048]{2,1,0:T(4,128)S(1)}, u32[]{:S(2)}) copy-start(f32[4,4,2048]{2,1,0:T(4,128)S(1)} %get-tuple-element.8) | copy-start | bytes 393220
  80.8 20.5 %collective-permute-start.5 = (bf16[4,1,2048]{2,1,0:T(2,128)(2,1)S(1)}, bf16[4,1,2048]{2,1,0:T(2,128)(2,1)S(1)}, u32[]{:S(2)}, u32[]{:S(2)}) collective-permute-start(bf16[4,1,2048]{2,1,0:T(2,128)(2,1)S(1)} %slice.421), channel_id=1, source_target_pairs={{0,496},{16,0},{32,16},{48,32},{64,48},{80,64},{96,80},{112,96},{1... | collective-permute-start | bytes 49160 | tf_op jit(solution)/shard_map/ppermute | solution.py:52
  97.0 5.1 %collective-permute-start.4 = (bf16[1,4,2048]{2,1,0:T(4,128)(2,1)S(1)}, bf16[1,4,2048]{2,1,0:T(4,128)(2,1)S(1)}, u32[]{:S(2)}, u32[]{:S(2)}) collective-permute-start(bf16[1,4,2048]{2,1,0:T(4,128)(2,1)S(1)} %slice.419), channel_id=1, source_target_pairs={{0,15},{1,0},{2,1},{3,2},{4,3},{5,4},{6,5},{7,6},{8,7},{9,8},{10,9... | collective-permute-start | bytes 49160 | tf_op jit(solution)/shard_map/ppermute | solution.py:52
  (17 other events, 26.8 us)

commit v6 on v5

--- a/solution.py
+++ b/solution.py
@@ -99,11 +99,22 @@
     frozen_in = jnp.where(frozen, u, 0.0).astype(jnp.bfloat16)
 
     packed = frozen_in[0::2] + frozen_in[1::2]
-    tokens = (
-        packed.reshape(2, P_SIZE, n_y, P_SIZE, n_z, P_SIZE)
-        .transpose(2, 4, 0, 1, 3, 5)
-        .reshape(tokens_dev, patch_len // 2)
-    )
+    n_off = P_SIZE * P_SIZE
+    tok_ids = lax.broadcasted_iota(jnp.int32, (tokens_dev, LY * LZ), 0)
+    lane_ids = lax.broadcasted_iota(jnp.int32, (tokens_dev, LY * LZ), 1)
+    tok_lane = tok_ids // n_z * (P_SIZE * LZ) + tok_ids % n_z * P_SIZE
+    spread_tok = (lane_ids == tok_lane).astype(jnp.bfloat16)
+    packed_rows_lat = packed.reshape(2 * P_SIZE, LY * LZ)
+    shifted_rows = jnp.stack(
+        [
+            jnp.roll(packed_rows_lat, -(k // P_SIZE * LZ + k % P_SIZE), axis=-1)
+            for k in range(n_off)
+        ],
+        axis=1,
+    ).reshape(2 * P_SIZE * n_off, LY * LZ)
+    tokens = jnp.einsum(
+        "fl,tl->tf", shifted_rows, spread_tok, preferred_element_type=jnp.float32
+    ).astype(jnp.bfloat16)
     bits_f = bits.reshape(1, tokens_dev).astype(jnp.bfloat16)
     send = jnp.concatenate([tokens, bits_f], axis=0)
     gathered, offsets = doubling_gather(send[None], "tm")
@@ -151,14 +162,9 @@
     mixed = (product / row_total.T[:, :, None]).reshape(tokens_dev, D)
     hidden = embedded + mixed
     normed_out = layer_norm(hidden, gain_out).astype(jnp.bfloat16)
-    tok_ids = lax.broadcasted_iota(jnp.int32, (tokens_dev, LY * LZ), 0)
-    lane_ids = lax.broadcasted_iota(jnp.int32, (tokens_dev, LY * LZ), 1)
-    tok_lane = tok_ids // n_z * (P_SIZE * LZ) + tok_ids % n_z * P_SIZE
-    spread_tok = (lane_ids == tok_lane).astype(jnp.bfloat16)
     normed_lanes = jnp.einsum(
         "tc,tl->cl", normed_out, spread_tok, preferred_element_type=jnp.float32
     ).astype(jnp.bfloat16)
-    n_off = P_SIZE * P_SIZE
     w_rows = w_head.reshape(D, 2 * P_SIZE * P_SIZE, n_off)
     affine_lanes = jnp.einsum(
         "crk,cl->krl", w_rows, normed_lanes, preferred_element_type=jnp.float32
@@ -166,17 +172,13 @@
     base_lane = (lane[0, 0] % P_SIZE == 0) & (lane[0, 0] // LZ % P_SIZE == 0)
     bias_rows = b_head.reshape(2 * P_SIZE * P_SIZE, n_off).T
     affine_lanes = affine_lanes + jnp.where(base_lane[None, None, :], bias_rows[:, :, None], 0.0)
-    half_rows = P_SIZE * P_SIZE
-    coupling_rows = jnp.concatenate(
-        [jnp.tanh(affine_lanes[:, :half_rows]), affine_lanes[:, half_rows:]], axis=1
-    )
-    coupling_lat = coupling_rows[0]
+    coupling_lat = affine_lanes[0]
     for k in range(1, n_off):
         offset = k // P_SIZE * LZ + k % P_SIZE
-        coupling_lat = coupling_lat + jnp.roll(coupling_rows[k], offset, axis=-1)
-    coupling_lat = coupling_lat.reshape(2, P_SIZE, P_SIZE, LY * LZ)
-    scale_lat = coupling_lat[0]
-    shift_lat = coupling_lat[1]
+        coupling_lat = coupling_lat + jnp.roll(affine_lanes[k], offset, axis=-1)
+    half_rows = P_SIZE * P_SIZE
+    scale_lat = jnp.tanh(coupling_lat[:half_rows]).reshape(P_SIZE, P_SIZE, LY * LZ)
+    shift_lat = coupling_lat[half_rows:].reshape(P_SIZE, P_SIZE, LY * LZ)
     log_det = jnp.sum(jnp.where(frozen, 0.0, scale_lat))
     new_field = jnp.where(frozen, u, u * jnp.exp(scale_lat) + shift_lat)
 

time: 149 us -> 139 us (0.933)
  waiting for transfers between devices: 8.54 us -> 2.93 us
  local copies, waits for them, and re-layouts: 23.4 us -> 20.4 us
  other arithmetic: 16.3 us -> 14.8 us
    ppermute x4, waiting for transfers between devices: 7.82 us -> 2.2 us  [exchange(): return lax.ppermute(x, axis, [(i, i ^ bit) for i in range(length)])]
    tanh x1 -> x0, local copies, waits for them, and re-layouts: 2.68 us -> none  [shards(): jnp.tanh(affine_lanes[:, :half_rows])]
    squeeze x1, local copies, waits for them, and re-layouts: 0.04 us -> 2.5 us  [shards(): coupling_lat = coupling_lat + jnp.roll(affine_lanes[k], offset, axis=-1)]
    reshape x2, local copies, waits for them, and re-layouts: 2.42 us -> 0.05 us  [the longest x1 0.04 us: shards(): shift_lat = coupling_lat[half_rows:].reshape(P_SIZE, P_SIZE, LY * LZ)]
    transpose x1 -> x0, local copies, waits for them, and re-layouts: 1.65 us -> none  [shards(): tokens = packed.reshape(2, P_SIZE, n_y, P_SIZE, n_z, P_SIZE).transpose(2,...]
    ppermute x4, starting transfers between devices: 21.9 us -> 23.5 us  [exchange(): return lax.ppermute(x, axis, [(i, i ^ bit) for i in range(length)])]
    ppermute x2, starting transfers between devices: 18.7 us -> 17.2 us  [shifted(): lax.ppermute(x, axis, [(i, (i + by) % length) for i in range(length)])]
    unnamed x76 -> x93, local copies, waits for them, and re-layouts: 3.36 us -> 3.41 us
  transfers between devices with their start and end apart: 6 -> 6, of which waited for: 4 -> 3; matrix products, arithmetic and copies ran while one was open for 8% -> 7% of each run, Pallas kernels for 0% -> 0%
where the time goes in v6:
time: 139 us
  starting transfers between devices  40.7 us (29%)
  blocking collectives  40.6 us (29%)
  local copies, waits for them, and re-layouts  20.4 us (15%)
  other arithmetic  14.8 us (11%)
  matrix products  14.8 us (11%)
  between operations  4.41 us (3%)
  waiting for transfers between devices  2.93 us (2%)
    all_to_all x1, blocking collectives, shards(): lax.all_to_all(partials, ('space', 'tm'), 0, 0, tiled=True)  40.6 us
    ppermute x4, starting transfers between devices, exchange(): return lax.ppermute(x, axis, [(i, i ^ bit) for i in range(length)])  23.5 us
    ppermute x2, starting transfers between devices, shifted(): lax.ppermute(x, axis, [(i, (i + by) % length) for i in range(length)])  17.2 us
    dot_general x1, matrix products, shards(): jnp.einsum('crk,cl->krl', w_rows, normed_lanes, preferred_element_type=jn...  4.78 us
    unnamed x93, local copies, waits for them, and re-layouts  3.41 us
    dot_general x1, matrix products, shards(): jnp.dot(sel_normed, w_qkv[:, D:], preferred_element_type=jnp.float32)  3.14 us
    slice x2, local copies, waits for them, and re-layouts, shards(): keys = kv[:, :D].reshape(n_sel * tokens_dev, HEADS, HS)  3.08 us
  transfers between devices with their start and end apart: 6, of which 3 were waited for; matrix products, arithmetic and copies ran while one was open for 7% of the time, Pallas kernels for 0%

profile of v6, /device:TPU:1, one launch (start us, length us, event | category | flops | bytes accessed | tf_op | source)
XLA Modules:
  0.0 138.6 jit_solution(13705403012380000671)
XLA Ops:
  1.2 1.4 %convert_bitcast_fusion = (bf16[1,128]{1,0:T(2,128)(2,1)S(1)}, s32[128]{0:T(128)S(1)}) fusion(s32[1,1,128]{2,1,0:T(1,128)} %param.16, s32[]{:T(128)} %broadcast.401), kind=kLoop, calls=%fused_computation.195 | loop fusion | flops 128 | bytes 1284 | tf_op jit(solution)/shard_map/convert_element_type | solution.py:118
  3.1 1.1 select_convert_fusion
  7.4 9.6 %collective-permute-start = (bf16[1,129,128]{2,1,0:T(8,128)(2,1)S(1)}, bf16[1,129,128]{2,1,0:T(8,128)(2,1)S(1)}, u32[]{:S(2)}, u32[]{:S(2)}) collective-permute-start(bf16[1,129,128]{2,1,0:T(8,128)(2,1)S(1)} %maximum_bitcast_fusion), channel_id=1, source_target_pairs={{0,8},{1,9},{2,10},{3,11},{4,12},{5,13},{6,14},{7,15},{8,0},{9,1},... | collective-permute-start | bytes 99080 | tf_op jit(solution)/shard_map/ppermute | solution.py:26
  21.1 1.6 %fusion.17 = bf16[128,768]{1,0:T(8,128)(2,1)S(1)} fusion(bf16[768,2304]{1,0:T(8,128)(2,1)} %param.21, f32[128,768]{1,0:T(8,128)S(1)} %get-tuple-element.12, f32[768]{0:T(1024)S(1)} %copy-done.29, f32[128]{0:T(128)S(1)} %add_rsqrt_fusion.2, f32[128]{0:T(128)S(1)} %broadcast_multiply_fusion.2), kind=kOutput, calls=%fused_computation.26 | convolution fusion | flops 151486464 | bytes 1773568 | tf_op jit(solution)/shard_map/dot_general | solution.py:138
  22.8 4.9 %collective-permute-start.1 = (bf16[2,129,128]{2,1,0:T(8,128)(2,1)S(1)}, bf16[2,129,128]{2,1,0:T(8,128)(2,1)S(1)}, u32[]{:S(2)}, u32[]{:S(2)}) collective-permute-start(bf16[2,129,128]{2,1,0:T(8,128)(2,1)S(1)} %pad_maximum_fusion.4), channel_id=1, source_target_pairs={{0,4},{1,5},{2,6},{3,7},{4,0},{5,1},{6,2},{7,3},{8,12},{9,13},{10,... | collective-permute-start | bytes 198152 | tf_op jit(solution)/shard_map/ppermute | solution.py:26
  28.3 1.1 collective-permute-done.1
  29.4 3.6 %collective-permute-start.2 = (bf16[4,129,128]{2,1,0:T(8,128)(2,1)S(1)}, bf16[4,129,128]{2,1,0:T(8,128)(2,1)S(1)}, u32[]{:S(2)}, u32[]{:S(2)}) collective-permute-start(bf16[4,129,128]{2,1,0:T(8,128)(2,1)S(1)} %pad_maximum_fusion.1), channel_id=1, source_target_pairs={{0,2},{1,3},{2,0},{3,1},{4,6},{5,7},{6,4},{7,5},{8,10},{9,11},{10,... | collective-permute-start | bytes 396296 | tf_op jit(solution)/shard_map/ppermute | solution.py:26
  33.9 1.2 copy.67
  36.5 5.3 %collective-permute-start.3 = (bf16[8,129,128]{2,1,0:T(8,128)(2,1)S(1)}, bf16[8,129,128]{2,1,0:T(8,128)(2,1)S(1)}, u32[]{:S(2)}, u32[]{:S(2)}) collective-permute-start(bf16[8,129,128]{2,1,0:T(8,128)(2,1)S(1)} %pad_maximum_fusion), channel_id=1, source_target_pairs={{0,1},{1,0},{2,3},{3,2},{4,5},{5,4},{6,7},{7,6},{8,9},{9,8},{10,11... | collective-permute-start | bytes 792584 | tf_op jit(solution)/shard_map/ppermute | solution.py:26
  41.9 1.1 collective-permute-done.3
  46.8 3.1 %convolution_convert_fusion = bf16[1024,1536]{1,0:T(8,128)(2,1)S(1)} fusion(bf16[768,2304]{1,0:T(8,128)(2,1)S(1)} %copy-done.28, f32[1024,768]{1,0:T(8,128)S(1)} %get-tuple-element.14, f32[768]{0:T(1024)S(1)} %copy-done.29, f32[1024]{0:T(1024)S(1)} %add_rsqrt_fusion, f32[1024]{0:T(1024)S(1)} %broadcast_multiply_fusion), kind=kOutput, calls=%fused_computation.9 | convolution fusion | flops 2420637696 | bytes 8663040 | tf_op jit(solution)/shard_map/dot_general | solution.py:141
  49.9 1.4 fusion.85
  51.3 1.7 %copy.65 = bf16[1024,768]{0,1:T(8,128)(2,1)S(1)} copy(bf16[1024,768]{1,0:T(8,128)(2,1)} %get-tuple-element.30) | data formatting | bytes 3145728 | tf_op jit(solution)/shard_map/slice | solution.py:144
  53.0 1.7 %copy.63 = bf16[1024,768]{0,1:T(8,128)(2,1)} copy(bf16[1024,768]{1,0:T(8,128)(2,1)S(1)} %get-tuple-element.31) | data formatting | bytes 3145728 | tf_op jit(solution)/shard_map/slice | solution.py:145
  54.7 2.0 %multiply_reduce_fusion = (f32[12,128]{1,0:T(8,128)S(1)}, f32[12,128,1024]{2,1,0:T(8,128)S(1)}) fusion(bf16[128,12,64]{0,2,1:T(8,128)(2,1)} %bitcast.189, bf16[1024,12,64]{0,2,1:T(8,128)(2,1)S(1)} %bitcast.177), kind=kOutput, calls=%fused_computation.5 | convolution fusion | flops 204470784 | bytes 8067072 | tf_op jit(solution)/shard_map/qhd,khd->hqk/dot_general | solution.py:147
  56.7 1.3 fusion
  58.2 1.6 %fusion.20 = f32[128,12,64]{0,2,1:T(8,128)S(1)} fusion(bf16[1024,12,64]{0,2,1:T(8,128)(2,1)S(1)} %bitcast.178, f32[12,128,1024]{2,1,0:T(8,128)S(1)} %get-tuple-element.43, f32[12,128]{1,0:T(8,128)S(1)} %get-tuple-element.42, f32[128,12]{0,1:T(8,128)S(1)} %bitcast.193), kind=kOutput, calls=%fused_computation.29 | convolution fusion | flops 206143488 | bytes 8269824 | tf_op jit(solution)/shard_map/hqk,khd->qhd/dot_general | solution.py:156
  60.4 4.8 %bitcast_add_fusion = f32[16,32,2048]{2,1,0:T(8,128)} fusion(f32[16,32]{1,0:T(8,128)S(1)} %copy-done.20, pred[2048]{0:T(1024)(128)(4,1)S(1)} %copy-done.24, bf16[768,32,16]{0,2,1:T(8,128)(2,1)S(1)} %bitcast.188, f32[128,768]{1,0:T(8,128)S(1)} %get-tuple-element.10, f32[768]{0:T(1024)S(1)} %copy-done.30, f32[128]{0:T(128)S(1)} %add_rsqrt_fusion.1, ...), kind=kOutput, calls=%fused_computation.8 | convolution fusion | flops 2018902016 | bytes 5384448 | tf_op jit(solution)/shard_map/crk,cl->krl/dot_general | solution.py:169
  65.2 2.5 %slice_bitcast_fusion = (f32[32,2048]{1,0:T(8,128)S(1)}, f32[32,2048]{1,0:T(8,128)S(1)}, f32[32,2048]{1,0:T(8,128)S(1)}, f32[32,2048]{1,0:T(8,128)S(1)}, f32[32,...) fusion(f32[16,32,2048]{2,1,0:T(8,128)} %bitcast_add_fusion), kind=kLoop, calls=%fused_computation.39 | loop fusion | bytes 7864320 | tf_op jit(solution)/shard_map/squeeze | solution.py:178
  69.0 2.0 %fusion.39 = f32[32,2048]{1,0:T(8,128)S(1)} fusion(f32[16,32,2048]{2,1,0:T(8,128)} %bitcast_add_fusion, f32[32,2047]{1,0:T(8,128)S(1)} %bitcast.187, f32[32,1]{1,0:T(8,128)S(1)} %slice.526, f32[32,2046]{1,0:T(8,128)S(1)} %bitcast.186, f32[32,2]{1,0:T(8,128)S(1)} %slice.529, f32[32,2045]{1,0:T(8,128)S(1)} %bitcast.185, f32[32,3]{1,0:T(8,128)S(1)} %slice.532, ...), kind=kLoop, calls=%fused_computation.69 | loop fusion | flops 1966080 | bytes 4456448 | tf_op jit(solution)/shard_map/add | solution.py:178
  72.7 14.7 %collective-permute-start.5 = (bf16[4,1,2048]{2,1,0:T(2,128)(2,1)S(1)}, bf16[4,1,2048]{2,1,0:T(2,128)(2,1)S(1)}, u32[]{:S(2)}, u32[]{:S(2)}) collective-permute-start(bf16[4,1,2048]{2,1,0:T(2,128)(2,1)S(1)} %slice.575), channel_id=1, source_target_pairs={{0,496},{16,0},{32,16},{48,32},{64,48},{80,64},{96,80},{112,96},{1... | collective-permute-start | bytes 49160 | tf_op jit(solution)/shard_map/ppermute | solution.py:52
  87.4 2.6 %collective-permute-start.4 = (bf16[1,4,2048]{2,1,0:T(4,128)(2,1)S(1)}, bf16[1,4,2048]{2,1,0:T(4,128)(2,1)S(1)}, u32[]{:S(2)}, u32[]{:S(2)}) collective-permute-start(bf16[1,4,2048]{2,1,0:T(4,128)(2,1)S(1)} %slice.573), channel_id=1, source_target_pairs={{0,15},{1,0},{2,1},{3,2},{4,3},{5,4},{6,5},{7,6},{8,7},{9,8},{10,9... | collective-permute-start | bytes 49160 | tf_op jit(solution)/shard_map/ppermute | solution.py:52
  92.5 1.6 %fusion.77 = (f32[]{:T(128)}, f32[4,4,2048]{2,1,0:T(4,128)}, f32[4,4,2048]{2,1,0:T(4,128)}, f32[4,4,2048]{2,1,0:T(4,128)}) fusion(f32[4,4,2048]{2,1,0:T(4,128)S(1)} %get-tuple-element.8, f32[4,4,1]{2,1,0:T(4,128)S(1)} %slice.581, f32[4,4,2047]{2,1,0:T(4,128)S(1)} %slice.580, f32[4,4,1985]{2,1,0:T(4,128)S(1)} %bitcast.176, f32[4,4,63]{2,1,0:T(4,128)S(1)} %slice.578, ...), kind=kLoop, calls=%fused_computation.201 | loop fusion | flops 720895 | bytes 1198084 | tf_op jit(solution)/shard_map/reduce_sum | solution.py:205
  94.9 40.6 %all_to_all.6 = f32[512,1,2]{2,1,0:T(1,128)S(1)} all-to-all(f32[512,1,2]{2,1,0:T(1,128)S(1)} %broadcast_in_dim.107), channel_id=1, replica_groups=mesh['space'=32,'tm'=16] {'space','tm'}, dimensions={0} | all-to-all | bytes 8192 | tf_op jit(solution)/shard_map/all_to_all | solution.py:208
  (242 shorter events, 21.8 us)
Async XLA Ops:
  0.6 17.4 %copy-start = (bf16[256,768]{1,0:T(8,128)(2,1)S(1)}, bf16[256,768]{1,0:T(8,128)(2,1)}, u32[]{:S(2)}) copy-start(bf16[256,768]{1,0:T(8,128)(2,1)} %param.18) | copy-start | bytes 1179652
  0.7 6.7 %copy-start.11 = (s32[2048]{0:T(1024)}, s32[2048]{0:T(1024)S(1)}, u32[]{:S(2)}) copy-start(s32[2048]{0:T(1024)S(1)} %get-tuple-element.44) | copy-start | bytes 24580
  0.7 6.7 %copy-start.13 = (s32[2048]{0:T(1024)}, s32[2048]{0:T(1024)S(1)}, u32[]{:S(2)}) copy-start(s32[2048]{0:T(1024)S(1)} %get-tuple-element.47) | copy-start | bytes 24580
  3.0 14.0 %copy-start.27 = (s32[1,1,128]{2,1,0:T(1,128)S(1)}, s32[1,1,128]{2,1,0:T(1,128)}, u32[]{:S(2)}) copy-start(s32[1,1,128]{2,1,0:T(1,128)} %param.16) | copy-start | bytes 1540
  3.0 14.0 %copy-start.21 = (s32[16,8]{0,1:T(8,128)S(1)}, s32[16,8]{0,1:T(8,128)}, u32[]{:S(2)}) copy-start(s32[16,8]{0,1:T(8,128)} %param.17) | copy-start | bytes 1540
  3.1 14.2 %copy-start.26 = (s32[128]{0:T(128)S(1)}, s32[128]{0:T(128)}, u32[]{:S(2)}) copy-start(s32[128]{0:T(128)} %constant.193) | copy-start | bytes 1540
  3.1 14.2 %copy-start.1 = (s32[16]{0:T(128)S(1)}, s32[16]{0:T(128)}, u32[]{:S(2)}) copy-start(s32[16]{0:T(128)} %constant.187.clone) | copy-start | bytes 196
  4.3 13.6 %copy-start.25 = (s32[128]{0:T(128)S(1)}, s32[128]{0:T(128)}, u32[]{:S(2)}) copy-start(s32[128]{0:T(128)} %constant.192) | copy-start | bytes 1540
  5.5 13.4 %copy-start.31 = (pred[128]{0:T(512)(128)(4,1)}, pred[128]{0:T(512)(128)(4,1)S(1)}, u32[]{:S(2)}) copy-start(pred[128]{0:T(512)(128)(4,1)S(1)} %get-tuple-element.50) | copy-start | bytes 388
  5.5 13.4 %copy-start.33 = (pred[128]{0:T(512)(128)(4,1)}, pred[128]{0:T(512)(128)(4,1)S(1)}, u32[]{:S(2)}) copy-start(pred[128]{0:T(512)(128)(4,1)S(1)} %get-tuple-element.51) | copy-start | bytes 388
  5.5 13.4 %copy-start.35 = (s32[128]{0:T(128)}, s32[128]{0:T(128)S(1)}, u32[]{:S(2)}) copy-start(s32[128]{0:T(128)S(1)} %get-tuple-element.52) | copy-start | bytes 1540
  5.5 13.4 %copy-start.37 = (s32[128]{0:T(128)}, s32[128]{0:T(128)S(1)}, u32[]{:S(2)}) copy-start(s32[128]{0:T(128)S(1)} %get-tuple-element.53) | copy-start | bytes 1540
  5.5 13.4 %copy-start.39 = (s32[128]{0:T(128)}, s32[128]{0:T(128)S(1)}, u32[]{:S(2)}) copy-start(s32[128]{0:T(128)S(1)} %get-tuple-element.54) | copy-start | bytes 1540
  5.5 13.4 %copy-start.41 = (s32[128]{0:T(128)}, s32[128]{0:T(128)S(1)}, u32[]{:S(2)}) copy-start(s32[128]{0:T(128)S(1)} %get-tuple-element.55) | copy-start | bytes 1540
  7.3 12.8 %copy-start.19 = (f32[768]{0:T(1024)S(1)}, f32[768]{0:T(1024)}, u32[]{:S(2)}) copy-start(f32[768]{0:T(1024)} %param.19) | copy-start | bytes 9220
  7.4 15.4 %collective-permute-start = (bf16[1,129,128]{2,1,0:T(8,128)(2,1)S(1)}, bf16[1,129,128]{2,1,0:T(8,128)(2,1)S(1)}, u32[]{:S(2)}, u32[]{:S(2)}) collective-permute-start(bf16[1,129,128]{2,1,0:T(8,128)(2,1)S(1)} %maximum_bitcast_fusion), channel_id=1, source_target_pairs={{0,8},{1,9},{2,10},{3,11},{4,12},{5,13},{6,14},{7,15},{8,0},{9,1},... | collective-permute-start | bytes 99080 | tf_op jit(solution)/shard_map/ppermute | solution.py:26
  19.8 14.1 %copy-start.6 = (bf16[768,512]{1,0:T(8,128)(2,1)S(1)}, bf16[768,512]{1,0:T(8,128)(2,1)}, u32[]{:S(2)}) copy-start(bf16[768,512]{1,0:T(8,128)(2,1)} %param.23) | copy-start | bytes 2359300
  20.1 14.9 %copy-start.23 = (f32[512]{0:T(512)S(1)}, f32[512]{0:T(512)}, u32[]{:S(2)}) copy-start(f32[512]{0:T(512)} %param.24) | copy-start | bytes 6148
  22.8 6.6 %collective-permute-start.1 = (bf16[2,129,128]{2,1,0:T(8,128)(2,1)S(1)}, bf16[2,129,128]{2,1,0:T(8,128)(2,1)S(1)}, u32[]{:S(2)}, u32[]{:S(2)}) collective-permute-start(bf16[2,129,128]{2,1,0:T(8,128)(2,1)S(1)} %pad_maximum_fusion.4), channel_id=1, source_target_pairs={{0,4},{1,5},{2,6},{3,7},{4,0},{5,1},{6,2},{7,3},{8,12},{9,13},{10,... | collective-permute-start | bytes 198152 | tf_op jit(solution)/shard_map/ppermute | solution.py:26
  29.4 7.1 %collective-permute-start.2 = (bf16[4,129,128]{2,1,0:T(8,128)(2,1)S(1)}, bf16[4,129,128]{2,1,0:T(8,128)(2,1)S(1)}, u32[]{:S(2)}, u32[]{:S(2)}) collective-permute-start(bf16[4,129,128]{2,1,0:T(8,128)(2,1)S(1)} %pad_maximum_fusion.1), channel_id=1, source_target_pairs={{0,2},{1,3},{2,0},{3,1},{4,6},{5,7},{6,4},{7,5},{8,10},{9,11},{10,... | collective-permute-start | bytes 396296 | tf_op jit(solution)/shard_map/ppermute | solution.py:26
  36.5 6.5 %collective-permute-start.3 = (bf16[8,129,128]{2,1,0:T(8,128)(2,1)S(1)}, bf16[8,129,128]{2,1,0:T(8,128)(2,1)S(1)}, u32[]{:S(2)}, u32[]{:S(2)}) collective-permute-start(bf16[8,129,128]{2,1,0:T(8,128)(2,1)S(1)} %pad_maximum_fusion), channel_id=1, source_target_pairs={{0,1},{1,0},{2,3},{3,2},{4,5},{5,4},{6,7},{7,6},{8,9},{9,8},{10,11... | collective-permute-start | bytes 792584 | tf_op jit(solution)/shard_map/ppermute | solution.py:26
  72.7 65.9 %copy-start.2 = (f32[4,4,2048]{2,1,0:T(4,128)}, f32[4,4,2048]{2,1,0:T(4,128)S(1)}, u32[]{:S(2)}) copy-start(f32[4,4,2048]{2,1,0:T(4,128)S(1)} %get-tuple-element.8) | copy-start | bytes 393220
  72.7 19.0 %collective-permute-start.5 = (bf16[4,1,2048]{2,1,0:T(2,128)(2,1)S(1)}, bf16[4,1,2048]{2,1,0:T(2,128)(2,1)S(1)}, u32[]{:S(2)}, u32[]{:S(2)}) collective-permute-start(bf16[4,1,2048]{2,1,0:T(2,128)(2,1)S(1)} %slice.575), channel_id=1, source_target_pairs={{0,496},{16,0},{32,16},{48,32},{64,48},{80,64},{96,80},{112,96},{1... | collective-permute-start | bytes 49160 | tf_op jit(solution)/shard_map/ppermute | solution.py:52
  87.4 5.1 %collective-permute-start.4 = (bf16[1,4,2048]{2,1,0:T(4,128)(2,1)S(1)}, bf16[1,4,2048]{2,1,0:T(4,128)(2,1)S(1)}, u32[]{:S(2)}, u32[]{:S(2)}) collective-permute-start(bf16[1,4,2048]{2,1,0:T(4,128)(2,1)S(1)} %slice.573), channel_id=1, source_target_pairs={{0,15},{1,0},{2,1},{3,2},{4,3},{5,4},{6,5},{7,6},{8,7},{9,8},{10,9... | collective-permute-start | bytes 49160 | tf_op jit(solution)/shard_map/ppermute | solution.py:52
  (25 other events, 62.8 us)

commit v7 on v6

--- a/solution.py
+++ b/solution.py
@@ -162,16 +162,19 @@
     mixed = (product / row_total.T[:, :, None]).reshape(tokens_dev, D)
     hidden = embedded + mixed
     normed_out = layer_norm(hidden, gain_out).astype(jnp.bfloat16)
-    normed_lanes = jnp.einsum(
-        "tc,tl->cl", normed_out, spread_tok, preferred_element_type=jnp.float32
-    ).astype(jnp.bfloat16)
     w_rows = w_head.reshape(D, 2 * P_SIZE * P_SIZE, n_off)
+    affine_rows = jnp.einsum(
+        "tc,crk->krt", normed_out, w_rows, preferred_element_type=jnp.float32
+    ) + b_head.reshape(2 * P_SIZE * P_SIZE, n_off).T[:, :, None]
+    high = lax.reduce_precision(affine_rows, exponent_bits=8, mantissa_bits=7)
+    rest = affine_rows - high
+    middle = lax.reduce_precision(rest, exponent_bits=8, mantissa_bits=7)
+    low = rest - middle
+    pieces = jnp.concatenate([high, middle, low], axis=-1).astype(jnp.bfloat16)
+    spread_three = jnp.concatenate([spread_tok, spread_tok, spread_tok], axis=0)
     affine_lanes = jnp.einsum(
-        "crk,cl->krl", w_rows, normed_lanes, preferred_element_type=jnp.float32
-    )
-    base_lane = (lane[0, 0] % P_SIZE == 0) & (lane[0, 0] // LZ % P_SIZE == 0)
-    bias_rows = b_head.reshape(2 * P_SIZE * P_SIZE, n_off).T
-    affine_lanes = affine_lanes + jnp.where(base_lane[None, None, :], bias_rows[:, :, None], 0.0)
+        "krt,tl->krl", pieces, spread_three, preferred_element_type=jnp.float32
+    )
     coupling_lat = affine_lanes[0]
     for k in range(1, n_off):
         offset = k // P_SIZE * LZ + k % P_SIZE

time: 139 us -> 133 us (0.957)
  matrix products: 14.8 us -> 11.8 us
  local copies, waits for them, and re-layouts: 20.4 us -> 17.7 us
    dot_general x1 -> x2, matrix products: 4.78 us -> 1.76 us  [the longest x1 1.27 us: shards(): jnp.einsum('krt,tl->krl', pieces, spread_three, preferred_element_type=jn...]
    squeeze x1, local copies, waits for them, and re-layouts: 2.5 us -> 0.45 us  [shards(): coupling_lat = coupling_lat + jnp.roll(affine_lanes[k], offset, axis=-1)]
    unnamed x93 -> x69, local copies, waits for them, and re-layouts: 3.41 us -> 2.8 us
where the time goes in v7:
time: 133 us
  starting transfers between devices  40.7 us (31%)
  blocking collectives  40.6 us (31%)
  local copies, waits for them, and re-layouts  17.7 us (13%)
  other arithmetic  14.2 us (11%)
  matrix products  11.8 us (9%)
  between operations  4.23 us (3%)
  waiting for transfers between devices  3.31 us (2%)
    all_to_all x1, blocking collectives, shards(): lax.all_to_all(partials, ('space', 'tm'), 0, 0, tiled=True)  40.6 us
    ppermute x4, starting transfers between devices, exchange(): return lax.ppermute(x, axis, [(i, i ^ bit) for i in range(length)])  23.6 us
    ppermute x2, starting transfers between devices, shifted(): lax.ppermute(x, axis, [(i, (i + by) % length) for i in range(length)])  17.2 us
    dot_general x1, matrix products, shards(): jnp.dot(sel_normed, w_qkv[:, D:], preferred_element_type=jnp.float32)  3.14 us
    slice x2, local copies, waits for them, and re-layouts, shards(): keys = kv[:, :D].reshape(n_sel * tokens_dev, HEADS, HS)  3.07 us
    unnamed x69, local copies, waits for them, and re-layouts  2.8 us
  transfers between devices with their start and end apart: 6, of which 3 were waited for; matrix products, arithmetic and copies ran while one was open for 7% of the time, Pallas kernels for 0%

profile of v7, /device:TPU:1, one launch (start us, length us, event | category | flops | bytes accessed | tf_op | source)
XLA Modules:
  0.0 132.6 jit_solution(9541550190103760757)
XLA Ops:
  1.2 1.4 %convert_bitcast_fusion = (bf16[1,128]{1,0:T(2,128)(2,1)S(1)}, s32[128]{0:T(128)S(1)}) fusion(s32[1,1,128]{2,1,0:T(1,128)} %param.16, s32[]{:T(128)} %broadcast.318), kind=kLoop, calls=%fused_computation.199 | loop fusion | flops 128 | bytes 1284 | tf_op jit(solution)/shard_map/convert_element_type | solution.py:118
  3.0 1.1 select_convert_fusion
  7.3 9.6 %collective-permute-start = (bf16[1,129,128]{2,1,0:T(8,128)(2,1)S(1)}, bf16[1,129,128]{2,1,0:T(8,128)(2,1)S(1)}, u32[]{:S(2)}, u32[]{:S(2)}) collective-permute-start(bf16[1,129,128]{2,1,0:T(8,128)(2,1)S(1)} %maximum_bitcast_fusion), channel_id=1, source_target_pairs={{0,8},{1,9},{2,10},{3,11},{4,12},{5,13},{6,14},{7,15},{8,0},{9,1},... | collective-permute-start | bytes 99080 | tf_op jit(solution)/shard_map/ppermute | solution.py:26
  17.0 1.0 add_compare_fusion
  21.4 1.6 %fusion.21 = bf16[128,768]{1,0:T(8,128)(2,1)S(1)} fusion(bf16[768,2304]{1,0:T(8,128)(2,1)} %param.21, f32[128,768]{1,0:T(8,128)S(1)} %get-tuple-element.12, f32[768]{0:T(1024)S(1)} %copy-done.29, f32[128]{0:T(128)S(1)} %add_rsqrt_fusion.2, f32[128]{0:T(128)S(1)} %broadcast_multiply_fusion.2), kind=kOutput, calls=%fused_computation.29 | convolution fusion | flops 151486464 | bytes 1773568 | tf_op jit(solution)/shard_map/dot_general | solution.py:138
  23.1 4.9 %collective-permute-start.1 = (bf16[2,129,128]{2,1,0:T(8,128)(2,1)S(1)}, bf16[2,129,128]{2,1,0:T(8,128)(2,1)S(1)}, u32[]{:S(2)}, u32[]{:S(2)}) collective-permute-start(bf16[2,129,128]{2,1,0:T(8,128)(2,1)S(1)} %pad_maximum_fusion.4), channel_id=1, source_target_pairs={{0,4},{1,5},{2,6},{3,7},{4,0},{5,1},{6,2},{7,3},{8,12},{9,13},{10,... | collective-permute-start | bytes 198152 | tf_op jit(solution)/shard_map/ppermute | solution.py:26
  28.0 1.7 %collective-permute-done.1 = bf16[2,129,128]{2,1,0:T(8,128)(2,1)S(1)} collective-permute-done((bf16[2,129,128]{2,1,0:T(8,128)(2,1)S(1)}, bf16[2,129,128]{2,1,0:T(8,128)(2,1)S(1)}, u32[]{:S(2)}, u32[]{:S(2)}) %collective-permute-start.1) | collective-permute-done | bytes 66080 | tf_op jit(solution)/shard_map/ppermute | solution.py:26
  29.7 3.6 %collective-permute-start.2 = (bf16[4,129,128]{2,1,0:T(8,128)(2,1)S(1)}, bf16[4,129,128]{2,1,0:T(8,128)(2,1)S(1)}, u32[]{:S(2)}, u32[]{:S(2)}) collective-permute-start(bf16[4,129,128]{2,1,0:T(8,128)(2,1)S(1)} %pad_maximum_fusion.1), channel_id=1, source_target_pairs={{0,2},{1,3},{2,0},{3,1},{4,6},{5,7},{6,4},{7,5},{8,10},{9,11},{10,... | collective-permute-start | bytes 396296 | tf_op jit(solution)/shard_map/ppermute | solution.py:26
  34.2 1.1 copy.67
  36.7 5.4 %collective-permute-start.3 = (bf16[8,129,128]{2,1,0:T(8,128)(2,1)S(1)}, bf16[8,129,128]{2,1,0:T(8,128)(2,1)S(1)}, u32[]{:S(2)}, u32[]{:S(2)}) collective-permute-start(bf16[8,129,128]{2,1,0:T(8,128)(2,1)S(1)} %pad_maximum_fusion), channel_id=1, source_target_pairs={{0,1},{1,0},{2,3},{3,2},{4,5},{5,4},{6,7},{7,6},{8,9},{9,8},{10,11... | collective-permute-start | bytes 792584 | tf_op jit(solution)/shard_map/ppermute | solution.py:26
  43.9 1.0 fusion.92
  46.8 3.1 %convolution_convert_fusion = bf16[1024,1536]{1,0:T(8,128)(2,1)S(1)} fusion(bf16[768,2304]{1,0:T(8,128)(2,1)S(1)} %copy-done.28, f32[1024,768]{1,0:T(8,128)S(1)} %get-tuple-element.14, f32[768]{0:T(1024)S(1)} %copy-done.29, f32[1024]{0:T(1024)S(1)} %add_rsqrt_fusion, f32[1024]{0:T(1024)S(1)} %broadcast_multiply_fusion), kind=kOutput, calls=%fused_computation.8 | convolution fusion | flops 2420637696 | bytes 8663040 | tf_op jit(solution)/shard_map/dot_general | solution.py:141
  50.0 1.4 %fusion.89 = (bf16[1024,768]{1,0:T(8,128)(2,1)}, bf16[1024,768]{1,0:T(8,128)(2,1)S(1)}) fusion(bf16[1024,1536]{1,0:T(8,128)(2,1)S(1)} %convolution_convert_fusion), kind=kLoop, calls=%fused_computation.212 | loop fusion | bytes 6291456 | tf_op jit(solution)/shard_map/slice | solution.py:144
  51.3 1.7 %copy.65 = bf16[1024,768]{0,1:T(8,128)(2,1)S(1)} copy(bf16[1024,768]{1,0:T(8,128)(2,1)} %get-tuple-element.30) | data formatting | bytes 3145728 | tf_op jit(solution)/shard_map/slice | solution.py:144
  53.1 1.7 %copy.63 = bf16[1024,768]{0,1:T(8,128)(2,1)} copy(bf16[1024,768]{1,0:T(8,128)(2,1)S(1)} %get-tuple-element.31) | data formatting | bytes 3145728 | tf_op jit(solution)/shard_map/slice | solution.py:145
  54.7 2.0 %multiply_reduce_fusion = (f32[12,128]{1,0:T(8,128)S(1)}, f32[12,128,1024]{2,1,0:T(8,128)S(1)}) fusion(bf16[128,12,64]{0,2,1:T(8,128)(2,1)} %bitcast.196, bf16[1024,12,64]{0,2,1:T(8,128)(2,1)S(1)} %bitcast.184), kind=kOutput, calls=%fused_computation.5 | convolution fusion | flops 204470784 | bytes 8067072 | tf_op jit(solution)/shard_map/qhd,khd->hqk/dot_general | solution.py:147
  56.8 1.3 fusion
  58.2 1.6 %fusion.25 = f32[128,12,64]{0,2,1:T(8,128)S(1)} fusion(bf16[1024,12,64]{0,2,1:T(8,128)(2,1)S(1)} %bitcast.185, f32[12,128,1024]{2,1,0:T(8,128)S(1)} %get-tuple-element.46, f32[12,128]{1,0:T(8,128)S(1)} %get-tuple-element.45, f32[128,12]{0,1:T(8,128)S(1)} %bitcast.200), kind=kOutput, calls=%fused_computation.34 | convolution fusion | flops 206143488 | bytes 8269824 | tf_op jit(solution)/shard_map/hqk,khd->qhd/dot_general | solution.py:156
  60.9 1.3 fusion.7
  63.9 1.0 fusion.50
  66.7 14.6 %collective-permute-start.5 = (bf16[4,1,2048]{2,1,0:T(2,128)(2,1)S(1)}, bf16[4,1,2048]{2,1,0:T(2,128)(2,1)S(1)}, u32[]{:S(2)}, u32[]{:S(2)}) collective-permute-start(bf16[4,1,2048]{2,1,0:T(2,128)(2,1)S(1)} %slice.573), channel_id=1, source_target_pairs={{0,496},{16,0},{32,16},{48,32},{64,48},{80,64},{96,80},{112,96},{1... | collective-permute-start | bytes 49160 | tf_op jit(solution)/shard_map/ppermute | solution.py:52
  81.3 2.6 %collective-permute-start.4 = (bf16[1,4,2048]{2,1,0:T(4,128)(2,1)S(1)}, bf16[1,4,2048]{2,1,0:T(4,128)(2,1)S(1)}, u32[]{:S(2)}, u32[]{:S(2)}) collective-permute-start(bf16[1,4,2048]{2,1,0:T(4,128)(2,1)S(1)} %slice.571), channel_id=1, source_target_pairs={{0,15},{1,0},{2,1},{3,2},{4,3},{5,4},{6,5},{7,6},{8,7},{9,8},{10,9... | collective-permute-start | bytes 49160 | tf_op jit(solution)/shard_map/ppermute | solution.py:52
  86.4 1.6 %fusion.81 = (f32[]{:T(128)}, f32[4,4,2048]{2,1,0:T(4,128)}, f32[4,4,2048]{2,1,0:T(4,128)}, f32[4,4,2048]{2,1,0:T(4,128)}) fusion(f32[4,4,2048]{2,1,0:T(4,128)S(1)} %get-tuple-element.8, f32[4,4,1]{2,1,0:T(4,128)S(1)} %slice.579, f32[4,4,2047]{2,1,0:T(4,128)S(1)} %slice.578, f32[4,4,1985]{2,1,0:T(4,128)S(1)} %bitcast.183, f32[4,4,63]{2,1,0:T(4,128)S(1)} %slice.576, ...), kind=kLoop, calls=%fused_computation.207 | loop fusion | flops 720895 | bytes 1198084 | tf_op jit(solution)/shard_map/reduce_sum | solution.py:208
  88.9 40.6 %all_to_all.6 = f32[512,1,2]{2,1,0:T(1,128)S(1)} all-to-all(f32[512,1,2]{2,1,0:T(1,128)S(1)} %broadcast_in_dim.83), channel_id=1, replica_groups=mesh['space'=32,'tm'=16] {'space','tm'}, dimensions={0} | all-to-all | bytes 8192 | tf_op jit(solution)/shard_map/all_to_all | solution.py:211
  (219 shorter events, 21.4 us)
Async XLA Ops:
  0.6 17.6 %copy-start = (bf16[256,768]{1,0:T(8,128)(2,1)S(1)}, bf16[256,768]{1,0:T(8,128)(2,1)}, u32[]{:S(2)}) copy-start(bf16[256,768]{1,0:T(8,128)(2,1)} %param.18) | copy-start | bytes 1179652
  0.7 6.6 %copy-start.12 = (s32[2048]{0:T(1024)}, s32[2048]{0:T(1024)S(1)}, u32[]{:S(2)}) copy-start(s32[2048]{0:T(1024)S(1)} %get-tuple-element.53) | copy-start | bytes 24580
  0.7 6.6 %copy-start.14 = (s32[2048]{0:T(1024)}, s32[2048]{0:T(1024)S(1)}, u32[]{:S(2)}) copy-start(s32[2048]{0:T(1024)S(1)} %get-tuple-element.56) | copy-start | bytes 24580
  0.7 3.6 %copy-start.16 = (pred[2048]{0:T(1024)(128)(4,1)}, pred[2048]{0:T(1024)(128)(4,1)S(1)}, u32[]{:S(2)}) copy-start(pred[2048]{0:T(1024)(128)(4,1)S(1)} %get-tuple-element.57) | copy-start | bytes 6148
  0.7 3.6 %copy-start.18 = (pred[2048]{0:T(1024)(128)(4,1)}, pred[2048]{0:T(1024)(128)(4,1)S(1)}, u32[]{:S(2)}) copy-start(pred[2048]{0:T(1024)(128)(4,1)S(1)} %get-tuple-element.58) | copy-start | bytes 6148
  3.0 4.3 %copy-start.10 = (s32[2048]{0:T(1024)}, s32[2048]{0:T(1024)S(1)}, u32[]{:S(2)}) copy-start(s32[2048]{0:T(1024)S(1)} %eq.36) | copy-start | bytes 24580
  3.0 13.9 %copy-start.27 = (s32[1,1,128]{2,1,0:T(1,128)S(1)}, s32[1,1,128]{2,1,0:T(1,128)}, u32[]{:S(2)}) copy-start(s32[1,1,128]{2,1,0:T(1,128)} %param.16) | copy-start | bytes 1540
  4.1 13.8 %copy-start.22 = (s32[16,8]{0,1:T(8,128)S(1)}, s32[16,8]{0,1:T(8,128)}, u32[]{:S(2)}) copy-start(s32[16,8]{0,1:T(8,128)} %param.17) | copy-start | bytes 1540
  4.1 14.0 %copy-start.26 = (s32[128]{0:T(128)S(1)}, s32[128]{0:T(128)}, u32[]{:S(2)}) copy-start(s32[128]{0:T(128)} %constant.161) | copy-start | bytes 1540
  4.2 14.0 %copy-start.25 = (s32[128]{0:T(128)S(1)}, s32[128]{0:T(128)}, u32[]{:S(2)}) copy-start(s32[128]{0:T(128)} %constant.162) | copy-start | bytes 1540
  7.3 13.0 %copy-start.20 = (f32[768]{0:T(1024)S(1)}, f32[768]{0:T(1024)}, u32[]{:S(2)}) copy-start(f32[768]{0:T(1024)} %param.19) | copy-start | bytes 9220
  7.3 15.7 %collective-permute-start = (bf16[1,129,128]{2,1,0:T(8,128)(2,1)S(1)}, bf16[1,129,128]{2,1,0:T(8,128)(2,1)S(1)}, u32[]{:S(2)}, u32[]{:S(2)}) collective-permute-start(bf16[1,129,128]{2,1,0:T(8,128)(2,1)S(1)} %maximum_bitcast_fusion), channel_id=1, source_target_pairs={{0,8},{1,9},{2,10},{3,11},{4,12},{5,13},{6,14},{7,15},{8,0},{9,1},... | collective-permute-start | bytes 99080 | tf_op jit(solution)/shard_map/ppermute | solution.py:26
  18.2 2.5 %copy-start.1 = (s32[16]{0:T(128)S(1)}, s32[16]{0:T(128)}, u32[]{:S(2)}) copy-start(s32[16]{0:T(128)} %constant.156.clone) | copy-start | bytes 196
  19.1 2.3 %copy-start.29 = (f32[768]{0:T(1024)S(1)}, f32[768]{0:T(1024)}, u32[]{:S(2)}) copy-start(f32[768]{0:T(1024)} %param.20) | copy-start | bytes 9220
  20.0 14.2 %copy-start.6 = (bf16[768,512]{1,0:T(8,128)(2,1)S(1)}, bf16[768,512]{1,0:T(8,128)(2,1)}, u32[]{:S(2)}) copy-start(bf16[768,512]{1,0:T(8,128)(2,1)} %param.23) | copy-start | bytes 2359300
  20.3 15.0 %copy-start.24 = (f32[512]{0:T(512)S(1)}, f32[512]{0:T(512)}, u32[]{:S(2)}) copy-start(f32[512]{0:T(512)} %param.24) | copy-start | bytes 6148
  20.5 21.7 %copy-start.4 = (f32[128,768]{1,0:T(8,128)}, f32[128,768]{1,0:T(8,128)S(1)}, u32[]{:S(2)}) copy-start(f32[128,768]{1,0:T(8,128)S(1)} %get-tuple-element.12) | copy-start | bytes 1179652
  23.1 6.6 %collective-permute-start.1 = (bf16[2,129,128]{2,1,0:T(8,128)(2,1)S(1)}, bf16[2,129,128]{2,1,0:T(8,128)(2,1)S(1)}, u32[]{:S(2)}, u32[]{:S(2)}) collective-permute-start(bf16[2,129,128]{2,1,0:T(8,128)(2,1)S(1)} %pad_maximum_fusion.4), channel_id=1, source_target_pairs={{0,4},{1,5},{2,6},{3,7},{4,0},{5,1},{6,2},{7,3},{8,12},{9,13},{10,... | collective-permute-start | bytes 198152 | tf_op jit(solution)/shard_map/ppermute | solution.py:26
  29.7 7.0 %collective-permute-start.2 = (bf16[4,129,128]{2,1,0:T(8,128)(2,1)S(1)}, bf16[4,129,128]{2,1,0:T(8,128)(2,1)S(1)}, u32[]{:S(2)}, u32[]{:S(2)}) collective-permute-start(bf16[4,129,128]{2,1,0:T(8,128)(2,1)S(1)} %pad_maximum_fusion.1), channel_id=1, source_target_pairs={{0,2},{1,3},{2,0},{3,1},{4,6},{5,7},{6,4},{7,5},{8,10},{9,11},{10,... | collective-permute-start | bytes 396296 | tf_op jit(solution)/shard_map/ppermute | solution.py:26
  36.7 6.4 %collective-permute-start.3 = (bf16[8,129,128]{2,1,0:T(8,128)(2,1)S(1)}, bf16[8,129,128]{2,1,0:T(8,128)(2,1)S(1)}, u32[]{:S(2)}, u32[]{:S(2)}) collective-permute-start(bf16[8,129,128]{2,1,0:T(8,128)(2,1)S(1)} %pad_maximum_fusion), channel_id=1, source_target_pairs={{0,1},{1,0},{2,3},{3,2},{4,5},{5,4},{6,7},{7,6},{8,9},{9,8},{10,11... | collective-permute-start | bytes 792584 | tf_op jit(solution)/shard_map/ppermute | solution.py:26
  63.4 2.4 %copy-start.8 = (f32[4,4,2048]{2,1,0:T(4,128)S(1)}, f32[4,4,2048]{2,1,0:T(4,128)}, u32[]{:S(2)}) copy-start(f32[4,4,2048]{2,1,0:T(4,128)} %param.15) | copy-start | bytes 393220
  66.6 65.9 %copy-start.2 = (f32[4,4,2048]{2,1,0:T(4,128)}, f32[4,4,2048]{2,1,0:T(4,128)S(1)}, u32[]{:S(2)}) copy-start(f32[4,4,2048]{2,1,0:T(4,128)S(1)} %get-tuple-element.8) | copy-start | bytes 393220
  66.7 18.9 %collective-permute-start.5 = (bf16[4,1,2048]{2,1,0:T(2,128)(2,1)S(1)}, bf16[4,1,2048]{2,1,0:T(2,128)(2,1)S(1)}, u32[]{:S(2)}, u32[]{:S(2)}) collective-permute-start(bf16[4,1,2048]{2,1,0:T(2,128)(2,1)S(1)} %slice.573), channel_id=1, source_target_pairs={{0,496},{16,0},{32,16},{48,32},{64,48},{80,64},{96,80},{112,96},{1... | collective-permute-start | bytes 49160 | tf_op jit(solution)/shard_map/ppermute | solution.py:52
  81.3 5.1 %collective-permute-start.4 = (bf16[1,4,2048]{2,1,0:T(4,128)(2,1)S(1)}, bf16[1,4,2048]{2,1,0:T(4,128)(2,1)S(1)}, u32[]{:S(2)}, u32[]{:S(2)}) collective-permute-start(bf16[1,4,2048]{2,1,0:T(4,128)(2,1)S(1)} %slice.571), channel_id=1, source_target_pairs={{0,15},{1,0},{2,1},{3,2},{4,3},{5,4},{6,5},{7,6},{8,7},{9,8},{10,9... | collective-permute-start | bytes 49160 | tf_op jit(solution)/shard_map/ppermute | solution.py:52
  (13 other events, 23.7 us)

commit v8 on v7

--- a/solution.py
+++ b/solution.py
@@ -138,14 +138,15 @@
     queries = jnp.dot(normed, w_qkv[:, :D], preferred_element_type=jnp.float32).astype(
         jnp.bfloat16
     )
-    kv = jnp.dot(sel_normed, w_qkv[:, D:], preferred_element_type=jnp.float32).astype(
-        jnp.bfloat16
-    )
-    keys = kv[:, :D].reshape(n_sel * tokens_dev, HEADS, HS)
-    values = kv[:, D:].reshape(n_sel * tokens_dev, HEADS, HS)
+    w_kv = w_qkv[:, D:].reshape(D, 2, HEADS, HS)
+    kv = jnp.einsum(
+        "tc,cnhd->nhtd", sel_normed, w_kv, preferred_element_type=jnp.float32
+    ).astype(jnp.bfloat16)
+    keys = kv[0]
+    values = kv[1]
 
     scores = jnp.einsum(
-        "qhd,khd->hqk",
+        "qhd,hkd->hqk",
         queries.reshape(tokens_dev, HEADS, HS),
         keys,
         preferred_element_type=jnp.float32,
@@ -154,7 +155,7 @@
     exp_scores = jnp.exp(scores - row_top)
     row_total = jnp.sum(exp_scores, axis=-1)
     product = jnp.einsum(
-        "hqk,khd->qhd",
+        "hqk,hkd->qhd",
         exp_scores.astype(jnp.bfloat16),
         values,
         preferred_element_type=jnp.float32,

time: 133 us -> 132 us (level)
  other arithmetic: 14.2 us -> 18.3 us
  local copies, waits for them, and re-layouts: 17.7 us -> 15.2 us
    slice x3 -> x0, local copies, waits for them, and re-layouts: 4.72 us -> none  [the longest x2 3.07 us: shards(): keys = kv[:, :D].reshape(n_sel * tokens_dev, HEADS, HS)]
    dot_general x3 -> x2, matrix products: 6.79 us -> 2.92 us  [the longest x1 1.81 us: shards(): jnp.einsum('hqk,hkd->qhd', exp_scores.astype(jnp.bfloat16), values, prefe...]
    unnamed x0 -> x1, matrix products: none -> 3.04 us
    ppermute x4, waiting for transfers between devices: 2.58 us -> 1.09 us  [exchange(): return lax.ppermute(x, axis, [(i, i ^ bit) for i in range(length)])]
    unnamed x69 -> x51, local copies, waits for them, and re-layouts: 2.8 us -> 3.62 us
  transfers between devices with their start and end apart: 6 -> 6, of which waited for: 3 -> 2; matrix products, arithmetic and copies ran while one was open for 7% -> 10% of each run, Pallas kernels for 0% -> 0%
where the time goes in v8:
time: 132 us; the launch traced here: 131 us
  blocking collectives  40.3 us (31%)
  starting transfers between devices  40.1 us (30%)
  other arithmetic  18.3 us (14%)
  local copies, waits for them, and re-layouts  15.2 us (12%)
  matrix products  11 us (8%)
  between operations  4.11 us (3%)
  waiting for transfers between devices  2.17 us (2%)
    all_to_all x1, blocking collectives, shards(): lax.all_to_all(partials, ('space', 'tm'), 0, 0, tiled=True)  40.3 us
    ppermute x4, starting transfers between devices, exchange(): return lax.ppermute(x, axis, [(i, i ^ bit) for i in range(length)])  23.2 us
    ppermute x2, starting transfers between devices, shifted(): lax.ppermute(x, axis, [(i, (i + by) % length) for i in range(length)])  16.8 us
    unnamed x51, local copies, waits for them, and re-layouts  3.62 us
    unnamed x1, matrix products  3.04 us
  transfers between devices with their start and end apart: 6, of which 2 were waited for; matrix products, arithmetic and copies ran while one was open for 10% of the time, Pallas kernels for 0%

profile of v8, /device:TPU:1, one launch (start us, length us, event | category | flops | bytes accessed | tf_op | source)
XLA Modules:
  0.0 131.0 jit_solution(15404721021975576184)
XLA Ops:
  1.2 1.4 %convert_bitcast_fusion.1 = (bf16[1,128]{1,0:T(2,128)(2,1)S(1)}, s32[128]{0:T(128)S(1)}) fusion(s32[1,1,128]{2,1,0:T(1,128)} %param.16, s32[]{:T(128)} %broadcast.318), kind=kLoop, calls=%fused_computation.203 | loop fusion | flops 128 | bytes 1284 | tf_op jit(solution)/shard_map/convert_element_type | solution.py:118
  3.0 1.1 select_convert_fusion
  7.3 9.6 %collective-permute-start = (bf16[1,129,128]{2,1,0:T(8,128)(2,1)S(1)}, bf16[1,129,128]{2,1,0:T(8,128)(2,1)S(1)}, u32[]{:S(2)}, u32[]{:S(2)}) collective-permute-start(bf16[1,129,128]{2,1,0:T(8,128)(2,1)S(1)} %maximum_bitcast_fusion), channel_id=1, source_target_pairs={{0,8},{1,9},{2,10},{3,11},{4,12},{5,13},{6,14},{7,15},{8,0},{9,1},... | collective-permute-start | bytes 99080 | tf_op jit(solution)/shard_map/ppermute | solution.py:26
  18.1 0.9 gather_fusion.1
  19.0 0.9 gather_fusion
  20.6 1.6 %fusion.23 = bf16[128,768]{1,0:T(8,128)(2,1)S(1)} fusion(bf16[768,2304]{1,0:T(8,128)(2,1)} %param.21, f32[128,768]{1,0:T(8,128)S(1)} %get-tuple-element.14, f32[768]{0:T(1024)S(1)} %copy-done.19, f32[128]{0:T(128)S(1)} %add_rsqrt_fusion.2, f32[128]{0:T(128)S(1)} %broadcast_multiply_fusion.2), kind=kOutput, calls=%fused_computation.33 | convolution fusion | flops 151486464 | bytes 1773568 | tf_op jit(solution)/shard_map/dot_general | solution.py:138
  22.9 4.9 %collective-permute-start.1 = (bf16[2,129,128]{2,1,0:T(8,128)(2,1)S(1)}, bf16[2,129,128]{2,1,0:T(8,128)(2,1)S(1)}, u32[]{:S(2)}, u32[]{:S(2)}) collective-permute-start(bf16[2,129,128]{2,1,0:T(8,128)(2,1)S(1)} %pad_maximum_fusion.4), channel_id=1, source_target_pairs={{0,4},{1,5},{2,6},{3,7},{4,0},{5,1},{6,2},{7,3},{8,12},{9,13},{10,... | collective-permute-start | bytes 198152 | tf_op jit(solution)/shard_map/ppermute | solution.py:26
  28.4 1.1 collective-permute-done.1
  30.1 3.6 %collective-permute-start.2 = (bf16[4,129,128]{2,1,0:T(8,128)(2,1)}, bf16[4,129,128]{2,1,0:T(8,128)(2,1)S(1)}, u32[]{:S(2)}, u32[]{:S(2)}) collective-permute-start(bf16[4,129,128]{2,1,0:T(8,128)(2,1)} %pad_maximum_fusion.1), channel_id=1, source_target_pairs={{0,2},{1,3},{2,0},{3,1},{4,6},{5,7},{6,4},{7,5},{8,10},{9,11},{10,... | collective-permute-start | bytes 396296 | tf_op jit(solution)/shard_map/ppermute | solution.py:26
  36.4 1.3 constant_dynamic-update-slice_fusion.22
  37.7 5.0 %collective-permute-start.3 = (bf16[8,129,128]{2,1,0:T(8,128)(2,1)S(1)}, bf16[8,129,128]{2,1,0:T(8,128)(2,1)S(1)}, u32[]{:S(2)}, u32[]{:S(2)}) collective-permute-start(bf16[8,129,128]{2,1,0:T(8,128)(2,1)S(1)} %pad_maximum_fusion), channel_id=1, source_target_pairs={{0,1},{1,0},{2,3},{3,2},{4,5},{5,4},{6,7},{7,6},{8,9},{9,8},{10,11... | collective-permute-start | bytes 792584 | tf_op jit(solution)/shard_map/ppermute | solution.py:26
  45.4 1.8 %gather_fusion.3 = bf16[8,129,128]{2,1,0:T(8,128)(2,1)S(1)} fusion(bf16[16,129,128]{2,1,0:T(8,128)(2,1)} %constant_dynamic-update-slice_fusion.18, s32[1024]{0:T(1024)} %pad_clamp_fusion), kind=kCustom, calls=%fused_computation.3 | custom fusion | bytes 528416 | tf_op jit(solution)/shard_map/jit(_take)/gather | solution.py:132
  48.0 1.0 fusion.93
  51.0 3.0 %fusion.12 = f32[1024,1536]{0,1:S(1)} fusion(bf16[768,2304]{1,0:T(8,128)(2,1)S(1)} %copy-done.18, f32[1024,768]{1,0:T(8,128)S(1)} %get-tuple-element.12, f32[768]{0:T(1024)S(1)} %copy-done.20, f32[1024]{0:T(1024)S(1)} %add_rsqrt_fusion, f32[1024]{0:T(1024)S(1)} %broadcast_multiply_fusion), kind=kOutput, calls=%fused_computation.22 | convolution fusion | flops 2419064832 | bytes 11808768
  54.5 1.1 multiply_reduce_fusion
  55.6 1.3 fusion
  56.9 1.8 %fusion.27 = f32[128,12,64]{0,2,1:T(8,128)S(1)} fusion(f32[12,128,1024]{2,1,0:T(8,128)S(1)} %get-tuple-element.44, f32[12,128]{1,0:T(8,128)S(1)} %get-tuple-element.43, bf16[2,12,1024,64]{2,3,1,0:T(8,128)(2,1)S(1)} %convert_bitcast_fusion, f32[128,12]{0,1:T(8,128)S(1)} %bitcast.213), kind=kOutput, calls=%fused_computation.38 | convolution fusion | flops 206143488 | bytes 8273920 | tf_op jit(solution)/shard_map/hqk,hkd->qhd/dot_general | solution.py:157
  59.8 1.3 fusion.7
  62.8 1.0 fusion.52
  65.5 14.6 %collective-permute-start.5 = (bf16[4,1,2048]{2,1,0:T(2,128)(2,1)S(1)}, bf16[4,1,2048]{2,1,0:T(2,128)(2,1)S(1)}, u32[]{:S(2)}, u32[]{:S(2)}) collective-permute-start(bf16[4,1,2048]{2,1,0:T(2,128)(2,1)S(1)} %slice.573), channel_id=1, source_target_pairs={{0,496},{16,0},{32,16},{48,32},{64,48},{80,64},{96,80},{112,96},{1... | collective-permute-start | bytes 49160 | tf_op jit(solution)/shard_map/ppermute | solution.py:52
  80.2 2.2 %collective-permute-start.4 = (bf16[1,4,2048]{2,1,0:T(4,128)(2,1)S(1)}, bf16[1,4,2048]{2,1,0:T(4,128)(2,1)S(1)}, u32[]{:S(2)}, u32[]{:S(2)}) collective-permute-start(bf16[1,4,2048]{2,1,0:T(4,128)(2,1)S(1)} %slice.571), channel_id=1, source_target_pairs={{0,15},{1,0},{2,1},{3,2},{4,3},{5,4},{6,5},{7,6},{8,7},{9,8},{10,9... | collective-permute-start | bytes 49160 | tf_op jit(solution)/shard_map/ppermute | solution.py:52
  84.2 1.1 collective-permute-done.4
  85.2 1.6 %fusion.83 = (f32[]{:T(128)}, f32[4,4,2048]{2,1,0:T(4,128)}, f32[4,4,2048]{2,1,0:T(4,128)}, f32[4,4,2048]{2,1,0:T(4,128)}) fusion(f32[4,4,2048]{2,1,0:T(4,128)S(1)} %get-tuple-element.8, f32[4,4,1]{2,1,0:T(4,128)S(1)} %slice.579, f32[4,4,2047]{2,1,0:T(4,128)S(1)} %slice.578, f32[4,4,1985]{2,1,0:T(4,128)S(1)} %bitcast.197, f32[4,4,63]{2,1,0:T(4,128)S(1)} %slice.576, ...), kind=kLoop, calls=%fused_computation.211 | loop fusion | flops 720895 | bytes 1198084 | tf_op jit(solution)/shard_map/reduce_sum | solution.py:209
  87.7 40.3 %all_to_all.6 = f32[512,1,2]{2,1,0:T(1,128)S(1)} all-to-all(f32[512,1,2]{2,1,0:T(1,128)S(1)} %broadcast_in_dim.83), channel_id=1, replica_groups=mesh['space'=32,'tm'=16] {'space','tm'}, dimensions={0} | all-to-all | bytes 8192 | tf_op jit(solution)/shard_map/all_to_all | solution.py:212
  (199 shorter events, 23.4 us)
Async XLA Ops:
  0.6 17.5 %copy-start = (bf16[256,768]{1,0:T(8,128)(2,1)S(1)}, bf16[256,768]{1,0:T(8,128)(2,1)}, u32[]{:S(2)}) copy-start(bf16[256,768]{1,0:T(8,128)(2,1)} %param.18) | copy-start | bytes 1179652
  0.7 6.6 %copy-start.5 = (s32[2048]{0:T(1024)}, s32[2048]{0:T(1024)S(1)}, u32[]{:S(2)}) copy-start(s32[2048]{0:T(1024)S(1)} %get-tuple-element.51) | copy-start | bytes 24580
  0.7 6.6 %copy-start.7 = (s32[2048]{0:T(1024)}, s32[2048]{0:T(1024)S(1)}, u32[]{:S(2)}) copy-start(s32[2048]{0:T(1024)S(1)} %get-tuple-element.54) | copy-start | bytes 24580
  0.7 3.6 %copy-start.9 = (pred[2048]{0:T(1024)(128)(4,1)}, pred[2048]{0:T(1024)(128)(4,1)S(1)}, u32[]{:S(2)}) copy-start(pred[2048]{0:T(1024)(128)(4,1)S(1)} %get-tuple-element.56) | copy-start | bytes 6148
  2.6 14.3 %copy-start.13 = (bf16[1,128]{1,0:T(2,128)(2,1)}, bf16[1,128]{1,0:T(2,128)(2,1)S(1)}, u32[]{:S(2)}) copy-start(bf16[1,128]{1,0:T(2,128)(2,1)S(1)} %get-tuple-element.41) | copy-start | bytes 772
  3.0 13.9 %copy-start.17 = (s32[1,1,128]{2,1,0:T(1,128)S(1)}, s32[1,1,128]{2,1,0:T(1,128)}, u32[]{:S(2)}) copy-start(s32[1,1,128]{2,1,0:T(1,128)} %param.16) | copy-start | bytes 1540
  4.1 13.1 %copy-start.14 = (s32[16,8]{0,1:T(8,128)S(1)}, s32[16,8]{0,1:T(8,128)}, u32[]{:S(2)}) copy-start(s32[16,8]{0,1:T(8,128)} %param.17) | copy-start | bytes 1540
  4.1 13.3 %copy-start.16 = (s32[128]{0:T(128)S(1)}, s32[128]{0:T(128)}, u32[]{:S(2)}) copy-start(s32[128]{0:T(128)} %constant.162) | copy-start | bytes 1540
  4.2 13.3 %copy-start.1 = (s32[16]{0:T(128)S(1)}, s32[16]{0:T(128)}, u32[]{:S(2)}) copy-start(s32[16]{0:T(128)} %constant.156.clone) | copy-start | bytes 196
  4.6 13.5 %copy-start.15 = (s32[128]{0:T(128)S(1)}, s32[128]{0:T(128)}, u32[]{:S(2)}) copy-start(s32[128]{0:T(128)} %constant.161) | copy-start | bytes 1540
  7.3 15.6 %collective-permute-start = (bf16[1,129,128]{2,1,0:T(8,128)(2,1)S(1)}, bf16[1,129,128]{2,1,0:T(8,128)(2,1)S(1)}, u32[]{:S(2)}, u32[]{:S(2)}) collective-permute-start(bf16[1,129,128]{2,1,0:T(8,128)(2,1)S(1)} %maximum_bitcast_fusion), channel_id=1, source_target_pairs={{0,8},{1,9},{2,10},{3,11},{4,12},{5,13},{6,14},{7,15},{8,0},{9,1},... | collective-permute-start | bytes 99080 | tf_op jit(solution)/shard_map/ppermute | solution.py:26
  17.0 3.2 %copy-start.11 = (f32[768]{0:T(1024)S(1)}, f32[768]{0:T(1024)}, u32[]{:S(2)}) copy-start(f32[768]{0:T(1024)} %param.19) | copy-start | bytes 9220
  18.1 2.5 %copy-start.19 = (f32[768]{0:T(1024)S(1)}, f32[768]{0:T(1024)}, u32[]{:S(2)}) copy-start(f32[768]{0:T(1024)} %param.20) | copy-start | bytes 9220
  19.9 14.6 %copy-start.3 = (bf16[768,512]{1,0:T(8,128)(2,1)S(1)}, bf16[768,512]{1,0:T(8,128)(2,1)}, u32[]{:S(2)}) copy-start(bf16[768,512]{1,0:T(8,128)(2,1)} %param.23) | copy-start | bytes 2359300
  22.9 6.6 %collective-permute-start.1 = (bf16[2,129,128]{2,1,0:T(8,128)(2,1)S(1)}, bf16[2,129,128]{2,1,0:T(8,128)(2,1)S(1)}, u32[]{:S(2)}, u32[]{:S(2)}) collective-permute-start(bf16[2,129,128]{2,1,0:T(8,128)(2,1)S(1)} %pad_maximum_fusion.4), channel_id=1, source_target_pairs={{0,4},{1,5},{2,6},{3,7},{4,0},{5,1},{6,2},{7,3},{8,12},{9,13},{10,... | collective-permute-start | bytes 198152 | tf_op jit(solution)/shard_map/ppermute | solution.py:26
  30.1 7.6 %collective-permute-start.2 = (bf16[4,129,128]{2,1,0:T(8,128)(2,1)}, bf16[4,129,128]{2,1,0:T(8,128)(2,1)S(1)}, u32[]{:S(2)}, u32[]{:S(2)}) collective-permute-start(bf16[4,129,128]{2,1,0:T(8,128)(2,1)} %pad_maximum_fusion.1), channel_id=1, source_target_pairs={{0,2},{1,3},{2,0},{3,1},{4,6},{5,7},{6,4},{7,5},{8,10},{9,11},{10,... | collective-permute-start | bytes 396296 | tf_op jit(solution)/shard_map/ppermute | solution.py:26
  37.7 7.0 %collective-permute-start.3 = (bf16[8,129,128]{2,1,0:T(8,128)(2,1)S(1)}, bf16[8,129,128]{2,1,0:T(8,128)(2,1)S(1)}, u32[]{:S(2)}, u32[]{:S(2)}) collective-permute-start(bf16[8,129,128]{2,1,0:T(8,128)(2,1)S(1)} %pad_maximum_fusion), channel_id=1, source_target_pairs={{0,1},{1,0},{2,3},{3,2},{4,5},{5,4},{6,7},{7,6},{8,9},{9,8},{10,11... | collective-permute-start | bytes 792584 | tf_op jit(solution)/shard_map/ppermute | solution.py:26
  49.0 2.0 %copy-start.18 = (bf16[768,2304]{1,0:T(8,128)(2,1)S(1)}, bf16[768,2304]{1,0:T(8,128)(2,1)}, u32[]{:S(2)}) copy-start(bf16[768,2304]{1,0:T(8,128)(2,1)} %param.21) | copy-start | bytes 10616836
  56.9 2.3 %copy-start.21 = (f32[768]{0:T(1024)S(1)}, f32[768]{0:T(1024)}, u32[]{:S(2)}) copy-start(f32[768]{0:T(1024)} %param.22) | copy-start | bytes 9220
  62.1 1.8 %copy-start.6 = (s32[2048]{0:T(1024)S(1)}, s32[2048]{0:T(1024)}, u32[]{:S(2)}) copy-start(s32[2048]{0:T(1024)} %copy-done.5) | copy-start | bytes 24580
  62.3 2.4 %copy-start.4 = (f32[4,4,2048]{2,1,0:T(4,128)S(1)}, f32[4,4,2048]{2,1,0:T(4,128)}, u32[]{:S(2)}) copy-start(f32[4,4,2048]{2,1,0:T(4,128)} %param.15) | copy-start | bytes 393220
  65.5 65.5 %copy-start.2 = (f32[4,4,2048]{2,1,0:T(4,128)}, f32[4,4,2048]{2,1,0:T(4,128)S(1)}, u32[]{:S(2)}) copy-start(f32[4,4,2048]{2,1,0:T(4,128)S(1)} %get-tuple-element.8) | copy-start | bytes 393220
  65.5 18.6 %collective-permute-start.5 = (bf16[4,1,2048]{2,1,0:T(2,128)(2,1)S(1)}, bf16[4,1,2048]{2,1,0:T(2,128)(2,1)S(1)}, u32[]{:S(2)}, u32[]{:S(2)}) collective-permute-start(bf16[4,1,2048]{2,1,0:T(2,128)(2,1)S(1)} %slice.573), channel_id=1, source_target_pairs={{0,496},{16,0},{32,16},{48,32},{64,48},{80,64},{96,80},{112,96},{1... | collective-permute-start | bytes 49160 | tf_op jit(solution)/shard_map/ppermute | solution.py:52
  80.2 5.1 %collective-permute-start.4 = (bf16[1,4,2048]{2,1,0:T(4,128)(2,1)S(1)}, bf16[1,4,2048]{2,1,0:T(4,128)(2,1)S(1)}, u32[]{:S(2)}, u32[]{:S(2)}) collective-permute-start(bf16[1,4,2048]{2,1,0:T(4,128)(2,1)S(1)} %slice.571), channel_id=1, source_target_pairs={{0,15},{1,0},{2,1},{3,2},{4,3},{5,4},{6,5},{7,6},{8,7},{9,8},{10,9... | collective-permute-start | bytes 49160 | tf_op jit(solution)/shard_map/ppermute | solution.py:52
  (4 other events, 5.9 us)

commit v9 on v8

--- a/solution.py
+++ b/solution.py
@@ -41,10 +41,12 @@
         bits.append(bit)
         bit *= 2
     offsets = [0]
-    for bit in reversed(bits):
+    for bit in reversed(bits[1:]):
         x = jnp.concatenate([x, exchange(x, axis, bit)], axis=0)
         offsets = offsets + [o ^ bit for o in offsets]
-    return x, offsets
+    received = exchange(x, axis, bits[0])
+    offsets = offsets + [o ^ bits[0] for o in offsets]
+    return x, received, offsets
 
 
 def shifted(x, axis, by):
@@ -117,7 +119,7 @@
     ).astype(jnp.bfloat16)
     bits_f = bits.reshape(1, tokens_dev).astype(jnp.bfloat16)
     send = jnp.concatenate([tokens, bits_f], axis=0)
-    gathered, offsets = doubling_gather(send[None], "tm")
+    kept, received, offsets = doubling_gather(send[None], "tm")
     slot_of = np.argsort(np.asarray(offsets)).astype(np.int32)
 
     w_pair = jnp.concatenate(
@@ -129,7 +131,15 @@
 
     block_rows = lax.dynamic_index_in_dim(block_list, lax.axis_index("tm"), 0, keepdims=False)
     own = lax.axis_index("tm")
-    chosen = jnp.take(gathered, jnp.asarray(slot_of)[block_rows ^ own], axis=0)
+    slots = jnp.asarray(slot_of)[block_rows ^ own]
+    n_half = kept.shape[0]
+    half_ids = jnp.arange(n_half, dtype=jnp.int32)[None, :]
+    pick_kept = (slots[:, None] == half_ids).astype(jnp.bfloat16)
+    pick_received = (slots[:, None] == half_ids + n_half).astype(jnp.bfloat16)
+    chosen = (
+        jnp.einsum("ip,pab->iab", pick_kept, kept, preferred_element_type=jnp.float32)
+        + jnp.einsum("ip,pab->iab", pick_received, received, preferred_element_type=jnp.float32)
+    ).astype(jnp.bfloat16)
     n_sel = chosen.shape[0]
     sel_tokens = chosen[:, :tokens_dev, :].reshape(n_sel * tokens_dev, patch_len // 2)
     sel_bits = chosen[:, tokens_dev, :].reshape(n_sel * tokens_dev).astype(jnp.float32)

time: 132 us -> 129 us (0.977)
  local copies, waits for them, and re-layouts: 15.2 us -> 9.45 us
  starting transfers between devices: 40.1 us -> 44.3 us
  other arithmetic: 18.3 us -> 15 us
  matrix products: 11 us -> 12.5 us
    ppermute x4, starting transfers between devices: 23.2 us -> 25.9 us  [exchange(): return lax.ppermute(x, axis, [(i, i ^ bit) for i in range(length)])]
    unnamed x51 -> x34, local copies, waits for them, and re-layouts: 3.62 us -> 1.69 us
    gather x2 -> x1, local copies, waits for them, and re-layouts: 2.42 us -> 0.64 us  [shards(): slots = jnp.asarray(slot_of)[block_rows ^ own]]
    dot_general x0 -> x2, matrix products: none -> 1.52 us  [the longest x1 1.23 us: shards(): jnp.einsum('ip,pab->iab', pick_received, received, preferred_element_type...]
    ppermute x2, starting transfers between devices: 16.8 us -> 18.3 us  [shifted(): lax.ppermute(x, axis, [(i, (i + by) % length) for i in range(length)])]
  transfers between devices with their start and end apart: 6 -> 6, of which waited for: 2 -> 2; matrix products, arithmetic and copies ran while one was open for 10% -> 6% of each run, Pallas kernels for 0% -> 0%
where the time goes in v9:
time: 129 us
  starting transfers between devices  44.3 us (34%)
  blocking collectives  40 us (31%)
  other arithmetic  15 us (12%)
  matrix products  12.5 us (10%)
  local copies, waits for them, and re-layouts  9.45 us (7%)
  between operations  4.09 us (3%)
  waiting for transfers between devices  3.33 us (3%)
    all_to_all x1, blocking collectives, shards(): lax.all_to_all(partials, ('space', 'tm'), 0, 0, tiled=True)  40 us
    ppermute x4, starting transfers between devices, exchange(): return lax.ppermute(x, axis, [(i, i ^ bit) for i in range(length)])  25.9 us
    ppermute x2, starting transfers between devices, shifted(): lax.ppermute(x, axis, [(i, (i + by) % length) for i in range(length)])  18.3 us
    unnamed x1, matrix products  3.04 us
  transfers between devices with their start and end apart: 6, of which 2 were waited for; matrix products, arithmetic and copies ran while one was open for 6% of the time, Pallas kernels for 0%

profile of v9, /device:TPU:1, one launch (start us, length us, event | category | flops | bytes accessed | tf_op | source)
XLA Modules:
  0.0 128.6 jit_solution(2529268476966611784)
XLA Ops:
  1.2 1.4 %convert_bitcast_fusion.1 = (bf16[1,128]{1,0:T(2,128)(2,1)S(1)}, s32[128]{0:T(128)S(1)}) fusion(s32[1,1,128]{2,1,0:T(1,128)} %param.16, s32[]{:T(128)} %broadcast.282), kind=kLoop, calls=%fused_computation.204 | loop fusion | flops 128 | bytes 1284 | tf_op jit(solution)/shard_map/convert_element_type | solution.py:120
  3.0 1.1 select_convert_fusion
  7.2 9.6 %collective-permute-start = (bf16[1,129,128]{2,1,0:T(8,128)(2,1)S(1)}, bf16[1,129,128]{2,1,0:T(8,128)(2,1)S(1)}, u32[]{:S(2)}, u32[]{:S(2)}) collective-permute-start(bf16[1,129,128]{2,1,0:T(8,128)(2,1)S(1)} %maximum_bitcast_fusion), channel_id=1, source_target_pairs={{0,8},{1,9},{2,10},{3,11},{4,12},{5,13},{6,14},{7,15},{8,0},{9,1},... | collective-permute-start | bytes 99080 | tf_op jit(solution)/shard_map/ppermute | solution.py:26
  17.1 0.9 gather_fusion
  18.1 0.9 gather_fusion.1
  19.7 4.9 %collective-permute-start.1 = (bf16[2,129,128]{2,1,0:T(8,128)(2,1)S(1)}, bf16[2,129,128]{2,1,0:T(8,128)(2,1)S(1)}, u32[]{:S(2)}, u32[]{:S(2)}) collective-permute-start(bf16[2,129,128]{2,1,0:T(8,128)(2,1)S(1)} %pad_maximum_fusion.4), channel_id=1, source_target_pairs={{0,4},{1,5},{2,6},{3,7},{4,0},{5,1},{6,2},{7,3},{8,12},{9,13},{10,... | collective-permute-start | bytes 198152 | tf_op jit(solution)/shard_map/ppermute | solution.py:26
  24.6 1.6 %fusion.24 = bf16[128,768]{1,0:T(8,128)(2,1)S(1)} fusion(bf16[768,2304]{1,0:T(8,128)(2,1)} %param.21, f32[128,768]{1,0:T(8,128)S(1)} %get-tuple-element.14, f32[768]{0:T(1024)S(1)} %copy-done.12, f32[128]{0:T(128)S(1)} %add_rsqrt_fusion.2, f32[128]{0:T(128)S(1)} %broadcast_multiply_fusion.2), kind=kOutput, calls=%fused_computation.34 | convolution fusion | flops 151486464 | bytes 1773568 | tf_op jit(solution)/shard_map/dot_general | solution.py:148
  26.5 3.5 %collective-permute-start.2 = (bf16[4,129,128]{2,1,0:T(8,128)(2,1)S(1)}, bf16[4,129,128]{2,1,0:T(8,128)(2,1)S(1)}, u32[]{:S(2)}, u32[]{:S(2)}) collective-permute-start(bf16[4,129,128]{2,1,0:T(8,128)(2,1)S(1)} %pad_maximum_fusion.1), channel_id=1, source_target_pairs={{0,2},{1,3},{2,0},{3,1},{4,6},{5,7},{6,4},{7,5},{8,10},{9,11},{10,... | collective-permute-start | bytes 396296 | tf_op jit(solution)/shard_map/ppermute | solution.py:26
  30.6 1.9 %collective-permute-done.2 = bf16[4,129,128]{2,1,0:T(8,128)(2,1)S(1)} collective-permute-done((bf16[4,129,128]{2,1,0:T(8,128)(2,1)S(1)}, bf16[4,129,128]{2,1,0:T(8,128)(2,1)S(1)}, u32[]{:S(2)}, u32[]{:S(2)}) %collective-permute-start.2) | collective-permute-done | bytes 132128 | tf_op jit(solution)/shard_map/ppermute | solution.py:26
  32.5 7.8 %collective-permute-start.3 = (bf16[8,129,128]{2,1,0:T(8,128)(2,1)S(1)}, bf16[8,129,128]{2,1,0:T(8,128)(2,1)}, u32[]{:S(2)}, u32[]{:S(2)}) collective-permute-start(bf16[8,129,128]{2,1,0:T(8,128)(2,1)S(1)} %pad_maximum_fusion), channel_id=1, source_target_pairs={{0,1},{1,0},{2,3},{3,2},{4,5},{5,4},{6,7},{7,6},{8,9},{9,8},{10,11... | collective-permute-start | bytes 792584 | tf_op jit(solution)/shard_map/ppermute | solution.py:26
  42.4 1.2 fusion.38
  44.0 1.0 fusion.104
  47.0 3.0 %fusion.12 = f32[1024,1536]{0,1:S(1)} fusion(bf16[768,2304]{1,0:T(8,128)(2,1)S(1)} %copy-done.11, f32[1024,768]{1,0:T(8,128)S(1)} %get-tuple-element.12, f32[768]{0:T(1024)S(1)} %copy-done.13, f32[1024]{0:T(1024)S(1)} %add_rsqrt_fusion, f32[1024]{0:T(1024)S(1)} %broadcast_multiply_fusion), kind=kOutput, calls=%fused_computation.21 | convolution fusion | flops 2419064832 | bytes 11808768
  50.5 1.1 multiply_reduce_fusion
  51.6 1.3 %fusion = f32[12,128]{1,0:T(8,128)S(1)} fusion(f32[12,128,1024]{2,1,0:T(8,128)S(1)} %get-tuple-element.44, f32[12,128]{1,0:T(8,128)S(1)} %get-tuple-element.43), kind=kLoop, calls=%fused_computation.5 | loop fusion | flops 4717056 | bytes 6303744 | tf_op jit(solution)/shard_map/reduce_sum | solution.py:166
  52.9 1.8 %fusion.28 = f32[128,12,64]{0,2,1:T(8,128)S(1)} fusion(f32[12,128,1024]{2,1,0:T(8,128)S(1)} %get-tuple-element.44, f32[12,128]{1,0:T(8,128)S(1)} %get-tuple-element.43, bf16[2,12,1024,64]{2,3,1,0:T(8,128)(2,1)S(1)} %convert_bitcast_fusion, f32[128,12]{0,1:T(8,128)S(1)} %bitcast.214), kind=kOutput, calls=%fused_computation.39 | convolution fusion | flops 206143488 | bytes 8273920 | tf_op jit(solution)/shard_map/hqk,hkd->qhd/dot_general | solution.py:167
  55.8 1.3 fusion.7
  58.8 1.0 fusion.56
  60.6 0.8 fusion.96
  61.5 16.1 %collective-permute-start.5 = (bf16[4,1,2048]{2,1,0:T(2,128)(2,1)S(1)}, bf16[4,1,2048]{2,1,0:T(2,128)(2,1)S(1)}, u32[]{:S(2)}, u32[]{:S(2)}) collective-permute-start(bf16[4,1,2048]{2,1,0:T(2,128)(2,1)S(1)} %slice.571), channel_id=1, source_target_pairs={{0,496},{16,0},{32,16},{48,32},{64,48},{80,64},{96,80},{112,96},{1... | collective-permute-start | bytes 49160 | tf_op jit(solution)/shard_map/ppermute | solution.py:54
  77.6 2.2 %collective-permute-start.4 = (bf16[1,4,2048]{2,1,0:T(4,128)(2,1)S(1)}, bf16[1,4,2048]{2,1,0:T(4,128)(2,1)S(1)}, u32[]{:S(2)}, u32[]{:S(2)}) collective-permute-start(bf16[1,4,2048]{2,1,0:T(4,128)(2,1)S(1)} %slice.569), channel_id=1, source_target_pairs={{0,15},{1,0},{2,1},{3,2},{4,3},{5,4},{6,5},{7,6},{8,7},{9,8},{10,9... | collective-permute-start | bytes 49160 | tf_op jit(solution)/shard_map/ppermute | solution.py:54
  81.6 1.4 %collective-permute-done.4 = bf16[1,4,2048]{2,1,0:T(4,128)(2,1)S(1)} collective-permute-done((bf16[1,4,2048]{2,1,0:T(4,128)(2,1)S(1)}, bf16[1,4,2048]{2,1,0:T(4,128)(2,1)S(1)}, u32[]{:S(2)}, u32[]{:S(2)}) %collective-permute-start.4) | collective-permute-done | bytes 16416 | tf_op jit(solution)/shard_map/ppermute | solution.py:54
  83.0 1.6 %fusion.94 = (f32[]{:T(128)}, f32[4,4,2048]{2,1,0:T(4,128)}, f32[4,4,2048]{2,1,0:T(4,128)}, f32[4,4,2048]{2,1,0:T(4,128)}) fusion(f32[4,4,2048]{2,1,0:T(4,128)S(1)} %get-tuple-element.8, f32[4,4,1]{2,1,0:T(4,128)S(1)} %slice.577, f32[4,4,2047]{2,1,0:T(4,128)S(1)} %slice.576, f32[4,4,1985]{2,1,0:T(4,128)S(1)} %bitcast.198, f32[4,4,63]{2,1,0:T(4,128)S(1)} %slice.574, ...), kind=kLoop, calls=%fused_computation.212 | loop fusion | flops 720895 | bytes 1198084 | tf_op jit(solution)/shard_map/reduce_sum | solution.py:219
  85.5 40.0 %all_to_all.6 = f32[512,1,2]{2,1,0:T(1,128)S(1)} all-to-all(f32[512,1,2]{2,1,0:T(1,128)S(1)} %broadcast_in_dim.74), channel_id=1, replica_groups=mesh['space'=32,'tm'=16] {'space','tm'}, dimensions={0} | all-to-all | bytes 8192 | tf_op jit(solution)/shard_map/all_to_all | solution.py:222
  (179 shorter events, 17.0 us)
Async XLA Ops:
  0.6 16.5 %copy-start = (bf16[256,768]{1,0:T(8,128)(2,1)S(1)}, bf16[256,768]{1,0:T(8,128)(2,1)}, u32[]{:S(2)}) copy-start(bf16[256,768]{1,0:T(8,128)(2,1)} %param.18) | copy-start | bytes 1179652
  3.0 13.9 %copy-start.10 = (s32[1,1,128]{2,1,0:T(1,128)S(1)}, s32[1,1,128]{2,1,0:T(1,128)}, u32[]{:S(2)}) copy-start(s32[1,1,128]{2,1,0:T(1,128)} %param.16) | copy-start | bytes 1540
  4.1 13.0 %copy-start.8 = (s32[128]{0:T(128)S(1)}, s32[128]{0:T(128)}, u32[]{:S(2)}) copy-start(s32[128]{0:T(128)} %constant.150) | copy-start | bytes 1540
  4.1 13.0 %copy-start.9 = (s32[128]{0:T(128)S(1)}, s32[128]{0:T(128)}, u32[]{:S(2)}) copy-start(s32[128]{0:T(128)} %constant.151) | copy-start | bytes 1540
  7.2 12.1 %copy-start.5 = (f32[768]{0:T(1024)S(1)}, f32[768]{0:T(1024)}, u32[]{:S(2)}) copy-start(f32[768]{0:T(1024)} %param.19) | copy-start | bytes 9220
  7.2 12.5 %collective-permute-start = (bf16[1,129,128]{2,1,0:T(8,128)(2,1)S(1)}, bf16[1,129,128]{2,1,0:T(8,128)(2,1)S(1)}, u32[]{:S(2)}, u32[]{:S(2)}) collective-permute-start(bf16[1,129,128]{2,1,0:T(8,128)(2,1)S(1)} %maximum_bitcast_fusion), channel_id=1, source_target_pairs={{0,8},{1,9},{2,10},{3,11},{4,12},{5,13},{6,14},{7,15},{8,0},{9,1},... | collective-permute-start | bytes 99080 | tf_op jit(solution)/shard_map/ppermute | solution.py:26
  18.0 6.6 %copy-start.12 = (f32[768]{0:T(1024)S(1)}, f32[768]{0:T(1024)}, u32[]{:S(2)}) copy-start(f32[768]{0:T(1024)} %param.20) | copy-start | bytes 9220
  18.0 8.2 %copy-start.6 = (s32[16,8]{0,1:T(8,128)S(1)}, s32[16,8]{0,1:T(8,128)}, u32[]{:S(2)}) copy-start(s32[16,8]{0,1:T(8,128)} %param.17) | copy-start | bytes 1540
  18.9 21.6 %copy-start.3 = (bf16[768,512]{1,0:T(8,128)(2,1)S(1)}, bf16[768,512]{1,0:T(8,128)(2,1)}, u32[]{:S(2)}) copy-start(bf16[768,512]{1,0:T(8,128)(2,1)} %param.23) | copy-start | bytes 2359300
  19.2 21.6 %copy-start.7 = (f32[512]{0:T(512)S(1)}, f32[512]{0:T(512)}, u32[]{:S(2)}) copy-start(f32[512]{0:T(512)} %param.24) | copy-start | bytes 6148
  19.2 22.5 %copy-start.1 = (s32[16]{0:T(128)S(1)}, s32[16]{0:T(128)}, u32[]{:S(2)}) copy-start(s32[16]{0:T(128)} %constant.145.clone) | copy-start | bytes 196
  19.7 6.8 %collective-permute-start.1 = (bf16[2,129,128]{2,1,0:T(8,128)(2,1)S(1)}, bf16[2,129,128]{2,1,0:T(8,128)(2,1)S(1)}, u32[]{:S(2)}, u32[]{:S(2)}) collective-permute-start(bf16[2,129,128]{2,1,0:T(8,128)(2,1)S(1)} %pad_maximum_fusion.4), channel_id=1, source_target_pairs={{0,4},{1,5},{2,6},{3,7},{4,0},{5,1},{6,2},{7,3},{8,12},{9,13},{10,... | collective-permute-start | bytes 198152 | tf_op jit(solution)/shard_map/ppermute | solution.py:26
  26.5 6.0 %collective-permute-start.2 = (bf16[4,129,128]{2,1,0:T(8,128)(2,1)S(1)}, bf16[4,129,128]{2,1,0:T(8,128)(2,1)S(1)}, u32[]{:S(2)}, u32[]{:S(2)}) collective-permute-start(bf16[4,129,128]{2,1,0:T(8,128)(2,1)S(1)} %pad_maximum_fusion.1), channel_id=1, source_target_pairs={{0,2},{1,3},{2,0},{3,1},{4,6},{5,7},{6,4},{7,5},{8,10},{9,11},{10,... | collective-permute-start | bytes 396296 | tf_op jit(solution)/shard_map/ppermute | solution.py:26
  32.5 9.9 %collective-permute-start.3 = (bf16[8,129,128]{2,1,0:T(8,128)(2,1)S(1)}, bf16[8,129,128]{2,1,0:T(8,128)(2,1)}, u32[]{:S(2)}, u32[]{:S(2)}) collective-permute-start(bf16[8,129,128]{2,1,0:T(8,128)(2,1)S(1)} %pad_maximum_fusion), channel_id=1, source_target_pairs={{0,1},{1,0},{2,3},{3,2},{4,5},{5,4},{6,7},{7,6},{8,9},{9,8},{10,11... | collective-permute-start | bytes 792584 | tf_op jit(solution)/shard_map/ppermute | solution.py:26
  45.0 2.0 %copy-start.11 = (bf16[768,2304]{1,0:T(8,128)(2,1)S(1)}, bf16[768,2304]{1,0:T(8,128)(2,1)}, u32[]{:S(2)}) copy-start(bf16[768,2304]{1,0:T(8,128)(2,1)} %param.21) | copy-start | bytes 10616836
  45.6 1.3 %copy-start.13 = (f32[768]{0:T(1024)S(1)}, f32[768]{0:T(1024)}, u32[]{:S(2)}) copy-start(f32[768]{0:T(1024)} %param.20) | copy-start | bytes 9220
  52.9 2.3 %copy-start.14 = (f32[768]{0:T(1024)S(1)}, f32[768]{0:T(1024)}, u32[]{:S(2)}) copy-start(f32[768]{0:T(1024)} %param.22) | copy-start | bytes 9220
  58.2 2.4 %copy-start.4 = (f32[4,4,2048]{2,1,0:T(4,128)S(1)}, f32[4,4,2048]{2,1,0:T(4,128)}, u32[]{:S(2)}) copy-start(f32[4,4,2048]{2,1,0:T(4,128)} %param.15) | copy-start | bytes 393220
  61.4 67.2 %copy-start.2 = (f32[4,4,2048]{2,1,0:T(4,128)}, f32[4,4,2048]{2,1,0:T(4,128)S(1)}, u32[]{:S(2)}) copy-start(f32[4,4,2048]{2,1,0:T(4,128)S(1)} %get-tuple-element.8) | copy-start | bytes 393220
  61.5 20.1 %collective-permute-start.5 = (bf16[4,1,2048]{2,1,0:T(2,128)(2,1)S(1)}, bf16[4,1,2048]{2,1,0:T(2,128)(2,1)S(1)}, u32[]{:S(2)}, u32[]{:S(2)}) collective-permute-start(bf16[4,1,2048]{2,1,0:T(2,128)(2,1)S(1)} %slice.571), channel_id=1, source_target_pairs={{0,496},{16,0},{32,16},{48,32},{64,48},{80,64},{96,80},{112,96},{1... | collective-permute-start | bytes 49160 | tf_op jit(solution)/shard_map/ppermute | solution.py:54
  77.6 5.4 %collective-permute-start.4 = (bf16[1,4,2048]{2,1,0:T(4,128)(2,1)S(1)}, bf16[1,4,2048]{2,1,0:T(4,128)(2,1)S(1)}, u32[]{:S(2)}, u32[]{:S(2)}) collective-permute-start(bf16[1,4,2048]{2,1,0:T(4,128)(2,1)S(1)} %slice.569), channel_id=1, source_target_pairs={{0,15},{1,0},{2,1},{3,2},{4,3},{5,4},{6,5},{7,6},{8,7},{9,8},{10,9... | collective-permute-start | bytes 49160 | tf_op jit(solution)/shard_map/ppermute | solution.py:54

commit v10 on v9

--- a/solution.py
+++ b/solution.py
@@ -145,9 +145,10 @@
     sel_bits = chosen[:, tokens_dev, :].reshape(n_sel * tokens_dev).astype(jnp.float32)
     sel_embedded = embed_packed(sel_tokens, sel_bits, w_pair, b_embed)
     sel_normed = layer_norm(sel_embedded, gain_in).astype(jnp.bfloat16)
-    queries = jnp.dot(normed, w_qkv[:, :D], preferred_element_type=jnp.float32).astype(
-        jnp.bfloat16
-    )
+    queries = jnp.einsum(
+        "tc,chd->htd", normed, w_qkv[:, :D].reshape(D, HEADS, HS),
+        preferred_element_type=jnp.float32,
+    ).astype(jnp.bfloat16)
     w_kv = w_qkv[:, D:].reshape(D, 2, HEADS, HS)
     kv = jnp.einsum(
         "tc,cnhd->nhtd", sel_normed, w_kv, preferred_element_type=jnp.float32
@@ -156,8 +157,8 @@
     values = kv[1]
 
     scores = jnp.einsum(
-        "qhd,hkd->hqk",
-        queries.reshape(tokens_dev, HEADS, HS),
+        "hqd,hkd->hqk",
+        queries,
         keys,
         preferred_element_type=jnp.float32,
     ) * HS ** (-0.5)

time: 129 us -> 128 us (level)
    unnamed x1 -> x2, matrix products: 3.04 us -> 4.96 us
    dot_general x2 -> x1, matrix products: 2.75 us -> 1.11 us  [shards(): jnp.einsum('hqd,hkd->hqk', queries, keys, preferred_element_type=jnp.floa...]
  transfers between devices with their start and end apart: 6 -> 6, of which waited for: 2 -> 3; matrix products, arithmetic and copies ran while one was open for 6% -> 5% of each run, Pallas kernels for 0% -> 0%
where the time goes in v10:
time: 128 us
  starting transfers between devices  44.2 us (35%)
  blocking collectives  40 us (31%)
  other arithmetic  13.9 us (11%)
  matrix products  11.8 us (9%)
  local copies, waits for them, and re-layouts  9.25 us (7%)
  waiting for transfers between devices  4.3 us (3%)
  between operations  4.07 us (3%)
    all_to_all x1, blocking collectives, shards(): lax.all_to_all(partials, ('space', 'tm'), 0, 0, tiled=True)  40 us
    ppermute x4, starting transfers between devices, exchange(): return lax.ppermute(x, axis, [(i, i ^ bit) for i in range(length)])  25.9 us
    ppermute x2, starting transfers between devices, shifted(): lax.ppermute(x, axis, [(i, (i + by) % length) for i in range(length)])  18.3 us
    unnamed x2, matrix products  4.96 us
    ppermute x4, waiting for transfers between devices, exchange(): return lax.ppermute(x, axis, [(i, i ^ bit) for i in range(length)])  2.9 us
  transfers between devices with their start and end apart: 6, of which 3 were waited for; matrix products, arithmetic and copies ran while one was open for 5% of the time, Pallas kernels for 0%

profile of v10, /device:TPU:1, one launch (start us, length us, event | category | flops | bytes accessed | tf_op | source)
XLA Modules:
  0.0 127.5 jit_solution(2233112849968950533)
XLA Ops:
  1.2 1.4 %convert_bitcast_fusion.1 = (bf16[1,128]{1,0:T(2,128)(2,1)S(1)}, s32[128]{0:T(128)S(1)}) fusion(s32[1,1,128]{2,1,0:T(1,128)} %param.16, s32[]{:T(128)} %broadcast.282), kind=kLoop, calls=%fused_computation.205 | loop fusion | flops 128 | bytes 1284 | tf_op jit(solution)/shard_map/convert_element_type | solution.py:120
  3.0 1.1 select_convert_fusion
  7.2 9.6 %collective-permute-start = (bf16[1,129,128]{2,1,0:T(8,128)(2,1)S(1)}, bf16[1,129,128]{2,1,0:T(8,128)(2,1)S(1)}, u32[]{:S(2)}, u32[]{:S(2)}) collective-permute-start(bf16[1,129,128]{2,1,0:T(8,128)(2,1)S(1)} %maximum_bitcast_fusion), channel_id=1, source_target_pairs={{0,8},{1,9},{2,10},{3,11},{4,12},{5,13},{6,14},{7,15},{8,0},{9,1},... | collective-permute-start | bytes 99080 | tf_op jit(solution)/shard_map/ppermute | solution.py:26
  17.2 0.9 gather_fusion
  18.1 0.9 gather_fusion.1
  19.9 4.9 %collective-permute-start.1 = (bf16[2,129,128]{2,1,0:T(8,128)(2,1)S(1)}, bf16[2,129,128]{2,1,0:T(8,128)(2,1)S(1)}, u32[]{:S(2)}, u32[]{:S(2)}) collective-permute-start(bf16[2,129,128]{2,1,0:T(8,128)(2,1)S(1)} %pad_maximum_fusion.4), channel_id=1, source_target_pairs={{0,4},{1,5},{2,6},{3,7},{4,0},{5,1},{6,2},{7,3},{8,12},{9,13},{10,... | collective-permute-start | bytes 198152 | tf_op jit(solution)/shard_map/ppermute | solution.py:26
  24.8 1.7 %collective-permute-done.1 = bf16[2,129,128]{2,1,0:T(8,128)(2,1)S(1)} collective-permute-done((bf16[2,129,128]{2,1,0:T(8,128)(2,1)S(1)}, bf16[2,129,128]{2,1,0:T(8,128)(2,1)S(1)}, u32[]{:S(2)}, u32[]{:S(2)}) %collective-permute-start.1) | collective-permute-done | bytes 66080 | tf_op jit(solution)/shard_map/ppermute | solution.py:26
  26.5 3.5 %collective-permute-start.2 = (bf16[4,129,128]{2,1,0:T(8,128)(2,1)S(1)}, bf16[4,129,128]{2,1,0:T(8,128)(2,1)S(1)}, u32[]{:S(2)}, u32[]{:S(2)}) collective-permute-start(bf16[4,129,128]{2,1,0:T(8,128)(2,1)S(1)} %pad_maximum_fusion.1), channel_id=1, source_target_pairs={{0,2},{1,3},{2,0},{3,1},{4,6},{5,7},{6,4},{7,5},{8,10},{9,11},{10,... | collective-permute-start | bytes 396296 | tf_op jit(solution)/shard_map/ppermute | solution.py:26
  31.3 1.2 collective-permute-done.2
  32.5 7.8 %collective-permute-start.3 = (bf16[8,129,128]{2,1,0:T(8,128)(2,1)S(1)}, bf16[8,129,128]{2,1,0:T(8,128)(2,1)S(1)}, u32[]{:S(2)}, u32[]{:S(2)}) collective-permute-start(bf16[8,129,128]{2,1,0:T(8,128)(2,1)S(1)} %pad_maximum_fusion), channel_id=1, source_target_pairs={{0,1},{1,0},{2,3},{3,2},{4,5},{5,4},{6,7},{7,6},{8,9},{9,8},{10,11... | collective-permute-start | bytes 792584 | tf_op jit(solution)/shard_map/ppermute | solution.py:26
  40.4 1.9 %fusion.22 = f32[128,768]{0,1:S(1)} fusion(bf16[768,2304]{1,0:T(8,128)(2,1)} %param.21, f32[128,768]{1,0:T(8,128)S(1)} %get-tuple-element.12, f32[768]{0:T(1024)S(1)} %copy-done.7, f32[128]{0:T(128)S(1)} %add_rsqrt_fusion.2, f32[128]{0:T(128)S(1)} %broadcast_multiply_fusion.2), kind=kOutput, calls=%fused_computation.32 | convolution fusion | flops 151388160 | bytes 1970176
  42.9 1.0 fusion.103
  45.9 3.0 %fusion.12 = f32[1024,1536]{0,1:S(1)} fusion(bf16[768,2304]{1,0:T(8,128)(2,1)S(1)} %copy-done.5, f32[1024,768]{1,0:T(8,128)S(1)} %get-tuple-element.14, f32[768]{0:T(1024)S(1)} %copy-done.7, f32[1024]{0:T(1024)S(1)} %add_rsqrt_fusion, f32[1024]{0:T(1024)S(1)} %broadcast_multiply_fusion), kind=kOutput, calls=%fused_computation.21 | convolution fusion | flops 2419064832 | bytes 11808768
  49.5 1.1 multiply_reduce_fusion
  50.6 1.3 %fusion = f32[12,128]{1,0:T(8,128)S(1)} fusion(f32[12,128,1024]{2,1,0:T(8,128)S(1)} %get-tuple-element.44, f32[12,128]{1,0:T(8,128)S(1)} %get-tuple-element.43), kind=kLoop, calls=%fused_computation.5 | loop fusion | flops 4717056 | bytes 6303744 | tf_op jit(solution)/shard_map/reduce_sum | solution.py:167
  51.9 1.8 %fusion.25 = f32[128,12,64]{0,2,1:T(8,128)S(1)} fusion(f32[12,128,1024]{2,1,0:T(8,128)S(1)} %get-tuple-element.44, f32[12,128]{1,0:T(8,128)S(1)} %get-tuple-element.43, bf16[2,12,1024,64]{2,3,1,0:T(8,128)(2,1)S(1)} %convert_bitcast_fusion, f32[128,12]{0,1:T(8,128)S(1)} %bitcast.221), kind=kOutput, calls=%fused_computation.38 | convolution fusion | flops 206143488 | bytes 8273920 | tf_op jit(solution)/shard_map/hqk,hkd->qhd/dot_general | solution.py:168
  54.7 1.3 %fusion.7 = f32[16,32,2048]{2,1,0:T(8,128)S(1)} fusion(pred[128,2048]{1,0:T(32,128)(4,1)S(1)} %add_compare_fusion, bf16[16,32,128]{2,1,0:T(8,128)(2,1)S(1)} %get-tuple-element.36, bf16[16,32,128]{2,1,0:T(8,128)(2,1)S(1)} %get-tuple-element.37, bf16[16,32,128]{2,1,0:T(8,128)(2,1)S(1)} %get-tuple-element.35), kind=kOutput, calls=%fused_computation.16 | convolution fusion | flops 808058880 | bytes 4849664 | tf_op jit(solution)/shard_map/krt,tl->krl/dot_general | solution.py:187
  57.7 1.0 fusion.53
  59.6 0.8 fusion.95
  60.4 16.1 %collective-permute-start.5 = (bf16[4,1,2048]{2,1,0:T(2,128)(2,1)S(1)}, bf16[4,1,2048]{2,1,0:T(2,128)(2,1)S(1)}, u32[]{:S(2)}, u32[]{:S(2)}) collective-permute-start(bf16[4,1,2048]{2,1,0:T(2,128)(2,1)S(1)} %slice.571), channel_id=1, source_target_pairs={{0,496},{16,0},{32,16},{48,32},{64,48},{80,64},{96,80},{112,96},{1... | collective-permute-start | bytes 49160 | tf_op jit(solution)/shard_map/ppermute | solution.py:54
  76.6 2.2 %collective-permute-start.4 = (bf16[1,4,2048]{2,1,0:T(4,128)(2,1)S(1)}, bf16[1,4,2048]{2,1,0:T(4,128)(2,1)S(1)}, u32[]{:S(2)}, u32[]{:S(2)}) collective-permute-start(bf16[1,4,2048]{2,1,0:T(4,128)(2,1)S(1)} %slice.569), channel_id=1, source_target_pairs={{0,15},{1,0},{2,1},{3,2},{4,3},{5,4},{6,5},{7,6},{8,7},{9,8},{10,9... | collective-permute-start | bytes 49160 | tf_op jit(solution)/shard_map/ppermute | solution.py:54
  80.5 1.4 %collective-permute-done.4 = bf16[1,4,2048]{2,1,0:T(4,128)(2,1)S(1)} collective-permute-done((bf16[1,4,2048]{2,1,0:T(4,128)(2,1)S(1)}, bf16[1,4,2048]{2,1,0:T(4,128)(2,1)S(1)}, u32[]{:S(2)}, u32[]{:S(2)}) %collective-permute-start.4) | collective-permute-done | bytes 16416 | tf_op jit(solution)/shard_map/ppermute | solution.py:54
  81.9 1.6 %fusion.93 = (f32[]{:T(128)}, f32[4,4,2048]{2,1,0:T(4,128)}, f32[4,4,2048]{2,1,0:T(4,128)}, f32[4,4,2048]{2,1,0:T(4,128)}) fusion(f32[4,4,2048]{2,1,0:T(4,128)S(1)} %get-tuple-element.8, f32[4,4,1]{2,1,0:T(4,128)S(1)} %slice.577, f32[4,4,2047]{2,1,0:T(4,128)S(1)} %slice.576, f32[4,4,1985]{2,1,0:T(4,128)S(1)} %bitcast.205, f32[4,4,63]{2,1,0:T(4,128)S(1)} %slice.574, ...), kind=kLoop, calls=%fused_computation.213 | loop fusion | flops 720895 | bytes 1198084 | tf_op jit(solution)/shard_map/reduce_sum | solution.py:220
  84.4 40.0 %all_to_all.6 = f32[512,1,2]{2,1,0:T(1,128)S(1)} all-to-all(f32[512,1,2]{2,1,0:T(1,128)S(1)} %broadcast_in_dim.74), channel_id=1, replica_groups=mesh['space'=32,'tm'=16] {'space','tm'}, dimensions={0} | all-to-all | bytes 8192 | tf_op jit(solution)/shard_map/all_to_all | solution.py:223
  (176 shorter events, 15.9 us)
Async XLA Ops:
  0.6 16.5 %copy-start = (bf16[256,768]{1,0:T(8,128)(2,1)S(1)}, bf16[256,768]{1,0:T(8,128)(2,1)}, u32[]{:S(2)}) copy-start(bf16[256,768]{1,0:T(8,128)(2,1)} %param.18) | copy-start | bytes 1179652
  3.0 13.9 %copy-start.12 = (s32[1,1,128]{2,1,0:T(1,128)S(1)}, s32[1,1,128]{2,1,0:T(1,128)}, u32[]{:S(2)}) copy-start(s32[1,1,128]{2,1,0:T(1,128)} %param.16) | copy-start | bytes 1540
  4.1 13.0 %copy-start.10 = (s32[128]{0:T(128)S(1)}, s32[128]{0:T(128)}, u32[]{:S(2)}) copy-start(s32[128]{0:T(128)} %constant.150) | copy-start | bytes 1540
  4.1 13.0 %copy-start.11 = (s32[128]{0:T(128)S(1)}, s32[128]{0:T(128)}, u32[]{:S(2)}) copy-start(s32[128]{0:T(128)} %constant.151) | copy-start | bytes 1540
  7.2 12.1 %copy-start.6 = (f32[768]{0:T(1024)S(1)}, f32[768]{0:T(1024)}, u32[]{:S(2)}) copy-start(f32[768]{0:T(1024)} %param.19) | copy-start | bytes 9220
  7.2 12.7 %collective-permute-start = (bf16[1,129,128]{2,1,0:T(8,128)(2,1)S(1)}, bf16[1,129,128]{2,1,0:T(8,128)(2,1)S(1)}, u32[]{:S(2)}, u32[]{:S(2)}) collective-permute-start(bf16[1,129,128]{2,1,0:T(8,128)(2,1)S(1)} %maximum_bitcast_fusion), channel_id=1, source_target_pairs={{0,8},{1,9},{2,10},{3,11},{4,12},{5,13},{6,14},{7,15},{8,0},{9,1},... | collective-permute-start | bytes 99080 | tf_op jit(solution)/shard_map/ppermute | solution.py:26
  17.1 2.5 %copy-start.8 = (s32[16,8]{0,1:T(8,128)S(1)}, s32[16,8]{0,1:T(8,128)}, u32[]{:S(2)}) copy-start(s32[16,8]{0,1:T(8,128)} %param.17) | copy-start | bytes 1540
  18.0 12.0 %copy-start.3 = (bf16[768,512]{1,0:T(8,128)(2,1)S(1)}, bf16[768,512]{1,0:T(8,128)(2,1)}, u32[]{:S(2)}) copy-start(bf16[768,512]{1,0:T(8,128)(2,1)} %param.23) | copy-start | bytes 2359300
  18.1 12.3 %copy-start.9 = (f32[512]{0:T(512)S(1)}, f32[512]{0:T(512)}, u32[]{:S(2)}) copy-start(f32[512]{0:T(512)} %param.24) | copy-start | bytes 6148
  18.1 12.5 %copy-start.1 = (s32[16]{0:T(128)S(1)}, s32[16]{0:T(128)}, u32[]{:S(2)}) copy-start(s32[16]{0:T(128)} %constant.145.clone) | copy-start | bytes 196
  19.0 21.4 %copy-start.7 = (f32[768]{0:T(1024)S(1)}, f32[768]{0:T(1024)}, u32[]{:S(2)}) copy-start(f32[768]{0:T(1024)} %param.20) | copy-start | bytes 9220
  19.9 6.6 %collective-permute-start.1 = (bf16[2,129,128]{2,1,0:T(8,128)(2,1)S(1)}, bf16[2,129,128]{2,1,0:T(8,128)(2,1)S(1)}, u32[]{:S(2)}, u32[]{:S(2)}) collective-permute-start(bf16[2,129,128]{2,1,0:T(8,128)(2,1)S(1)} %pad_maximum_fusion.4), channel_id=1, source_target_pairs={{0,4},{1,5},{2,6},{3,7},{4,0},{5,1},{6,2},{7,3},{8,12},{9,13},{10,... | collective-permute-start | bytes 198152 | tf_op jit(solution)/shard_map/ppermute | solution.py:26
  26.5 6.0 %collective-permute-start.2 = (bf16[4,129,128]{2,1,0:T(8,128)(2,1)S(1)}, bf16[4,129,128]{2,1,0:T(8,128)(2,1)S(1)}, u32[]{:S(2)}, u32[]{:S(2)}) collective-permute-start(bf16[4,129,128]{2,1,0:T(8,128)(2,1)S(1)} %pad_maximum_fusion.1), channel_id=1, source_target_pairs={{0,2},{1,3},{2,0},{3,1},{4,6},{5,7},{6,4},{7,5},{8,10},{9,11},{10,... | collective-permute-start | bytes 396296 | tf_op jit(solution)/shard_map/ppermute | solution.py:26
  32.5 9.8 %collective-permute-start.3 = (bf16[8,129,128]{2,1,0:T(8,128)(2,1)S(1)}, bf16[8,129,128]{2,1,0:T(8,128)(2,1)S(1)}, u32[]{:S(2)}, u32[]{:S(2)}) collective-permute-start(bf16[8,129,128]{2,1,0:T(8,128)(2,1)S(1)} %pad_maximum_fusion), channel_id=1, source_target_pairs={{0,1},{1,0},{2,3},{3,2},{4,5},{5,4},{6,7},{7,6},{8,9},{9,8},{10,11... | collective-permute-start | bytes 792584 | tf_op jit(solution)/shard_map/ppermute | solution.py:26
  43.9 2.0 %copy-start.5 = (bf16[768,2304]{1,0:T(8,128)(2,1)S(1)}, bf16[768,2304]{1,0:T(8,128)(2,1)}, u32[]{:S(2)}) copy-start(bf16[768,2304]{1,0:T(8,128)(2,1)} %param.21) | copy-start | bytes 10616836
  51.9 2.3 %copy-start.13 = (f32[768]{0:T(1024)S(1)}, f32[768]{0:T(1024)}, u32[]{:S(2)}) copy-start(f32[768]{0:T(1024)} %param.22) | copy-start | bytes 9220
  57.2 2.4 %copy-start.4 = (f32[4,4,2048]{2,1,0:T(4,128)S(1)}, f32[4,4,2048]{2,1,0:T(4,128)}, u32[]{:S(2)}) copy-start(f32[4,4,2048]{2,1,0:T(4,128)} %param.15) | copy-start | bytes 393220
  60.4 67.1 %copy-start.2 = (f32[4,4,2048]{2,1,0:T(4,128)}, f32[4,4,2048]{2,1,0:T(4,128)S(1)}, u32[]{:S(2)}) copy-start(f32[4,4,2048]{2,1,0:T(4,128)S(1)} %get-tuple-element.8) | copy-start | bytes 393220
  60.4 20.1 %collective-permute-start.5 = (bf16[4,1,2048]{2,1,0:T(2,128)(2,1)S(1)}, bf16[4,1,2048]{2,1,0:T(2,128)(2,1)S(1)}, u32[]{:S(2)}, u32[]{:S(2)}) collective-permute-start(bf16[4,1,2048]{2,1,0:T(2,128)(2,1)S(1)} %slice.571), channel_id=1, source_target_pairs={{0,496},{16,0},{32,16},{48,32},{64,48},{80,64},{96,80},{112,96},{1... | collective-permute-start | bytes 49160 | tf_op jit(solution)/shard_map/ppermute | solution.py:54
  76.6 5.4 %collective-permute-start.4 = (bf16[1,4,2048]{2,1,0:T(4,128)(2,1)S(1)}, bf16[1,4,2048]{2,1,0:T(4,128)(2,1)S(1)}, u32[]{:S(2)}, u32[]{:S(2)}) collective-permute-start(bf16[1,4,2048]{2,1,0:T(4,128)(2,1)S(1)} %slice.569), channel_id=1, source_target_pairs={{0,15},{1,0},{2,1},{3,2},{4,3},{5,4},{6,5},{7,6},{8,7},{9,8},{10,9... | collective-permute-start | bytes 49160 | tf_op jit(solution)/shard_map/ppermute | solution.py:54

commit v11 on v10

--- a/solution.py
+++ b/solution.py
@@ -197,8 +197,12 @@
     log_det = jnp.sum(jnp.where(frozen, 0.0, scale_lat))
     new_field = jnp.where(frozen, u, u * jnp.exp(scale_lat) + shift_lat)
 
-    ahead_time = shifted(new_field[0:1].astype(jnp.bfloat16), "tm", -1).astype(jnp.float32)
-    ahead_slab = shifted(new_field[:, 0:1].astype(jnp.bfloat16), "space", -1).astype(jnp.float32)
+    ahead_time = shifted(new_field[0:1].astype(jnp.bfloat16), "tm", -1)
+    slab_plane, ahead_time = lax.optimization_barrier(
+        (new_field[:, 0:1].astype(jnp.bfloat16), ahead_time)
+    )
+    ahead_time = ahead_time.astype(jnp.float32)
+    ahead_slab = shifted(slab_plane, "space", -1).astype(jnp.float32)
     next_time_field = jnp.concatenate([new_field[1:], ahead_time], axis=0)
     next_slab_field = jnp.concatenate([new_field[:, 1:], ahead_slab], axis=1)
     next_y_field = jnp.roll(new_field, -LZ, axis=2)

time: 128 us -> 135 us (1.055)
  blocking collectives: 40 us -> 45.7 us
  waiting for transfers between devices: 4.3 us -> 6 us
    all_to_all x1, blocking collectives: 40 us -> 45.7 us  [shards(): lax.all_to_all(partials, ('space', 'tm'), 0, 0, tiled=True)]
    ppermute x2, waiting for transfers between devices: 1.39 us -> 3.1 us  [shifted(): lax.ppermute(x, axis, [(i, (i + by) % length) for i in range(length)])]
where the time goes in v11:
time: 135 us
  blocking collectives  45.7 us (34%)
  starting transfers between devices  43.9 us (33%)
  other arithmetic  13.9 us (10%)
  matrix products  11.8 us (9%)
  local copies, waits for them, and re-layouts  9.25 us (7%)
  waiting for transfers between devices  6 us (4%)
  between operations  4.08 us (3%)
    all_to_all x1, blocking collectives, shards(): lax.all_to_all(partials, ('space', 'tm'), 0, 0, tiled=True)  45.7 us
    ppermute x4, starting transfers between devices, exchange(): return lax.ppermute(x, axis, [(i, i ^ bit) for i in range(length)])  25.9 us
    ppermute x2, starting transfers between devices, shifted(): lax.ppermute(x, axis, [(i, (i + by) % length) for i in range(length)])  18 us
    unnamed x2, matrix products  4.96 us
    ppermute x2, waiting for transfers between devices, shifted(): lax.ppermute(x, axis, [(i, (i + by) % length) for i in range(length)])  3.1 us
    ppermute x4, waiting for transfers between devices, exchange(): return lax.ppermute(x, axis, [(i, i ^ bit) for i in range(length)])  2.9 us
  transfers between devices with their start and end apart: 6, of which 3 were waited for; matrix products, arithmetic and copies ran while one was open for 5% of the time, Pallas kernels for 0%

profile of v11, /device:TPU:1, one launch (start us, length us, event | category | flops | bytes accessed | tf_op | source)
XLA Modules:
  0.0 134.6 jit_solution(14363440954562405227)
XLA Ops:
  1.2 1.4 %convert_bitcast_fusion.1 = (bf16[1,128]{1,0:T(2,128)(2,1)S(1)}, s32[128]{0:T(128)S(1)}) fusion(s32[1,1,128]{2,1,0:T(1,128)} %param.16, s32[]{:T(128)} %broadcast.282), kind=kLoop, calls=%fused_computation.205 | loop fusion | flops 128 | bytes 1284 | tf_op jit(solution)/shard_map/convert_element_type | solution.py:120
  3.0 1.1 select_convert_fusion
  7.2 9.6 %collective-permute-start = (bf16[1,129,128]{2,1,0:T(8,128)(2,1)S(1)}, bf16[1,129,128]{2,1,0:T(8,128)(2,1)S(1)}, u32[]{:S(2)}, u32[]{:S(2)}) collective-permute-start(bf16[1,129,128]{2,1,0:T(8,128)(2,1)S(1)} %maximum_bitcast_fusion), channel_id=1, source_target_pairs={{0,8},{1,9},{2,10},{3,11},{4,12},{5,13},{6,14},{7,15},{8,0},{9,1},... | collective-permute-start | bytes 99080 | tf_op jit(solution)/shard_map/ppermute | solution.py:26
  17.2 0.9 gather_fusion
  18.1 0.9 gather_fusion.1
  19.9 4.9 %collective-permute-start.1 = (bf16[2,129,128]{2,1,0:T(8,128)(2,1)S(1)}, bf16[2,129,128]{2,1,0:T(8,128)(2,1)S(1)}, u32[]{:S(2)}, u32[]{:S(2)}) collective-permute-start(bf16[2,129,128]{2,1,0:T(8,128)(2,1)S(1)} %pad_maximum_fusion.4), channel_id=1, source_target_pairs={{0,4},{1,5},{2,6},{3,7},{4,0},{5,1},{6,2},{7,3},{8,12},{9,13},{10,... | collective-permute-start | bytes 198152 | tf_op jit(solution)/shard_map/ppermute | solution.py:26
  24.8 1.7 %collective-permute-done.1 = bf16[2,129,128]{2,1,0:T(8,128)(2,1)S(1)} collective-permute-done((bf16[2,129,128]{2,1,0:T(8,128)(2,1)S(1)}, bf16[2,129,128]{2,1,0:T(8,128)(2,1)S(1)}, u32[]{:S(2)}, u32[]{:S(2)}) %collective-permute-start.1) | collective-permute-done | bytes 66080 | tf_op jit(solution)/shard_map/ppermute | solution.py:26
  26.5 3.5 %collective-permute-start.2 = (bf16[4,129,128]{2,1,0:T(8,128)(2,1)S(1)}, bf16[4,129,128]{2,1,0:T(8,128)(2,1)S(1)}, u32[]{:S(2)}, u32[]{:S(2)}) collective-permute-start(bf16[4,129,128]{2,1,0:T(8,128)(2,1)S(1)} %pad_maximum_fusion.1), channel_id=1, source_target_pairs={{0,2},{1,3},{2,0},{3,1},{4,6},{5,7},{6,4},{7,5},{8,10},{9,11},{10,... | collective-permute-start | bytes 396296 | tf_op jit(solution)/shard_map/ppermute | solution.py:26
  31.3 1.2 collective-permute-done.2
  32.5 7.8 %collective-permute-start.3 = (bf16[8,129,128]{2,1,0:T(8,128)(2,1)S(1)}, bf16[8,129,128]{2,1,0:T(8,128)(2,1)S(1)}, u32[]{:S(2)}, u32[]{:S(2)}) collective-permute-start(bf16[8,129,128]{2,1,0:T(8,128)(2,1)S(1)} %pad_maximum_fusion), channel_id=1, source_target_pairs={{0,1},{1,0},{2,3},{3,2},{4,5},{5,4},{6,7},{7,6},{8,9},{9,8},{10,11... | collective-permute-start | bytes 792584 | tf_op jit(solution)/shard_map/ppermute | solution.py:26
  40.4 1.9 %fusion.22 = f32[128,768]{0,1:S(1)} fusion(bf16[768,2304]{1,0:T(8,128)(2,1)} %param.21, f32[128,768]{1,0:T(8,128)S(1)} %get-tuple-element.16, f32[768]{0:T(1024)S(1)} %copy-done.7, f32[128]{0:T(128)S(1)} %add_rsqrt_fusion.2, f32[128]{0:T(128)S(1)} %broadcast_multiply_fusion.2), kind=kOutput, calls=%fused_computation.32 | convolution fusion | flops 151388160 | bytes 1970176
  42.9 1.0 fusion.103
  45.9 3.0 %fusion.12 = f32[1024,1536]{0,1:S(1)} fusion(bf16[768,2304]{1,0:T(8,128)(2,1)S(1)} %copy-done.5, f32[1024,768]{1,0:T(8,128)S(1)} %get-tuple-element.18, f32[768]{0:T(1024)S(1)} %copy-done.7, f32[1024]{0:T(1024)S(1)} %add_rsqrt_fusion, f32[1024]{0:T(1024)S(1)} %broadcast_multiply_fusion), kind=kOutput, calls=%fused_computation.21 | convolution fusion | flops 2419064832 | bytes 11808768
  49.5 1.1 multiply_reduce_fusion
  50.6 1.3 fusion
  51.9 1.8 %fusion.25 = f32[128,12,64]{0,2,1:T(8,128)S(1)} fusion(f32[12,128,1024]{2,1,0:T(8,128)S(1)} %get-tuple-element.48, f32[12,128]{1,0:T(8,128)S(1)} %get-tuple-element.47, bf16[2,12,1024,64]{2,3,1,0:T(8,128)(2,1)S(1)} %convert_bitcast_fusion, f32[128,12]{0,1:T(8,128)S(1)} %bitcast.221), kind=kOutput, calls=%fused_computation.38 | convolution fusion | flops 206143488 | bytes 8273920 | tf_op jit(solution)/shard_map/hqk,hkd->qhd/dot_general | solution.py:168
  54.7 1.3 fusion.7
  57.7 1.0 fusion.53
  59.6 0.8 fusion.95
  60.4 1.9 %collective-permute-start.4 = (bf16[1,4,2048]{2,1,0:T(4,128)(2,1)S(1)}, bf16[1,4,2048]{2,1,0:T(4,128)(2,1)S(1)}, u32[]{:S(2)}, u32[]{:S(2)}) collective-permute-start(bf16[1,4,2048]{2,1,0:T(4,128)(2,1)S(1)} %slice.570), channel_id=1, source_target_pairs={{0,15},{1,0},{2,1},{3,2},{4,3},{5,4},{6,5},{7,6},{8,7},{9,8},{10,9... | collective-permute-start | bytes 49160 | tf_op jit(solution)/shard_map/ppermute | solution.py:54
  62.4 3.1 %collective-permute-done.4 = bf16[1,4,2048]{2,1,0:T(4,128)(2,1)S(1)} collective-permute-done((bf16[1,4,2048]{2,1,0:T(4,128)(2,1)S(1)}, bf16[1,4,2048]{2,1,0:T(4,128)(2,1)S(1)}, u32[]{:S(2)}, u32[]{:S(2)}) %collective-permute-start.4) | collective-permute-done | bytes 16416 | tf_op jit(solution)/shard_map/ppermute | solution.py:54
  65.5 16.1 %collective-permute-start.5 = (bf16[4,1,2048]{2,1,0:T(2,128)(2,1)S(1)}, bf16[4,1,2048]{2,1,0:T(2,128)(2,1)S(1)}, u32[]{:S(2)}, u32[]{:S(2)}) collective-permute-start(bf16[4,1,2048]{2,1,0:T(2,128)(2,1)S(1)} %slice.569), channel_id=1, source_target_pairs={{0,496},{16,0},{32,16},{48,32},{64,48},{80,64},{96,80},{112,96},{1... | collective-permute-start | bytes 49160 | tf_op jit(solution)/shard_map/ppermute | solution.py:54
  83.4 1.6 %fusion.93 = (f32[]{:T(128)}, f32[4,4,2048]{2,1,0:T(4,128)}, f32[4,4,2048]{2,1,0:T(4,128)}, f32[4,4,2048]{2,1,0:T(4,128)}) fusion(f32[4,4,2048]{2,1,0:T(4,128)S(1)} %get-tuple-element.12, f32[4,4,1]{2,1,0:T(4,128)S(1)} %slice.577, f32[4,4,2047]{2,1,0:T(4,128)S(1)} %slice.576, f32[4,4,1985]{2,1,0:T(4,128)S(1)} %bitcast.205, f32[4,4,63]{2,1,0:T(4,128)S(1)} %slice.574, ...), kind=kLoop, calls=%fused_computation.213 | loop fusion | flops 720895 | bytes 1198084 | tf_op jit(solution)/shard_map/reduce_sum | solution.py:224
  85.8 45.7 %all_to_all.6 = f32[512,1,2]{2,1,0:T(1,128)S(1)} all-to-all(f32[512,1,2]{2,1,0:T(1,128)S(1)} %broadcast_in_dim.74), channel_id=1, replica_groups=mesh['space'=32,'tm'=16] {'space','tm'}, dimensions={0} | all-to-all | bytes 8192 | tf_op jit(solution)/shard_map/all_to_all | solution.py:227
  (176 shorter events, 15.9 us)
Async XLA Ops:
  0.6 16.5 %copy-start = (bf16[256,768]{1,0:T(8,128)(2,1)S(1)}, bf16[256,768]{1,0:T(8,128)(2,1)}, u32[]{:S(2)}) copy-start(bf16[256,768]{1,0:T(8,128)(2,1)} %param.18) | copy-start | bytes 1179652
  3.0 13.9 %copy-start.12 = (s32[1,1,128]{2,1,0:T(1,128)S(1)}, s32[1,1,128]{2,1,0:T(1,128)}, u32[]{:S(2)}) copy-start(s32[1,1,128]{2,1,0:T(1,128)} %param.16) | copy-start | bytes 1540
  4.1 13.0 %copy-start.10 = (s32[128]{0:T(128)S(1)}, s32[128]{0:T(128)}, u32[]{:S(2)}) copy-start(s32[128]{0:T(128)} %constant.150) | copy-start | bytes 1540
  4.1 13.0 %copy-start.11 = (s32[128]{0:T(128)S(1)}, s32[128]{0:T(128)}, u32[]{:S(2)}) copy-start(s32[128]{0:T(128)} %constant.151) | copy-start | bytes 1540
  7.2 12.1 %copy-start.6 = (f32[768]{0:T(1024)S(1)}, f32[768]{0:T(1024)}, u32[]{:S(2)}) copy-start(f32[768]{0:T(1024)} %param.19) | copy-start | bytes 9220
  7.2 12.7 %collective-permute-start = (bf16[1,129,128]{2,1,0:T(8,128)(2,1)S(1)}, bf16[1,129,128]{2,1,0:T(8,128)(2,1)S(1)}, u32[]{:S(2)}, u32[]{:S(2)}) collective-permute-start(bf16[1,129,128]{2,1,0:T(8,128)(2,1)S(1)} %maximum_bitcast_fusion), channel_id=1, source_target_pairs={{0,8},{1,9},{2,10},{3,11},{4,12},{5,13},{6,14},{7,15},{8,0},{9,1},... | collective-permute-start | bytes 99080 | tf_op jit(solution)/shard_map/ppermute | solution.py:26
  17.1 2.5 %copy-start.8 = (s32[16,8]{0,1:T(8,128)S(1)}, s32[16,8]{0,1:T(8,128)}, u32[]{:S(2)}) copy-start(s32[16,8]{0,1:T(8,128)} %param.17) | copy-start | bytes 1540
  18.0 12.0 %copy-start.3 = (bf16[768,512]{1,0:T(8,128)(2,1)S(1)}, bf16[768,512]{1,0:T(8,128)(2,1)}, u32[]{:S(2)}) copy-start(bf16[768,512]{1,0:T(8,128)(2,1)} %param.23) | copy-start | bytes 2359300
  18.1 12.3 %copy-start.9 = (f32[512]{0:T(512)S(1)}, f32[512]{0:T(512)}, u32[]{:S(2)}) copy-start(f32[512]{0:T(512)} %param.24) | copy-start | bytes 6148
  18.1 12.5 %copy-start.1 = (s32[16]{0:T(128)S(1)}, s32[16]{0:T(128)}, u32[]{:S(2)}) copy-start(s32[16]{0:T(128)} %constant.145.clone) | copy-start | bytes 196
  19.0 21.4 %copy-start.7 = (f32[768]{0:T(1024)S(1)}, f32[768]{0:T(1024)}, u32[]{:S(2)}) copy-start(f32[768]{0:T(1024)} %param.20) | copy-start | bytes 9220
  19.9 6.6 %collective-permute-start.1 = (bf16[2,129,128]{2,1,0:T(8,128)(2,1)S(1)}, bf16[2,129,128]{2,1,0:T(8,128)(2,1)S(1)}, u32[]{:S(2)}, u32[]{:S(2)}) collective-permute-start(bf16[2,129,128]{2,1,0:T(8,128)(2,1)S(1)} %pad_maximum_fusion.4), channel_id=1, source_target_pairs={{0,4},{1,5},{2,6},{3,7},{4,0},{5,1},{6,2},{7,3},{8,12},{9,13},{10,... | collective-permute-start | bytes 198152 | tf_op jit(solution)/shard_map/ppermute | solution.py:26
  26.5 6.0 %collective-permute-start.2 = (bf16[4,129,128]{2,1,0:T(8,128)(2,1)S(1)}, bf16[4,129,128]{2,1,0:T(8,128)(2,1)S(1)}, u32[]{:S(2)}, u32[]{:S(2)}) collective-permute-start(bf16[4,129,128]{2,1,0:T(8,128)(2,1)S(1)} %pad_maximum_fusion.1), channel_id=1, source_target_pairs={{0,2},{1,3},{2,0},{3,1},{4,6},{5,7},{6,4},{7,5},{8,10},{9,11},{10,... | collective-permute-start | bytes 396296 | tf_op jit(solution)/shard_map/ppermute | solution.py:26
  32.5 9.8 %collective-permute-start.3 = (bf16[8,129,128]{2,1,0:T(8,128)(2,1)S(1)}, bf16[8,129,128]{2,1,0:T(8,128)(2,1)S(1)}, u32[]{:S(2)}, u32[]{:S(2)}) collective-permute-start(bf16[8,129,128]{2,1,0:T(8,128)(2,1)S(1)} %pad_maximum_fusion), channel_id=1, source_target_pairs={{0,1},{1,0},{2,3},{3,2},{4,5},{5,4},{6,7},{7,6},{8,9},{9,8},{10,11... | collective-permute-start | bytes 792584 | tf_op jit(solution)/shard_map/ppermute | solution.py:26
  43.9 2.0 %copy-start.5 = (bf16[768,2304]{1,0:T(8,128)(2,1)S(1)}, bf16[768,2304]{1,0:T(8,128)(2,1)}, u32[]{:S(2)}) copy-start(bf16[768,2304]{1,0:T(8,128)(2,1)} %param.21) | copy-start | bytes 10616836
  51.9 2.3 %copy-start.13 = (f32[768]{0:T(1024)S(1)}, f32[768]{0:T(1024)}, u32[]{:S(2)}) copy-start(f32[768]{0:T(1024)} %param.22) | copy-start | bytes 9220
  57.2 2.4 %copy-start.4 = (f32[4,4,2048]{2,1,0:T(4,128)S(1)}, f32[4,4,2048]{2,1,0:T(4,128)}, u32[]{:S(2)}) copy-start(f32[4,4,2048]{2,1,0:T(4,128)} %param.15) | copy-start | bytes 393220
  60.4 74.3 %copy-start.2 = (f32[4,4,2048]{2,1,0:T(4,128)}, f32[4,4,2048]{2,1,0:T(4,128)S(1)}, u32[]{:S(2)}) copy-start(f32[4,4,2048]{2,1,0:T(4,128)S(1)} %get-tuple-element.12) | copy-start | bytes 393220
  60.4 5.1 %collective-permute-start.4 = (bf16[1,4,2048]{2,1,0:T(4,128)(2,1)S(1)}, bf16[1,4,2048]{2,1,0:T(4,128)(2,1)S(1)}, u32[]{:S(2)}, u32[]{:S(2)}) collective-permute-start(bf16[1,4,2048]{2,1,0:T(4,128)(2,1)S(1)} %slice.570), channel_id=1, source_target_pairs={{0,15},{1,0},{2,1},{3,2},{4,3},{5,4},{6,5},{7,6},{8,7},{9,8},{10,9... | collective-permute-start | bytes 49160 | tf_op jit(solution)/shard_map/ppermute | solution.py:54
  65.5 17.9 %collective-permute-start.5 = (bf16[4,1,2048]{2,1,0:T(2,128)(2,1)S(1)}, bf16[4,1,2048]{2,1,0:T(2,128)(2,1)S(1)}, u32[]{:S(2)}, u32[]{:S(2)}) collective-permute-start(bf16[4,1,2048]{2,1,0:T(2,128)(2,1)S(1)} %slice.569), channel_id=1, source_target_pairs={{0,496},{16,0},{32,16},{48,32},{64,48},{80,64},{96,80},{112,96},{1... | collective-permute-start | bytes 49160 | tf_op jit(solution)/shard_map/ppermute | solution.py:54

commit v12 on v10

--- a/solution.py
+++ b/solution.py
@@ -58,6 +58,12 @@
     centre = values - jnp.mean(values, axis=-1, keepdims=True)
     spread = jnp.mean(centre * centre, axis=-1, keepdims=True)
     return centre * lax.rsqrt(spread + epsilon) * gain_vec
+
+
+def layer_norm_heads(values, gain_vec):
+    centre = values - jnp.mean(values, axis=(0, 2), keepdims=True)
+    spread = jnp.mean(centre * centre, axis=(0, 2), keepdims=True)
+    return centre * lax.rsqrt(spread + epsilon) * gain_vec.reshape(HEADS, 1, HS)
 
 
 def site_parity(patch_side):
@@ -126,8 +132,14 @@
         [w_embed[packed_rows(0)], w_embed[packed_rows(1)]], axis=1
     )
     bits_own = bits.reshape(tokens_dev).astype(jnp.float32)
-    embedded = embed_packed(tokens, bits_own, w_pair, b_embed)
-    normed = layer_norm(embedded, gain_in).astype(jnp.bfloat16)
+    both_h = jnp.einsum(
+        "tf,fshd->shtd", tokens, w_pair.reshape(patch_len // 2, 2, HEADS, HS),
+        preferred_element_type=jnp.float32,
+    )
+    embedded_h = jnp.where(bits_own[None, :, None] > 0.5, both_h[1], both_h[0]) + b_embed.reshape(
+        HEADS, 1, HS
+    )
+    normed_h = layer_norm_heads(embedded_h, gain_in).astype(jnp.bfloat16)
 
     block_rows = lax.dynamic_index_in_dim(block_list, lax.axis_index("tm"), 0, keepdims=False)
     own = lax.axis_index("tm")
@@ -146,7 +158,7 @@
     sel_embedded = embed_packed(sel_tokens, sel_bits, w_pair, b_embed)
     sel_normed = layer_norm(sel_embedded, gain_in).astype(jnp.bfloat16)
     queries = jnp.einsum(
-        "tc,chd->htd", normed, w_qkv[:, :D].reshape(D, HEADS, HS),
+        "gte,gehd->htd", normed_h, w_qkv[:, :D].reshape(HEADS, HS, HEADS, HS),
         preferred_element_type=jnp.float32,
     ).astype(jnp.bfloat16)
     w_kv = w_qkv[:, D:].reshape(D, 2, HEADS, HS)
@@ -166,17 +178,16 @@
     exp_scores = jnp.exp(scores - row_top)
     row_total = jnp.sum(exp_scores, axis=-1)
     product = jnp.einsum(
-        "hqk,hkd->qhd",
+        "hqk,hkd->hqd",
         exp_scores.astype(jnp.bfloat16),
         values,
         preferred_element_type=jnp.float32,
     )
-    mixed = (product / row_total.T[:, :, None]).reshape(tokens_dev, D)
-    hidden = embedded + mixed
-    normed_out = layer_norm(hidden, gain_out).astype(jnp.bfloat16)
-    w_rows = w_head.reshape(D, 2 * P_SIZE * P_SIZE, n_off)
+    hidden_h = embedded_h + product / row_total[:, :, None]
+    normed_out_h = layer_norm_heads(hidden_h, gain_out).astype(jnp.bfloat16)
+    w_rows = w_head.reshape(HEADS, HS, 2 * P_SIZE * P_SIZE, n_off)
     affine_rows = jnp.einsum(
-        "tc,crk->krt", normed_out, w_rows, preferred_element_type=jnp.float32
+        "htd,hdrk->krt", normed_out_h, w_rows, preferred_element_type=jnp.float32
     ) + b_head.reshape(2 * P_SIZE * P_SIZE, n_off).T[:, :, None]
     high = lax.reduce_precision(affine_rows, exponent_bits=8, mantissa_bits=7)
     rest = affine_rows - high

time: 128 us -> 164 us (1.28)
  local copies, waits for them, and re-layouts: 9.25 us -> 29.2 us
  other arithmetic: 13.9 us -> 23.1 us
  matrix products: 11.8 us -> 20.6 us
    reshape x1 -> x2, local copies, waits for them, and re-layouts: 0.16 us -> 7.14 us  [the longest x1 3.75 us: shards(): w_rows = w_head.reshape(HEADS, HS, 2 * P_SIZE * P_SIZE, n_off)]
    dot_general x1, matrix products: 1.11 us -> 6.9 us  [shards(): jnp.einsum('hqd,hkd->hqk', queries, keys, preferred_element_type=jnp.floa...]
    dot_general x2 -> x3, matrix products: 2.29 us -> 5.5 us  [the longest x1 2.98 us: shards(): jnp.einsum('hqk,hkd->hqd', exp_scores.astype(jnp.bfloat16), values, prefe...]
    unnamed x32 -> x72, local copies, waits for them, and re-layouts: 1.64 us -> 4.76 us
    reduce_sum x1, other arithmetic: 1.3 us -> 4.16 us  [shards(): row_total = jnp.sum(exp_scores, axis=-1)]
    mul x0 -> x2, local copies, waits for them, and re-layouts: none -> 2.71 us  [layer_norm_heads(): return centre * lax.rsqrt(spread + epsilon) * gain_vec.reshape(HEADS, 1, HS)]
    slice x0 -> x1, local copies, waits for them, and re-layouts: none -> 2.37 us  [shards(): w_qkv[:, :D].reshape(HEADS, HS, HEADS, HS)]
    unnamed x2 -> x1, matrix products: 4.96 us -> 3.04 us
  transfers between devices with their start and end apart: 6 -> 6, of which waited for: 3 -> 3; matrix products, arithmetic and copies ran while one was open for 5% -> 17% of each run, Pallas kernels for 0% -> 0%
where the time goes in v12:
time: 164 us; the launch traced here: 163 us
  starting transfers between devices  42.8 us (26%)
  blocking collectives  40 us (24%)
  local copies, waits for them, and re-layouts  29.2 us (18%)
  other arithmetic  23.1 us (14%)
  matrix products  20.6 us (13%)
  between operations  4.14 us (3%)
  waiting for transfers between devices  3.66 us (2%)
    all_to_all x1, blocking collectives, shards(): lax.all_to_all(partials, ('space', 'tm'), 0, 0, tiled=True)  40 us
    ppermute x4, starting transfers between devices, exchange(): return lax.ppermute(x, axis, [(i, i ^ bit) for i in range(length)])  24.9 us
    ppermute x2, starting transfers between devices, shifted(): lax.ppermute(x, axis, [(i, (i + by) % length) for i in range(length)])  17.9 us
    dot_general x1, matrix products, shards(): jnp.einsum('hqd,hkd->hqk', queries, keys, preferred_element_type=jnp.floa...  6.9 us
    unnamed x72, local copies, waits for them, and re-layouts  4.76 us
    reduce_sum x1, other arithmetic, shards(): row_total = jnp.sum(exp_scores, axis=-1)  4.16 us
    reshape x1, local copies, waits for them, and re-layouts, shards(): w_rows = w_head.reshape(HEADS, HS, 2 * P_SIZE * P_SIZE, n_off)  3.75 us
    reshape x1, local copies, waits for them, and re-layouts, shards(): w_qkv[:, :D].reshape(HEADS, HS, HEADS, HS)  3.39 us
  transfers between devices with their start and end apart: 6, of which 3 were waited for; matrix products, arithmetic and copies ran while one was open for 17% of the time, Pallas kernels for 0%

profile of v12, /device:TPU:1, one launch (start us, length us, event | category | flops | bytes accessed | tf_op | source)
XLA Modules:
  0.0 163.3 jit_solution(13707016548917388013)
XLA Ops:
  1.2 1.4 convert_bitcast_fusion.1
  7.3 9.6 %collective-permute-start = (bf16[1,129,128]{2,1,0:T(8,128)(2,1)S(1)}, bf16[1,129,128]{2,1,0:T(8,128)(2,1)S(1)}, u32[]{:S(2)}, u32[]{:S(2)}) collective-permute-start(bf16[1,129,128]{2,1,0:T(8,128)(2,1)S(1)} %maximum_bitcast_fusion), channel_id=1, source_target_pairs={{0,8},{1,9},{2,10},{3,11},{4,12},{5,13},{6,14},{7,15},{8,0},{9,1},... | collective-permute-start | bytes 99080 | tf_op jit(solution)/shard_map/ppermute | solution.py:26
  21.3 4.9 %collective-permute-start.1 = (bf16[2,129,128]{2,1,0:T(8,128)(2,1)S(1)}, bf16[2,129,128]{2,1,0:T(8,128)(2,1)S(1)}, u32[]{:S(2)}, u32[]{:S(2)}) collective-permute-start(bf16[2,129,128]{2,1,0:T(8,128)(2,1)S(1)} %pad_maximum_fusion.4), channel_id=1, source_target_pairs={{0,4},{1,5},{2,6},{3,7},{4,0},{5,1},{6,2},{7,3},{8,12},{9,13},{10,... | collective-permute-start | bytes 198152 | tf_op jit(solution)/shard_map/ppermute | solution.py:26
  27.9 3.6 %collective-permute-start.2 = (bf16[4,129,128]{2,1,0:T(8,128)(2,1)S(1)}, bf16[4,129,128]{2,1,0:T(8,128)(2,1)S(1)}, u32[]{:S(2)}, u32[]{:S(2)}) collective-permute-start(bf16[4,129,128]{2,1,0:T(8,128)(2,1)S(1)} %pad_maximum_fusion.1), channel_id=1, source_target_pairs={{0,2},{1,3},{2,0},{3,1},{4,6},{5,7},{6,4},{7,5},{8,10},{9,11},{10,... | collective-permute-start | bytes 396296 | tf_op jit(solution)/shard_map/ppermute | solution.py:26
  34.6 6.8 %collective-permute-start.3 = (bf16[8,129,128]{2,1,0:T(8,128)(2,1)}, bf16[8,129,128]{2,1,0:T(8,128)(2,1)}, u32[]{:S(2)}, u32[]{:S(2)}) collective-permute-start(bf16[8,129,128]{2,1,0:T(8,128)(2,1)} %pad_maximum_fusion), channel_id=1, source_target_pairs={{0,1},{1,0},{2,3},{3,2},{4,5},{5,4},{6,7},{7,6},{8,9},{9,8},{10,11... | collective-permute-start | bytes 792584 | tf_op jit(solution)/shard_map/ppermute | solution.py:26
  41.9 2.4 %slice.408 = bf16[768,768]{1,0:T(8,128)(2,1)} slice(bf16[768,2304]{1,0:T(8,128)(2,1)} %param.21), slice={[0:768], [0:768]} | slice | bytes 2359296 | tf_op jit(solution)/shard_map/slice | solution.py:161
  44.3 3.4 %reshape.176 = bf16[12,64,12,64]{3,2,1,0:T(8,128)(2,1)S(1)} reshape(bf16[768,768]{1,0:T(8,128)(2,1)} %slice.408) | data formatting | bytes 2359296 | tf_op jit(solution)/shard_map/reshape | solution.py:161
  47.7 1.4 mul.131
  49.1 2.3 %copy.74 = bf16[768,512]{0,1:T(8,128)(2,1)} copy(bf16[768,512]{1,0:T(8,128)(2,1)} %param.23) | data formatting | bytes 1572864 | tf_op args[8]
  51.4 3.8 %reshape.179 = bf16[12,64,32,16]{1,0,3,2:T(8,128)(2,1)} reshape(bf16[768,512]{0,1:T(8,128)(2,1)} %copy.74) | data formatting | bytes 1572864 | tf_op jit(solution)/shard_map/reshape | solution.py:188
  55.1 1.4 reshape.180
  56.5 1.4 copy.76
  57.9 1.4 mul.144
  68.8 3.0 %fusion.14 = f32[1024,1536]{0,1:S(1)} fusion(bf16[768,2304]{1,0:T(8,128)(2,1)S(1)} %copy-done.9, f32[1024,768]{1,0:T(8,128)S(1)} %get-tuple-element.12, f32[768]{0:T(1024)S(1)} %copy-done.26, f32[1024]{0:T(1024)S(1)} %add_rsqrt_fusion, f32[1024]{0:T(1024)S(1)} %broadcast_multiply_fusion), kind=kOutput, calls=%fused_computation.23 | convolution fusion | flops 2419064832 | bytes 11808768
  71.8 2.2 %convert_bitcast_fusion = bf16[2,12,1024,64]{2,3,1,0:T(8,128)(2,1)} fusion(f32[1024,2,12,64]{0,3,2,1:T(8,128)S(1)} %bitcast.240), kind=kLoop, calls=%fused_computation.12 | loop fusion | flops 1572864 | bytes 9437184 | tf_op jit(solution)/shard_map/convert_element_type | solution.py:167
  74.0 6.9 %multiply_reduce_fusion = (f32[12,128]{1,0:T(8,128)}, f32[12,128,1024]{2,1,0:T(8,128)}) fusion(bf16[2,12,1024,64]{2,3,1,0:T(8,128)(2,1)} %convert_bitcast_fusion, bf16[12,64,12,64]{3,2,1,0:T(8,128)(2,1)S(1)} %reshape.176, f32[12,128,64]{1,2,0:T(8,128)} %copy-done.4, f32[12,64]{1,0:T(8,128)} %mul.131, f32[128]{0:T(128)} %add_rsqrt_fusion.2, f32[128]{0:T(128)S(1)} %copy-done.29), kind=kOutput, calls=%fused_computation.4 | convolution fusion | flops 355957248 | bytes 9452544 | tf_op jit(solution)/shard_map/hqd,hkd->hqk/dot_general | solution.py:171
  80.9 4.2 %fusion = f32[12,128]{1,0:T(8,128)S(1)} fusion(f32[12,128,1024]{2,1,0:T(8,128)} %get-tuple-element.42, f32[12,128]{1,0:T(8,128)} %get-tuple-element.41), kind=kLoop, calls=%fused_computation.5 | loop fusion | flops 4717056 | bytes 6303744 | tf_op jit(solution)/shard_map/reduce_sum | solution.py:179
  85.6 3.0 %fusion.128 = (f32[128]{0:T(128)S(1)}, f32[12,128,64]{1,2,0:T(8,128)S(1)}) fusion(f32[12,128,64]{1,2,0:T(8,128)} %copy-done.4, f32[12,128]{1,0:T(8,128)S(1)} %fusion, bf16[2,12,1024,64]{2,3,1,0:T(8,128)(2,1)} %convert_bitcast_fusion, f32[12,128,1024]{2,1,0:T(8,128)S(1)} %copy-done.2, f32[12,128]{1,0:T(8,128)S(1)} %copy-done.21), kind=kOutput, calls=%fused_computation.225 | convolution fusion | flops 206339968 | bytes 8663552 | tf_op jit(solution)/shard_map/hqk,hkd->hqd/dot_general | solution.py:180
  88.7 2.3 %reduce-precision_convert_fusion.1 = (bf16[16,32,128]{2,1,0:T(8,128)(2,1)S(1)}, bf16[16,32,128]{2,1,0:T(8,128)(2,1)S(1)}, bf16[16,32,128]{2,1,0:T(8,128)(2,1)S(1)}) fusion(f32[16,32]{1,0:T(8,128)S(1)} %copy-done.24, bf16[12,64,32,16]{1,0,3,2:T(8,128)(2,1)S(1)} %copy-done.7, f32[12,128,64]{1,2,0:T(8,128)S(1)} %get-tuple-element.44, ...), kind=kOutput, calls=%fused_computation.61 | convolution fusion | flops 101580800 | bytes 1579008 | tf_op jit(solution)/shard_map/htd,hdrk->krt/dot_general | solution.py:189
  96.8 15.7 %collective-permute-start.5 = (bf16[4,1,2048]{2,1,0:T(2,128)(2,1)S(1)}, bf16[4,1,2048]{2,1,0:T(2,128)(2,1)S(1)}, u32[]{:S(2)}, u32[]{:S(2)}) collective-permute-start(bf16[4,1,2048]{2,1,0:T(2,128)(2,1)S(1)} %slice.571), channel_id=1, source_target_pairs={{0,496},{16,0},{32,16},{48,32},{64,48},{80,64},{96,80},{112,96},{1... | collective-permute-start | bytes 49160 | tf_op jit(solution)/shard_map/ppermute | solution.py:54
  112.5 2.2 %collective-permute-start.4 = (bf16[1,4,2048]{2,1,0:T(4,128)(2,1)S(1)}, bf16[1,4,2048]{2,1,0:T(4,128)(2,1)S(1)}, u32[]{:S(2)}, u32[]{:S(2)}) collective-permute-start(bf16[1,4,2048]{2,1,0:T(4,128)(2,1)S(1)} %slice.569), channel_id=1, source_target_pairs={{0,15},{1,0},{2,1},{3,2},{4,3},{5,4},{6,5},{7,6},{8,7},{9,8},{10,9... | collective-permute-start | bytes 49160 | tf_op jit(solution)/shard_map/ppermute | solution.py:54
  116.5 1.4 collective-permute-done.4
  117.9 1.6 fusion.116
  120.3 40.0 %all_to_all.6 = f32[512,1,2]{2,1,0:T(1,128)S(1)} all-to-all(f32[512,1,2]{2,1,0:T(1,128)S(1)} %broadcast_in_dim.71), channel_id=1, replica_groups=mesh['space'=32,'tm'=16] {'space','tm'}, dimensions={0} | all-to-all | bytes 8192 | tf_op jit(solution)/shard_map/all_to_all | solution.py:234
  (220 shorter events, 33.2 us)
Async XLA Ops:
  0.6 17.5 %copy-start = (bf16[256,768]{1,0:T(8,128)(2,1)S(1)}, bf16[256,768]{1,0:T(8,128)(2,1)}, u32[]{:S(2)}) copy-start(bf16[256,768]{1,0:T(8,128)(2,1)} %param.18) | copy-start | bytes 1179652
  0.7 6.6 %copy-start.15 = (s32[2048]{0:T(1024)}, s32[2048]{0:T(1024)S(1)}, u32[]{:S(2)}) copy-start(s32[2048]{0:T(1024)S(1)} %get-tuple-element.53) | copy-start | bytes 24580
  0.7 6.6 %copy-start.11 = (s32[2048]{0:T(1024)}, s32[2048]{0:T(1024)S(1)}, u32[]{:S(2)}) copy-start(s32[2048]{0:T(1024)S(1)} %get-tuple-element.55) | copy-start | bytes 24580
  0.7 6.6 %copy-start.17 = (s32[2048]{0:T(1024)}, s32[2048]{0:T(1024)S(1)}, u32[]{:S(2)}) copy-start(s32[2048]{0:T(1024)S(1)} %get-tuple-element.56) | copy-start | bytes 24580
  0.7 3.6 %copy-start.19 = (pred[2048]{0:T(1024)(128)(4,1)}, pred[2048]{0:T(1024)(128)(4,1)S(1)}, u32[]{:S(2)}) copy-start(pred[2048]{0:T(1024)(128)(4,1)S(1)} %get-tuple-element.58) | copy-start | bytes 6148
  3.0 4.3 %copy-start.13 = (s32[2048]{0:T(1024)}, s32[2048]{0:T(1024)S(1)}, u32[]{:S(2)}) copy-start(s32[2048]{0:T(1024)S(1)} %eq.60) | copy-start | bytes 24580
  3.0 13.9 %copy-start.33 = (s32[1,1,128]{2,1,0:T(1,128)S(1)}, s32[1,1,128]{2,1,0:T(1,128)}, u32[]{:S(2)}) copy-start(s32[1,1,128]{2,1,0:T(1,128)} %param.16) | copy-start | bytes 1540
  4.1 13.8 %copy-start.27 = (s32[16,8]{0,1:T(8,128)S(1)}, s32[16,8]{0,1:T(8,128)}, u32[]{:S(2)}) copy-start(s32[16,8]{0,1:T(8,128)} %param.17) | copy-start | bytes 1540
  4.1 14.0 %copy-start.31 = (s32[128]{0:T(128)S(1)}, s32[128]{0:T(128)}, u32[]{:S(2)}) copy-start(s32[128]{0:T(128)} %constant.150) | copy-start | bytes 1540
  4.1 14.0 %copy-start.32 = (s32[128]{0:T(128)S(1)}, s32[128]{0:T(128)}, u32[]{:S(2)}) copy-start(s32[128]{0:T(128)} %constant.151) | copy-start | bytes 1540
  7.3 14.0 %collective-permute-start = (bf16[1,129,128]{2,1,0:T(8,128)(2,1)S(1)}, bf16[1,129,128]{2,1,0:T(8,128)(2,1)S(1)}, u32[]{:S(2)}, u32[]{:S(2)}) collective-permute-start(bf16[1,129,128]{2,1,0:T(8,128)(2,1)S(1)} %maximum_bitcast_fusion), channel_id=1, source_target_pairs={{0,8},{1,9},{2,10},{3,11},{4,12},{5,13},{6,14},{7,15},{8,0},{9,1},... | collective-permute-start | bytes 99080 | tf_op jit(solution)/shard_map/ppermute | solution.py:26
  21.2 10.8 %copy-start.4 = (f32[12,128,64]{1,2,0:T(8,128)}, f32[12,128,64]{1,2,0:T(8,128)S(1)}, u32[]{:S(2)}) copy-start(f32[12,128,64]{1,2,0:T(8,128)S(1)} %get-tuple-element.10) | copy-start | bytes 1179652
  21.2 11.5 %copy-start.28 = (f32[128]{0:T(128)}, f32[128]{0:T(128)S(1)}, u32[]{:S(2)}) copy-start(f32[128]{0:T(128)S(1)} %broadcast_multiply_fusion.2) | copy-start | bytes 1540
  21.3 6.6 %collective-permute-start.1 = (bf16[2,129,128]{2,1,0:T(8,128)(2,1)S(1)}, bf16[2,129,128]{2,1,0:T(8,128)(2,1)S(1)}, u32[]{:S(2)}, u32[]{:S(2)}) collective-permute-start(bf16[2,129,128]{2,1,0:T(8,128)(2,1)S(1)} %pad_maximum_fusion.4), channel_id=1, source_target_pairs={{0,4},{1,5},{2,6},{3,7},{4,0},{5,1},{6,2},{7,3},{8,12},{9,13},{10,... | collective-permute-start | bytes 198152 | tf_op jit(solution)/shard_map/ppermute | solution.py:26
  27.9 6.0 %collective-permute-start.2 = (bf16[4,129,128]{2,1,0:T(8,128)(2,1)S(1)}, bf16[4,129,128]{2,1,0:T(8,128)(2,1)S(1)}, u32[]{:S(2)}, u32[]{:S(2)}) collective-permute-start(bf16[4,129,128]{2,1,0:T(8,128)(2,1)S(1)} %pad_maximum_fusion.1), channel_id=1, source_target_pairs={{0,2},{1,3},{2,0},{3,1},{4,6},{5,7},{6,4},{7,5},{8,10},{9,11},{10,... | collective-permute-start | bytes 396296 | tf_op jit(solution)/shard_map/ppermute | solution.py:26
  34.6 28.5 %collective-permute-start.3 = (bf16[8,129,128]{2,1,0:T(8,128)(2,1)}, bf16[8,129,128]{2,1,0:T(8,128)(2,1)}, u32[]{:S(2)}, u32[]{:S(2)}) collective-permute-start(bf16[8,129,128]{2,1,0:T(8,128)(2,1)} %pad_maximum_fusion), channel_id=1, source_target_pairs={{0,1},{1,0},{2,3},{3,2},{4,5},{5,4},{6,7},{7,6},{8,9},{9,8},{10,11... | collective-permute-start | bytes 792584 | tf_op jit(solution)/shard_map/ppermute | solution.py:26
  47.7 12.9 %copy-start.1 = (s32[16]{0:T(128)S(1)}, s32[16]{0:T(128)}, u32[]{:S(2)}) copy-start(s32[16]{0:T(128)} %constant.145.clone) | copy-start | bytes 196
  61.8 3.9 %copy-start.6 = (bf16[128,1536]{1,0:T(8,128)(2,1)S(1)}, bf16[128,1536]{1,0:T(8,128)(2,1)}, u32[]{:S(2)}) copy-start(bf16[128,1536]{1,0:T(8,128)(2,1)} %copy-done.5) | copy-start | bytes 1179652
  80.9 4.6 %copy-start.2 = (f32[12,128,1024]{2,1,0:T(8,128)S(1)}, f32[12,128,1024]{2,1,0:T(8,128)}, u32[]{:S(2)}) copy-start(f32[12,128,1024]{2,1,0:T(8,128)} %get-tuple-element.42) | copy-start | bytes 18874372
  80.9 4.6 %copy-start.21 = (f32[12,128]{1,0:T(8,128)S(1)}, f32[12,128]{1,0:T(8,128)}, u32[]{:S(2)}) copy-start(f32[12,128]{1,0:T(8,128)} %get-tuple-element.41) | copy-start | bytes 18436
  85.6 3.1 %copy-start.25 = (f32[12,64]{1,0:T(8,128)S(1)}, f32[12,64]{1,0:T(8,128)}, u32[]{:S(2)}) copy-start(f32[12,64]{1,0:T(8,128)} %mul.144) | copy-start | bytes 9220
  96.7 66.6 %copy-start.3 = (f32[4,4,2048]{2,1,0:T(4,128)}, f32[4,4,2048]{2,1,0:T(4,128)S(1)}, u32[]{:S(2)}) copy-start(f32[4,4,2048]{2,1,0:T(4,128)S(1)} %get-tuple-element.8) | copy-start | bytes 393220
  96.8 19.6 %collective-permute-start.5 = (bf16[4,1,2048]{2,1,0:T(2,128)(2,1)S(1)}, bf16[4,1,2048]{2,1,0:T(2,128)(2,1)S(1)}, u32[]{:S(2)}, u32[]{:S(2)}) collective-permute-start(bf16[4,1,2048]{2,1,0:T(2,128)(2,1)S(1)} %slice.571), channel_id=1, source_target_pairs={{0,496},{16,0},{32,16},{48,32},{64,48},{80,64},{96,80},{112,96},{1... | collective-permute-start | bytes 49160 | tf_op jit(solution)/shard_map/ppermute | solution.py:54
  112.5 5.4 %collective-permute-start.4 = (bf16[1,4,2048]{2,1,0:T(4,128)(2,1)S(1)}, bf16[1,4,2048]{2,1,0:T(4,128)(2,1)S(1)}, u32[]{:S(2)}, u32[]{:S(2)}) collective-permute-start(bf16[1,4,2048]{2,1,0:T(4,128)(2,1)S(1)} %slice.569), channel_id=1, source_target_pairs={{0,15},{1,0},{2,1},{3,2},{4,3},{5,4},{6,5},{7,6},{8,7},{9,8},{10,9... | collective-permute-start | bytes 49160 | tf_op jit(solution)/shard_map/ppermute | solution.py:54
  (16 other events, 32.1 us)

commit v13 on v10

--- a/solution.py
+++ b/solution.py
@@ -217,7 +217,15 @@
     time_link = new_field * next_time_field
     slab_link = new_field * next_slab_field
     local_log = -0.5 * jnp.sum(u * u) - log_det
-    local_act = jnp.sum(density)
+    on_site = squared + quartic * (squared - 1.0) * (squared - 1.0)
+    inner = next_y_field + next_z_field
+    inner_t = jnp.sum(new_field[:-1] * new_field[1:])
+    inner_x = jnp.sum(new_field[:, :-1] * new_field[:, 1:])
+    local_part = jnp.sum(on_site - 2.0 * hopping * new_field * inner) - 2.0 * hopping * (
+        inner_t + inner_x
+    )
+    edge_part = jnp.sum(new_field[-1:] * ahead_time) + jnp.sum(new_field[:, -1:] * ahead_slab)
+    local_act = local_part - 2.0 * hopping * edge_part
     members = lax.axis_size("space") * lax.axis_size("tm")
     partials = jnp.broadcast_to(jnp.stack([local_log, local_act])[None], (members, 2))
     sums = jnp.sum(lax.all_to_all(partials, ("space", "tm"), 0, 0, tiled=True), axis=0)

time: 128 us -> 131 us (1.023)
  blocking collectives: 40 us -> 0 us
  waiting for transfers between devices: 4.3 us -> 26.3 us
  starting transfers between devices: 44.2 us -> 58.9 us
  between operations: 4.07 us -> 7.36 us
  other arithmetic: 13.9 us -> 16.1 us
    all_to_all x1 -> x0, blocking collectives: 40 us -> none  [shards(): lax.all_to_all(partials, ('space', 'tm'), 0, 0, tiled=True)]
    all_to_all x0 -> x1, waiting for transfers between devices: none -> 23.4 us  [shards(): lax.all_to_all(partials, ('space', 'tm'), 0, 0, tiled=True)]
    all_to_all x0 -> x1, starting transfers between devices: none -> 14.6 us  [shards(): lax.all_to_all(partials, ('space', 'tm'), 0, 0, tiled=True)]
    reduce_sum x1 -> x5, other arithmetic: 1.6 us -> 3.48 us  [the longest x1 0.87 us: shards(): jnp.sum(on_site - 2.0 * hopping * new_field * inner)]
    ppermute x2, waiting for transfers between devices: 1.39 us -> 0.01 us  [shifted(): lax.ppermute(x, axis, [(i, (i + by) % length) for i in range(length)])]
  transfers between devices with their start and end apart: 6 -> 7, of which waited for: 3 -> 3; matrix products, arithmetic and copies ran while one was open for 5% -> 7% of each run, Pallas kernels for 0% -> 0%
where the time goes in v13:
time: 131 us; the launch traced here: 130 us
  starting transfers between devices  58.9 us (45%)
  waiting for transfers between devices  26.3 us (20%)
  other arithmetic  16.1 us (12%)
  matrix products  11.8 us (9%)
  local copies, waits for them, and re-layouts  9.89 us (8%)
  between operations  7.36 us (6%)
    ppermute x4, starting transfers between devices, exchange(): return lax.ppermute(x, axis, [(i, i ^ bit) for i in range(length)])  25.9 us
    all_to_all x1, waiting for transfers between devices, shards(): lax.all_to_all(partials, ('space', 'tm'), 0, 0, tiled=True)  23.4 us
    ppermute x2, starting transfers between devices, shifted(): lax.ppermute(x, axis, [(i, (i + by) % length) for i in range(length)])  18.3 us
    all_to_all x1, starting transfers between devices, shards(): lax.all_to_all(partials, ('space', 'tm'), 0, 0, tiled=True)  14.6 us
    unnamed x2, matrix products  4.96 us
    ppermute x4, waiting for transfers between devices, exchange(): return lax.ppermute(x, axis, [(i, i ^ bit) for i in range(length)])  2.9 us
  transfers between devices with their start and end apart: 7, of which 3 were waited for; matrix products, arithmetic and copies ran while one was open for 7% of the time, Pallas kernels for 0%

profile of v13, /device:TPU:1, one launch (start us, length us, event | category | flops | bytes accessed | tf_op | source)
XLA Modules:
  0.0 130.4 jit_solution(9808822403147981042)
XLA Ops:
  1.2 1.4 %convert_bitcast_fusion.1 = (bf16[1,128]{1,0:T(2,128)(2,1)S(1)}, s32[128]{0:T(128)S(1)}) fusion(s32[1,1,128]{2,1,0:T(1,128)} %param.16, s32[]{:T(128)} %broadcast.289), kind=kLoop, calls=%fused_computation.211 | loop fusion | flops 128 | bytes 1284 | tf_op jit(solution)/shard_map/convert_element_type | solution.py:120
  3.0 1.1 select_convert_fusion
  7.2 9.6 %collective-permute-start = (bf16[1,129,128]{2,1,0:T(8,128)(2,1)S(1)}, bf16[1,129,128]{2,1,0:T(8,128)(2,1)S(1)}, u32[]{:S(2)}, u32[]{:S(2)}) collective-permute-start(bf16[1,129,128]{2,1,0:T(8,128)(2,1)S(1)} %maximum_bitcast_fusion), channel_id=1, source_target_pairs={{0,8},{1,9},{2,10},{3,11},{4,12},{5,13},{6,14},{7,15},{8,0},{9,1},... | collective-permute-start | bytes 99080 | tf_op jit(solution)/shard_map/ppermute | solution.py:26
  17.2 0.9 gather_fusion
  18.1 0.9 gather_fusion.1
  19.9 4.9 %collective-permute-start.1 = (bf16[2,129,128]{2,1,0:T(8,128)(2,1)S(1)}, bf16[2,129,128]{2,1,0:T(8,128)(2,1)S(1)}, u32[]{:S(2)}, u32[]{:S(2)}) collective-permute-start(bf16[2,129,128]{2,1,0:T(8,128)(2,1)S(1)} %pad_maximum_fusion.5), channel_id=1, source_target_pairs={{0,4},{1,5},{2,6},{3,7},{4,0},{5,1},{6,2},{7,3},{8,12},{9,13},{10,... | collective-permute-start | bytes 198152 | tf_op jit(solution)/shard_map/ppermute | solution.py:26
  24.8 1.7 %collective-permute-done.1 = bf16[2,129,128]{2,1,0:T(8,128)(2,1)S(1)} collective-permute-done((bf16[2,129,128]{2,1,0:T(8,128)(2,1)S(1)}, bf16[2,129,128]{2,1,0:T(8,128)(2,1)S(1)}, u32[]{:S(2)}, u32[]{:S(2)}) %collective-permute-start.1) | collective-permute-done | bytes 66080 | tf_op jit(solution)/shard_map/ppermute | solution.py:26
  26.5 3.5 %collective-permute-start.2 = (bf16[4,129,128]{2,1,0:T(8,128)(2,1)S(1)}, bf16[4,129,128]{2,1,0:T(8,128)(2,1)S(1)}, u32[]{:S(2)}, u32[]{:S(2)}) collective-permute-start(bf16[4,129,128]{2,1,0:T(8,128)(2,1)S(1)} %pad_maximum_fusion.1), channel_id=1, source_target_pairs={{0,2},{1,3},{2,0},{3,1},{4,6},{5,7},{6,4},{7,5},{8,10},{9,11},{10,... | collective-permute-start | bytes 396296 | tf_op jit(solution)/shard_map/ppermute | solution.py:26
  31.3 1.2 collective-permute-done.2
  32.5 7.8 %collective-permute-start.3 = (bf16[8,129,128]{2,1,0:T(8,128)(2,1)S(1)}, bf16[8,129,128]{2,1,0:T(8,128)(2,1)S(1)}, u32[]{:S(2)}, u32[]{:S(2)}) collective-permute-start(bf16[8,129,128]{2,1,0:T(8,128)(2,1)S(1)} %pad_maximum_fusion), channel_id=1, source_target_pairs={{0,1},{1,0},{2,3},{3,2},{4,5},{5,4},{6,7},{7,6},{8,9},{9,8},{10,11... | collective-permute-start | bytes 792584 | tf_op jit(solution)/shard_map/ppermute | solution.py:26
  40.4 1.9 %fusion.22 = f32[128,768]{0,1:S(1)} fusion(bf16[768,2304]{1,0:T(8,128)(2,1)} %param.21, f32[128,768]{1,0:T(8,128)S(1)} %get-tuple-element.10, f32[768]{0:T(1024)S(1)} %copy-done.7, f32[128]{0:T(128)S(1)} %add_rsqrt_fusion.2, f32[128]{0:T(128)S(1)} %broadcast_multiply_fusion.2), kind=kOutput, calls=%fused_computation.32 | convolution fusion | flops 151388160 | bytes 1970176
  42.9 1.0 fusion.102
  45.9 3.0 %fusion.12 = f32[1024,1536]{0,1:S(1)} fusion(bf16[768,2304]{1,0:T(8,128)(2,1)S(1)} %copy-done.5, f32[1024,768]{1,0:T(8,128)S(1)} %get-tuple-element.12, f32[768]{0:T(1024)S(1)} %copy-done.7, f32[1024]{0:T(1024)S(1)} %add_rsqrt_fusion, f32[1024]{0:T(1024)S(1)} %broadcast_multiply_fusion), kind=kOutput, calls=%fused_computation.21 | convolution fusion | flops 2419064832 | bytes 11808768
  49.5 1.1 multiply_reduce_fusion
  50.6 1.3 %fusion = f32[12,128]{1,0:T(8,128)S(1)} fusion(f32[12,128,1024]{2,1,0:T(8,128)S(1)} %get-tuple-element.47, f32[12,128]{1,0:T(8,128)S(1)} %get-tuple-element.46), kind=kLoop, calls=%fused_computation.5 | loop fusion | flops 4717056 | bytes 6303744 | tf_op jit(solution)/shard_map/reduce_sum | solution.py:167
  51.9 1.8 %fusion.25 = f32[128,12,64]{0,2,1:T(8,128)S(1)} fusion(f32[12,128,1024]{2,1,0:T(8,128)S(1)} %get-tuple-element.47, f32[12,128]{1,0:T(8,128)S(1)} %get-tuple-element.46, bf16[2,12,1024,64]{2,3,1,0:T(8,128)(2,1)S(1)} %convert_bitcast_fusion, f32[128,12]{0,1:T(8,128)S(1)} %bitcast.222), kind=kOutput, calls=%fused_computation.38 | convolution fusion | flops 206143488 | bytes 8273920 | tf_op jit(solution)/shard_map/hqk,hkd->qhd/dot_general | solution.py:168
  54.7 1.3 fusion.7
  57.7 1.0 fusion.53
  62.1 16.1 %collective-permute-start.5 = (bf16[4,1,2048]{2,1,0:T(2,128)(2,1)S(1)}, bf16[4,1,2048]{2,1,0:T(2,128)(2,1)S(1)}, u32[]{:S(2)}, u32[]{:S(2)}) collective-permute-start(bf16[4,1,2048]{2,1,0:T(2,128)(2,1)S(1)} %slice.589), channel_id=1, source_target_pairs={{0,496},{16,0},{32,16},{48,32},{64,48},{80,64},{96,80},{112,96},{1... | collective-permute-start | bytes 49160 | tf_op jit(solution)/shard_map/ppermute | solution.py:54
  78.2 2.2 %collective-permute-start.4 = (bf16[1,4,2048]{2,1,0:T(4,128)(2,1)S(1)}, bf16[1,4,2048]{2,1,0:T(4,128)(2,1)S(1)}, u32[]{:S(2)}, u32[]{:S(2)}) collective-permute-start(bf16[1,4,2048]{2,1,0:T(4,128)(2,1)S(1)} %slice.587), channel_id=1, source_target_pairs={{0,15},{1,0},{2,1},{3,2},{4,3},{5,4},{6,5},{7,6},{8,7},{9,8},{10,9... | collective-permute-start | bytes 49160 | tf_op jit(solution)/shard_map/ppermute | solution.py:54
  80.4 0.9 subtract_reduce_fusion
  88.1 14.6 %all-to-all-start = ((f32[512,1,2]{2,1,0:T(1,128)}), f32[512,1,2]{2,1,0:T(1,128)S(1)}, u32[]{:S(2)}, u32[]{:S(2)}) async-start(f32[512,1,2]{2,1,0:T(1,128)} %broadcast_in_dim.74), calls=%async_computation | async-start | bytes 524288 | tf_op jit(solution)/shard_map/all_to_all | solution.py:231
  102.8 1.0 fusion.73
  103.8 23.4 %all-to-all-done = f32[512,1,2]{2,1,0:T(1,128)S(1)} async-done(((f32[512,1,2]{2,1,0:T(1,128)}), f32[512,1,2]{2,1,0:T(1,128)S(1)}, u32[]{:S(2)}, u32[]{:S(2)}) %all-to-all-start) | async-done | bytes 4128 | tf_op jit(solution)/shard_map/all_to_all | solution.py:231
  (180 shorter events, 19.3 us)
Async XLA Ops:
  0.6 16.5 %copy-start = (bf16[256,768]{1,0:T(8,128)(2,1)S(1)}, bf16[256,768]{1,0:T(8,128)(2,1)}, u32[]{:S(2)}) copy-start(bf16[256,768]{1,0:T(8,128)(2,1)} %param.18) | copy-start | bytes 1179652
  3.0 13.9 %copy-start.12 = (s32[1,1,128]{2,1,0:T(1,128)S(1)}, s32[1,1,128]{2,1,0:T(1,128)}, u32[]{:S(2)}) copy-start(s32[1,1,128]{2,1,0:T(1,128)} %param.16) | copy-start | bytes 1540
  4.1 13.0 %copy-start.10 = (s32[128]{0:T(128)S(1)}, s32[128]{0:T(128)}, u32[]{:S(2)}) copy-start(s32[128]{0:T(128)} %constant.153) | copy-start | bytes 1540
  4.1 13.0 %copy-start.11 = (s32[128]{0:T(128)S(1)}, s32[128]{0:T(128)}, u32[]{:S(2)}) copy-start(s32[128]{0:T(128)} %constant.154) | copy-start | bytes 1540
  7.2 12.1 %copy-start.6 = (f32[768]{0:T(1024)S(1)}, f32[768]{0:T(1024)}, u32[]{:S(2)}) copy-start(f32[768]{0:T(1024)} %param.19) | copy-start | bytes 9220
  7.2 12.7 %collective-permute-start = (bf16[1,129,128]{2,1,0:T(8,128)(2,1)S(1)}, bf16[1,129,128]{2,1,0:T(8,128)(2,1)S(1)}, u32[]{:S(2)}, u32[]{:S(2)}) collective-permute-start(bf16[1,129,128]{2,1,0:T(8,128)(2,1)S(1)} %maximum_bitcast_fusion), channel_id=1, source_target_pairs={{0,8},{1,9},{2,10},{3,11},{4,12},{5,13},{6,14},{7,15},{8,0},{9,1},... | collective-permute-start | bytes 99080 | tf_op jit(solution)/shard_map/ppermute | solution.py:26
  17.1 2.5 %copy-start.8 = (s32[16,8]{0,1:T(8,128)S(1)}, s32[16,8]{0,1:T(8,128)}, u32[]{:S(2)}) copy-start(s32[16,8]{0,1:T(8,128)} %param.17) | copy-start | bytes 1540
  18.0 12.0 %copy-start.3 = (bf16[768,512]{1,0:T(8,128)(2,1)S(1)}, bf16[768,512]{1,0:T(8,128)(2,1)}, u32[]{:S(2)}) copy-start(bf16[768,512]{1,0:T(8,128)(2,1)} %param.23) | copy-start | bytes 2359300
  18.1 12.3 %copy-start.9 = (f32[512]{0:T(512)S(1)}, f32[512]{0:T(512)}, u32[]{:S(2)}) copy-start(f32[512]{0:T(512)} %param.24) | copy-start | bytes 6148
  18.1 12.5 %copy-start.1 = (s32[16]{0:T(128)S(1)}, s32[16]{0:T(128)}, u32[]{:S(2)}) copy-start(s32[16]{0:T(128)} %constant.148.clone) | copy-start | bytes 196
  19.0 21.4 %copy-start.7 = (f32[768]{0:T(1024)S(1)}, f32[768]{0:T(1024)}, u32[]{:S(2)}) copy-start(f32[768]{0:T(1024)} %param.20) | copy-start | bytes 9220
  19.9 6.6 %collective-permute-start.1 = (bf16[2,129,128]{2,1,0:T(8,128)(2,1)S(1)}, bf16[2,129,128]{2,1,0:T(8,128)(2,1)S(1)}, u32[]{:S(2)}, u32[]{:S(2)}) collective-permute-start(bf16[2,129,128]{2,1,0:T(8,128)(2,1)S(1)} %pad_maximum_fusion.5), channel_id=1, source_target_pairs={{0,4},{1,5},{2,6},{3,7},{4,0},{5,1},{6,2},{7,3},{8,12},{9,13},{10,... | collective-permute-start | bytes 198152 | tf_op jit(solution)/shard_map/ppermute | solution.py:26
  26.5 6.0 %collective-permute-start.2 = (bf16[4,129,128]{2,1,0:T(8,128)(2,1)S(1)}, bf16[4,129,128]{2,1,0:T(8,128)(2,1)S(1)}, u32[]{:S(2)}, u32[]{:S(2)}) collective-permute-start(bf16[4,129,128]{2,1,0:T(8,128)(2,1)S(1)} %pad_maximum_fusion.1), channel_id=1, source_target_pairs={{0,2},{1,3},{2,0},{3,1},{4,6},{5,7},{6,4},{7,5},{8,10},{9,11},{10,... | collective-permute-start | bytes 396296 | tf_op jit(solution)/shard_map/ppermute | solution.py:26
  32.5 9.8 %collective-permute-start.3 = (bf16[8,129,128]{2,1,0:T(8,128)(2,1)S(1)}, bf16[8,129,128]{2,1,0:T(8,128)(2,1)S(1)}, u32[]{:S(2)}, u32[]{:S(2)}) collective-permute-start(bf16[8,129,128]{2,1,0:T(8,128)(2,1)S(1)} %pad_maximum_fusion), channel_id=1, source_target_pairs={{0,1},{1,0},{2,3},{3,2},{4,5},{5,4},{6,7},{7,6},{8,9},{9,8},{10,11... | collective-permute-start | bytes 792584 | tf_op jit(solution)/shard_map/ppermute | solution.py:26
  43.9 2.0 %copy-start.5 = (bf16[768,2304]{1,0:T(8,128)(2,1)S(1)}, bf16[768,2304]{1,0:T(8,128)(2,1)}, u32[]{:S(2)}) copy-start(bf16[768,2304]{1,0:T(8,128)(2,1)} %param.21) | copy-start | bytes 10616836
  51.9 2.3 %copy-start.13 = (f32[768]{0:T(1024)S(1)}, f32[768]{0:T(1024)}, u32[]{:S(2)}) copy-start(f32[768]{0:T(1024)} %param.22) | copy-start | bytes 9220
  57.2 2.4 %copy-start.4 = (f32[4,4,2048]{2,1,0:T(4,128)S(1)}, f32[4,4,2048]{2,1,0:T(4,128)}, u32[]{:S(2)}) copy-start(f32[4,4,2048]{2,1,0:T(4,128)} %param.15) | copy-start | bytes 393220
  60.4 70.0 %copy-start.2 = (f32[4,4,2048]{2,1,0:T(4,128)}, f32[4,4,2048]{2,1,0:T(4,128)S(1)}, u32[]{:S(2)}) copy-start(f32[4,4,2048]{2,1,0:T(4,128)S(1)} %get-tuple-element.6) | copy-start | bytes 393220
  62.1 22.5 %collective-permute-start.5 = (bf16[4,1,2048]{2,1,0:T(2,128)(2,1)S(1)}, bf16[4,1,2048]{2,1,0:T(2,128)(2,1)S(1)}, u32[]{:S(2)}, u32[]{:S(2)}) collective-permute-start(bf16[4,1,2048]{2,1,0:T(2,128)(2,1)S(1)} %slice.589), channel_id=1, source_target_pairs={{0,496},{16,0},{32,16},{48,32},{64,48},{80,64},{96,80},{112,96},{1... | collective-permute-start | bytes 49160 | tf_op jit(solution)/shard_map/ppermute | solution.py:54
  78.2 7.1 %collective-permute-start.4 = (bf16[1,4,2048]{2,1,0:T(4,128)(2,1)S(1)}, bf16[1,4,2048]{2,1,0:T(4,128)(2,1)S(1)}, u32[]{:S(2)}, u32[]{:S(2)}) collective-permute-start(bf16[1,4,2048]{2,1,0:T(4,128)(2,1)S(1)} %slice.587), channel_id=1, source_target_pairs={{0,15},{1,0},{2,1},{3,2},{4,3},{5,4},{6,5},{7,6},{8,7},{9,8},{10,9... | collective-permute-start | bytes 49160 | tf_op jit(solution)/shard_map/ppermute | solution.py:54
  88.1 39.1 %all-to-all-start = ((f32[512,1,2]{2,1,0:T(1,128)}), f32[512,1,2]{2,1,0:T(1,128)S(1)}, u32[]{:S(2)}, u32[]{:S(2)}) async-start(f32[512,1,2]{2,1,0:T(1,128)} %broadcast_in_dim.74), calls=%async_computation | async-start | bytes 524288 | tf_op jit(solution)/shard_map/all_to_all | solution.py:231

commit v14 on v10

--- a/solution.py
+++ b/solution.py
@@ -41,11 +41,11 @@
         bits.append(bit)
         bit *= 2
     offsets = [0]
-    for bit in reversed(bits[1:]):
+    for bit in bits[:-1]:
         x = jnp.concatenate([x, exchange(x, axis, bit)], axis=0)
         offsets = offsets + [o ^ bit for o in offsets]
-    received = exchange(x, axis, bits[0])
-    offsets = offsets + [o ^ bits[0] for o in offsets]
+    received = exchange(x, axis, bits[-1])
+    offsets = offsets + [o ^ bits[-1] for o in offsets]
     return x, received, offsets
 
 

time: 128 us -> 151 us (1.18)
  waiting for transfers between devices: 4.3 us -> 36.3 us
  starting transfers between devices: 44.2 us -> 34.7 us
    ppermute x4, waiting for transfers between devices: 2.9 us -> 35.7 us  [exchange(): return lax.ppermute(x, axis, [(i, i ^ bit) for i in range(length)])]
    ppermute x4, starting transfers between devices: 25.9 us -> 16.5 us  [exchange(): return lax.ppermute(x, axis, [(i, i ^ bit) for i in range(length)])]
  transfers between devices with their start and end apart: 6 -> 6, of which waited for: 3 -> 4; matrix products, arithmetic and copies ran while one was open for 5% -> 4% of each run, Pallas kernels for 0% -> 0%
where the time goes in v14:
time: 151 us
  blocking collectives  40.8 us (27%)
  waiting for transfers between devices  36.3 us (24%)
  starting transfers between devices  34.7 us (23%)
  other arithmetic  13.9 us (9%)
  matrix products  11.8 us (8%)
  local copies, waits for them, and re-layouts  9.25 us (6%)
  between operations  4.06 us (3%)
    all_to_all x1, blocking collectives, shards(): lax.all_to_all(partials, ('space', 'tm'), 0, 0, tiled=True)  40.8 us
    ppermute x4, waiting for transfers between devices, exchange(): return lax.ppermute(x, axis, [(i, i ^ bit) for i in range(length)])  35.7 us
    ppermute x2, starting transfers between devices, shifted(): lax.ppermute(x, axis, [(i, (i + by) % length) for i in range(length)])  18.2 us
    ppermute x4, starting transfers between devices, exchange(): return lax.ppermute(x, axis, [(i, i ^ bit) for i in range(length)])  16.5 us
    unnamed x2, matrix products  4.97 us
  transfers between devices with their start and end apart: 6, of which 4 were waited for; matrix products, arithmetic and copies ran while one was open for 4% of the time, Pallas kernels for 0%

profile of v14, /device:TPU:1, one launch (start us, length us, event | category | flops | bytes accessed | tf_op | source)
XLA Modules:
  0.0 150.8 jit_solution(8122673644123683874)
XLA Ops:
  1.2 1.4 convert_bitcast_fusion.1
  3.0 1.1 select_convert_fusion
  7.2 8.8 %collective-permute-start = (bf16[1,129,128]{2,1,0:T(8,128)(2,1)S(1)}, bf16[1,129,128]{2,1,0:T(8,128)(2,1)S(1)}, u32[]{:S(2)}, u32[]{:S(2)}) collective-permute-start(bf16[1,129,128]{2,1,0:T(8,128)(2,1)S(1)} %maximum_bitcast_fusion), channel_id=1, source_target_pairs={{0,1},{1,0},{2,3},{3,2},{4,5},{5,4},{6,7},{7,6},{8,9},{9,8},{10,11... | collective-permute-start | bytes 99080 | tf_op jit(solution)/shard_map/ppermute | solution.py:26
  16.3 0.9 gather_fusion
  17.2 0.9 gather_fusion.1
  19.0 1.9 %collective-permute-start.1 = (bf16[2,129,128]{2,1,0:T(8,128)(2,1)S(1)}, bf16[2,129,128]{2,1,0:T(8,128)(2,1)S(1)}, u32[]{:S(2)}, u32[]{:S(2)}) collective-permute-start(bf16[2,129,128]{2,1,0:T(8,128)(2,1)S(1)} %pad_maximum_fusion.4), channel_id=1, source_target_pairs={{0,2},{1,3},{2,0},{3,1},{4,6},{5,7},{6,4},{7,5},{8,10},{9,11},{10,... | collective-permute-start | bytes 198152 | tf_op jit(solution)/shard_map/ppermute | solution.py:26
  21.0 3.8 %collective-permute-done.1 = bf16[2,129,128]{2,1,0:T(8,128)(2,1)S(1)} collective-permute-done((bf16[2,129,128]{2,1,0:T(8,128)(2,1)S(1)}, bf16[2,129,128]{2,1,0:T(8,128)(2,1)S(1)}, u32[]{:S(2)}, u32[]{:S(2)}) %collective-permute-start.1) | collective-permute-done | bytes 66080 | tf_op jit(solution)/shard_map/ppermute | solution.py:26
  24.7 1.9 %collective-permute-start.2 = (bf16[4,129,128]{2,1,0:T(8,128)(2,1)S(1)}, bf16[4,129,128]{2,1,0:T(8,128)(2,1)S(1)}, u32[]{:S(2)}, u32[]{:S(2)}) collective-permute-start(bf16[4,129,128]{2,1,0:T(8,128)(2,1)S(1)} %pad_maximum_fusion.1), channel_id=1, source_target_pairs={{0,4},{1,5},{2,6},{3,7},{4,0},{5,1},{6,2},{7,3},{8,12},{9,13},{10,... | collective-permute-start | bytes 396296 | tf_op jit(solution)/shard_map/ppermute | solution.py:26
  27.9 8.2 %collective-permute-done.2 = bf16[4,129,128]{2,1,0:T(8,128)(2,1)S(1)} collective-permute-done((bf16[4,129,128]{2,1,0:T(8,128)(2,1)S(1)}, bf16[4,129,128]{2,1,0:T(8,128)(2,1)S(1)}, u32[]{:S(2)}, u32[]{:S(2)}) %collective-permute-start.2) | collective-permute-done | bytes 132128 | tf_op jit(solution)/shard_map/ppermute | solution.py:26
  36.1 3.9 %collective-permute-start.3 = (bf16[8,129,128]{2,1,0:T(8,128)(2,1)S(1)}, bf16[8,129,128]{2,1,0:T(8,128)(2,1)S(1)}, u32[]{:S(2)}, u32[]{:S(2)}) collective-permute-start(bf16[8,129,128]{2,1,0:T(8,128)(2,1)S(1)} %pad_maximum_fusion), channel_id=1, source_target_pairs={{0,8},{1,9},{2,10},{3,11},{4,12},{5,13},{6,14},{7,15},{8,0},{9,1},... | collective-permute-start | bytes 792584 | tf_op jit(solution)/shard_map/ppermute | solution.py:26
  40.0 1.9 %fusion.22 = f32[128,768]{0,1:S(1)} fusion(bf16[768,2304]{1,0:T(8,128)(2,1)} %param.21, f32[128,768]{1,0:T(8,128)S(1)} %get-tuple-element.12, f32[768]{0:T(1024)S(1)} %copy-done.6, f32[128]{0:T(128)S(1)} %add_rsqrt_fusion.2, f32[128]{0:T(128)S(1)} %broadcast_multiply_fusion.2), kind=kOutput, calls=%fused_computation.32 | convolution fusion | flops 151388160 | bytes 1970176
  41.9 23.8 %collective-permute-done.3 = bf16[8,129,128]{2,1,0:T(8,128)(2,1)S(1)} collective-permute-done((bf16[8,129,128]{2,1,0:T(8,128)(2,1)S(1)}, bf16[8,129,128]{2,1,0:T(8,128)(2,1)S(1)}, u32[]{:S(2)}, u32[]{:S(2)}) %collective-permute-start.3) | collective-permute-done | bytes 264224 | tf_op jit(solution)/shard_map/ppermute | solution.py:26
  66.3 1.0 fusion.103
  69.3 3.0 %fusion.12 = f32[1024,1536]{0,1:S(1)} fusion(bf16[768,2304]{1,0:T(8,128)(2,1)S(1)} %copy-done.4, f32[1024,768]{1,0:T(8,128)S(1)} %get-tuple-element.14, f32[768]{0:T(1024)S(1)} %copy-done.6, f32[1024]{0:T(1024)S(1)} %add_rsqrt_fusion, f32[1024]{0:T(1024)S(1)} %broadcast_multiply_fusion), kind=kOutput, calls=%fused_computation.21 | convolution fusion | flops 2419064832 | bytes 11808768
  72.9 1.1 multiply_reduce_fusion
  74.0 1.3 fusion
  75.3 1.8 %fusion.25 = f32[128,12,64]{0,2,1:T(8,128)S(1)} fusion(f32[12,128,1024]{2,1,0:T(8,128)S(1)} %get-tuple-element.44, f32[12,128]{1,0:T(8,128)S(1)} %get-tuple-element.43, bf16[2,12,1024,64]{2,3,1,0:T(8,128)(2,1)S(1)} %convert_bitcast_fusion, f32[128,12]{0,1:T(8,128)S(1)} %bitcast.221), kind=kOutput, calls=%fused_computation.38 | convolution fusion | flops 206143488 | bytes 8273920 | tf_op jit(solution)/shard_map/hqk,hkd->qhd/dot_general | solution.py:168
  78.1 1.3 fusion.7
  81.1 1.0 fusion.53
  83.0 0.8 fusion.95
  83.8 15.5 %collective-permute-start.5 = (bf16[4,1,2048]{2,1,0:T(2,128)(2,1)S(1)}, bf16[4,1,2048]{2,1,0:T(2,128)(2,1)S(1)}, u32[]{:S(2)}, u32[]{:S(2)}) collective-permute-start(bf16[4,1,2048]{2,1,0:T(2,128)(2,1)S(1)} %slice.571), channel_id=1, source_target_pairs={{0,496},{16,0},{32,16},{48,32},{64,48},{80,64},{96,80},{112,96},{1... | collective-permute-start | bytes 49160 | tf_op jit(solution)/shard_map/ppermute | solution.py:54
  99.4 2.7 %collective-permute-start.4 = (bf16[1,4,2048]{2,1,0:T(4,128)(2,1)S(1)}, bf16[1,4,2048]{2,1,0:T(4,128)(2,1)S(1)}, u32[]{:S(2)}, u32[]{:S(2)}) collective-permute-start(bf16[1,4,2048]{2,1,0:T(4,128)(2,1)S(1)} %slice.569), channel_id=1, source_target_pairs={{0,15},{1,0},{2,1},{3,2},{4,3},{5,4},{6,5},{7,6},{8,7},{9,8},{10,9... | collective-permute-start | bytes 49160 | tf_op jit(solution)/shard_map/ppermute | solution.py:54
  104.4 1.6 %fusion.93 = (f32[]{:T(128)}, f32[4,4,2048]{2,1,0:T(4,128)}, f32[4,4,2048]{2,1,0:T(4,128)}, f32[4,4,2048]{2,1,0:T(4,128)}) fusion(f32[4,4,2048]{2,1,0:T(4,128)S(1)} %get-tuple-element.8, f32[4,4,1]{2,1,0:T(4,128)S(1)} %slice.577, f32[4,4,2047]{2,1,0:T(4,128)S(1)} %slice.576, f32[4,4,1985]{2,1,0:T(4,128)S(1)} %bitcast.205, f32[4,4,63]{2,1,0:T(4,128)S(1)} %slice.574, ...), kind=kLoop, calls=%fused_computation.213 | loop fusion | flops 720895 | bytes 1198084 | tf_op jit(solution)/shard_map/reduce_sum | solution.py:220
  106.9 40.8 %all_to_all.6 = f32[512,1,2]{2,1,0:T(1,128)S(1)} all-to-all(f32[512,1,2]{2,1,0:T(1,128)S(1)} %broadcast_in_dim.74), channel_id=1, replica_groups=mesh['space'=32,'tm'=16] {'space','tm'}, dimensions={0} | all-to-all | bytes 8192 | tf_op jit(solution)/shard_map/all_to_all | solution.py:223
  (175 shorter events, 16.5 us)
Async XLA Ops:
  0.6 15.6 %copy-start = (bf16[256,768]{1,0:T(8,128)(2,1)S(1)}, bf16[256,768]{1,0:T(8,128)(2,1)}, u32[]{:S(2)}) copy-start(bf16[256,768]{1,0:T(8,128)(2,1)} %param.18) | copy-start | bytes 1179652
  3.0 13.0 %copy-start.11 = (s32[1,1,128]{2,1,0:T(1,128)S(1)}, s32[1,1,128]{2,1,0:T(1,128)}, u32[]{:S(2)}) copy-start(s32[1,1,128]{2,1,0:T(1,128)} %param.16) | copy-start | bytes 1540
  4.1 12.2 %copy-start.9 = (s32[128]{0:T(128)S(1)}, s32[128]{0:T(128)}, u32[]{:S(2)}) copy-start(s32[128]{0:T(128)} %constant.149) | copy-start | bytes 1540
  4.1 12.2 %copy-start.10 = (s32[128]{0:T(128)S(1)}, s32[128]{0:T(128)}, u32[]{:S(2)}) copy-start(s32[128]{0:T(128)} %constant.150) | copy-start | bytes 1540
  7.2 11.2 %copy-start.5 = (f32[768]{0:T(1024)S(1)}, f32[768]{0:T(1024)}, u32[]{:S(2)}) copy-start(f32[768]{0:T(1024)} %param.19) | copy-start | bytes 9220
  7.2 11.8 %collective-permute-start = (bf16[1,129,128]{2,1,0:T(8,128)(2,1)S(1)}, bf16[1,129,128]{2,1,0:T(8,128)(2,1)S(1)}, u32[]{:S(2)}, u32[]{:S(2)}) collective-permute-start(bf16[1,129,128]{2,1,0:T(8,128)(2,1)S(1)} %maximum_bitcast_fusion), channel_id=1, source_target_pairs={{0,1},{1,0},{2,3},{3,2},{4,5},{5,4},{6,7},{7,6},{8,9},{9,8},{10,11... | collective-permute-start | bytes 99080 | tf_op jit(solution)/shard_map/ppermute | solution.py:26
  16.3 2.5 %copy-start.7 = (s32[16,8]{0,1:T(8,128)S(1)}, s32[16,8]{0,1:T(8,128)}, u32[]{:S(2)}) copy-start(s32[16,8]{0,1:T(8,128)} %param.17) | copy-start | bytes 1540
  17.2 9.5 %copy-start.2 = (bf16[768,512]{1,0:T(8,128)(2,1)S(1)}, bf16[768,512]{1,0:T(8,128)(2,1)}, u32[]{:S(2)}) copy-start(bf16[768,512]{1,0:T(8,128)(2,1)} %param.23) | copy-start | bytes 2359300
  17.2 9.8 %copy-start.8 = (f32[512]{0:T(512)S(1)}, f32[512]{0:T(512)}, u32[]{:S(2)}) copy-start(f32[512]{0:T(512)} %param.24) | copy-start | bytes 6148
  18.1 21.9 %copy-start.6 = (f32[768]{0:T(1024)S(1)}, f32[768]{0:T(1024)}, u32[]{:S(2)}) copy-start(f32[768]{0:T(1024)} %param.20) | copy-start | bytes 9220
  19.0 5.7 %collective-permute-start.1 = (bf16[2,129,128]{2,1,0:T(8,128)(2,1)S(1)}, bf16[2,129,128]{2,1,0:T(8,128)(2,1)S(1)}, u32[]{:S(2)}, u32[]{:S(2)}) collective-permute-start(bf16[2,129,128]{2,1,0:T(8,128)(2,1)S(1)} %pad_maximum_fusion.4), channel_id=1, source_target_pairs={{0,2},{1,3},{2,0},{3,1},{4,6},{5,7},{6,4},{7,5},{8,10},{9,11},{10,... | collective-permute-start | bytes 198152 | tf_op jit(solution)/shard_map/ppermute | solution.py:26
  24.7 11.3 %collective-permute-start.2 = (bf16[4,129,128]{2,1,0:T(8,128)(2,1)S(1)}, bf16[4,129,128]{2,1,0:T(8,128)(2,1)S(1)}, u32[]{:S(2)}, u32[]{:S(2)}) collective-permute-start(bf16[4,129,128]{2,1,0:T(8,128)(2,1)S(1)} %pad_maximum_fusion.1), channel_id=1, source_target_pairs={{0,4},{1,5},{2,6},{3,7},{4,0},{5,1},{6,2},{7,3},{8,12},{9,13},{10,... | collective-permute-start | bytes 396296 | tf_op jit(solution)/shard_map/ppermute | solution.py:26
  36.1 29.6 %collective-permute-start.3 = (bf16[8,129,128]{2,1,0:T(8,128)(2,1)S(1)}, bf16[8,129,128]{2,1,0:T(8,128)(2,1)S(1)}, u32[]{:S(2)}, u32[]{:S(2)}) collective-permute-start(bf16[8,129,128]{2,1,0:T(8,128)(2,1)S(1)} %pad_maximum_fusion), channel_id=1, source_target_pairs={{0,8},{1,9},{2,10},{3,11},{4,12},{5,13},{6,14},{7,15},{8,0},{9,1},... | collective-permute-start | bytes 792584 | tf_op jit(solution)/shard_map/ppermute | solution.py:26
  67.3 2.0 %copy-start.4 = (bf16[768,2304]{1,0:T(8,128)(2,1)S(1)}, bf16[768,2304]{1,0:T(8,128)(2,1)}, u32[]{:S(2)}) copy-start(bf16[768,2304]{1,0:T(8,128)(2,1)} %param.21) | copy-start | bytes 10616836
  75.3 2.3 %copy-start.12 = (f32[768]{0:T(1024)S(1)}, f32[768]{0:T(1024)}, u32[]{:S(2)}) copy-start(f32[768]{0:T(1024)} %param.22) | copy-start | bytes 9220
  80.6 2.4 %copy-start.3 = (f32[4,4,2048]{2,1,0:T(4,128)S(1)}, f32[4,4,2048]{2,1,0:T(4,128)}, u32[]{:S(2)}) copy-start(f32[4,4,2048]{2,1,0:T(4,128)} %param.15) | copy-start | bytes 393220
  83.8 67.0 %copy-start.1 = (f32[4,4,2048]{2,1,0:T(4,128)}, f32[4,4,2048]{2,1,0:T(4,128)S(1)}, u32[]{:S(2)}) copy-start(f32[4,4,2048]{2,1,0:T(4,128)S(1)} %get-tuple-element.8) | copy-start | bytes 393220
  83.8 19.9 %collective-permute-start.5 = (bf16[4,1,2048]{2,1,0:T(2,128)(2,1)S(1)}, bf16[4,1,2048]{2,1,0:T(2,128)(2,1)S(1)}, u32[]{:S(2)}, u32[]{:S(2)}) collective-permute-start(bf16[4,1,2048]{2,1,0:T(2,128)(2,1)S(1)} %slice.571), channel_id=1, source_target_pairs={{0,496},{16,0},{32,16},{48,32},{64,48},{80,64},{96,80},{112,96},{1... | collective-permute-start | bytes 49160 | tf_op jit(solution)/shard_map/ppermute | solution.py:54
  99.4 5.1 %collective-permute-start.4 = (bf16[1,4,2048]{2,1,0:T(4,128)(2,1)S(1)}, bf16[1,4,2048]{2,1,0:T(4,128)(2,1)S(1)}, u32[]{:S(2)}, u32[]{:S(2)}) collective-permute-start(bf16[1,4,2048]{2,1,0:T(4,128)(2,1)S(1)} %slice.569), channel_id=1, source_target_pairs={{0,15},{1,0},{2,1},{3,2},{4,3},{5,4},{6,5},{7,6},{8,7},{9,8},{10,9... | collective-permute-start | bytes 49160 | tf_op jit(solution)/shard_map/ppermute | solution.py:54

commit v15 on v10

--- a/solution.py
+++ b/solution.py
@@ -175,9 +175,11 @@
     hidden = embedded + mixed
     normed_out = layer_norm(hidden, gain_out).astype(jnp.bfloat16)
     w_rows = w_head.reshape(D, 2 * P_SIZE * P_SIZE, n_off)
-    affine_rows = jnp.einsum(
-        "tc,crk->krt", normed_out, w_rows, preferred_element_type=jnp.float32
-    ) + b_head.reshape(2 * P_SIZE * P_SIZE, n_off).T[:, :, None]
+    affine_rows = jnp.dot(
+        normed_out, w_head, preferred_element_type=jnp.float32
+    ).reshape(tokens_dev, 2 * P_SIZE * P_SIZE, n_off).transpose(2, 1, 0) + b_head.reshape(
+        2 * P_SIZE * P_SIZE, n_off
+    ).T[:, :, None]
     high = lax.reduce_precision(affine_rows, exponent_bits=8, mantissa_bits=7)
     rest = affine_rows - high
     middle = lax.reduce_precision(rest, exponent_bits=8, mantissa_bits=7)

time: 128 us -> 128 us (level)
  no operation moved by 1% of the time
where the time goes in v15:
time: 128 us
  starting transfers between devices  44.2 us (35%)
  blocking collectives  40 us (31%)
  other arithmetic  14 us (11%)
  matrix products  11.8 us (9%)
  local copies, waits for them, and re-layouts  8.98 us (7%)
  waiting for transfers between devices  4.59 us (4%)
  between operations  4.07 us (3%)
    all_to_all x1, blocking collectives, shards(): lax.all_to_all(partials, ('space', 'tm'), 0, 0, tiled=True)  40 us
    ppermute x4, starting transfers between devices, exchange(): return lax.ppermute(x, axis, [(i, i ^ bit) for i in range(length)])  25.9 us
    ppermute x2, starting transfers between devices, shifted(): lax.ppermute(x, axis, [(i, (i + by) % length) for i in range(length)])  18.3 us
    unnamed x2, matrix products  4.96 us
    ppermute x4, waiting for transfers between devices, exchange(): return lax.ppermute(x, axis, [(i, i ^ bit) for i in range(length)])  3.19 us
  transfers between devices with their start and end apart: 6, of which 3 were waited for; matrix products, arithmetic and copies ran while one was open for 5% of the time, Pallas kernels for 0%

profile of v15, /device:TPU:1, one launch (start us, length us, event | category | flops | bytes accessed | tf_op | source)
XLA Modules:
  0.0 127.7 jit_solution(9280671097341568935)
XLA Ops:
  1.2 1.4 %convert_bitcast_fusion.1 = (bf16[1,128]{1,0:T(2,128)(2,1)S(1)}, s32[128]{0:T(128)S(1)}) fusion(s32[1,1,128]{2,1,0:T(1,128)} %param.16, s32[]{:T(128)} %broadcast.282), kind=kLoop, calls=%fused_computation.203 | loop fusion | flops 128 | bytes 1284 | tf_op jit(solution)/shard_map/convert_element_type | solution.py:120
  3.0 1.1 select_convert_fusion
  7.2 9.6 %collective-permute-start = (bf16[1,129,128]{2,1,0:T(8,128)(2,1)S(1)}, bf16[1,129,128]{2,1,0:T(8,128)(2,1)S(1)}, u32[]{:S(2)}, u32[]{:S(2)}) collective-permute-start(bf16[1,129,128]{2,1,0:T(8,128)(2,1)S(1)} %maximum_bitcast_fusion), channel_id=1, source_target_pairs={{0,8},{1,9},{2,10},{3,11},{4,12},{5,13},{6,14},{7,15},{8,0},{9,1},... | collective-permute-start | bytes 99080 | tf_op jit(solution)/shard_map/ppermute | solution.py:26
  17.2 0.9 gather_fusion
  18.1 0.9 gather_fusion.1
  19.9 4.9 %collective-permute-start.1 = (bf16[2,129,128]{2,1,0:T(8,128)(2,1)S(1)}, bf16[2,129,128]{2,1,0:T(8,128)(2,1)S(1)}, u32[]{:S(2)}, u32[]{:S(2)}) collective-permute-start(bf16[2,129,128]{2,1,0:T(8,128)(2,1)S(1)} %pad_maximum_fusion.4), channel_id=1, source_target_pairs={{0,4},{1,5},{2,6},{3,7},{4,0},{5,1},{6,2},{7,3},{8,12},{9,13},{10,... | collective-permute-start | bytes 198152 | tf_op jit(solution)/shard_map/ppermute | solution.py:26
  24.8 1.7 %collective-permute-done.1 = bf16[2,129,128]{2,1,0:T(8,128)(2,1)S(1)} collective-permute-done((bf16[2,129,128]{2,1,0:T(8,128)(2,1)S(1)}, bf16[2,129,128]{2,1,0:T(8,128)(2,1)S(1)}, u32[]{:S(2)}, u32[]{:S(2)}) %collective-permute-start.1) | collective-permute-done | bytes 66080 | tf_op jit(solution)/shard_map/ppermute | solution.py:26
  26.5 3.5 %collective-permute-start.2 = (bf16[4,129,128]{2,1,0:T(8,128)(2,1)S(1)}, bf16[4,129,128]{2,1,0:T(8,128)(2,1)S(1)}, u32[]{:S(2)}, u32[]{:S(2)}) collective-permute-start(bf16[4,129,128]{2,1,0:T(8,128)(2,1)S(1)} %pad_maximum_fusion.1), channel_id=1, source_target_pairs={{0,2},{1,3},{2,0},{3,1},{4,6},{5,7},{6,4},{7,5},{8,10},{9,11},{10,... | collective-permute-start | bytes 396296 | tf_op jit(solution)/shard_map/ppermute | solution.py:26
  31.0 1.5 %collective-permute-done.2 = bf16[4,129,128]{2,1,0:T(8,128)(2,1)S(1)} collective-permute-done((bf16[4,129,128]{2,1,0:T(8,128)(2,1)S(1)}, bf16[4,129,128]{2,1,0:T(8,128)(2,1)S(1)}, u32[]{:S(2)}, u32[]{:S(2)}) %collective-permute-start.2) | collective-permute-done | bytes 132128 | tf_op jit(solution)/shard_map/ppermute | solution.py:26
  32.5 7.8 %collective-permute-start.3 = (bf16[8,129,128]{2,1,0:T(8,128)(2,1)S(1)}, bf16[8,129,128]{2,1,0:T(8,128)(2,1)S(1)}, u32[]{:S(2)}, u32[]{:S(2)}) collective-permute-start(bf16[8,129,128]{2,1,0:T(8,128)(2,1)S(1)} %pad_maximum_fusion), channel_id=1, source_target_pairs={{0,1},{1,0},{2,3},{3,2},{4,5},{5,4},{6,7},{7,6},{8,9},{9,8},{10,11... | collective-permute-start | bytes 792584 | tf_op jit(solution)/shard_map/ppermute | solution.py:26
  40.4 1.9 %fusion.22 = f32[128,768]{0,1:S(1)} fusion(bf16[768,2304]{1,0:T(8,128)(2,1)} %param.21, f32[128,768]{1,0:T(8,128)S(1)} %get-tuple-element.12, f32[768]{0:T(1024)S(1)} %copy-done.7, f32[128]{0:T(128)S(1)} %add_rsqrt_fusion.2, f32[128]{0:T(128)S(1)} %broadcast_multiply_fusion.2), kind=kOutput, calls=%fused_computation.32 | convolution fusion | flops 151388160 | bytes 1970176
  43.0 1.0 fusion.100
  45.9 3.0 %fusion.12 = f32[1024,1536]{0,1:S(1)} fusion(bf16[768,2304]{1,0:T(8,128)(2,1)S(1)} %copy-done.5, f32[1024,768]{1,0:T(8,128)S(1)} %get-tuple-element.14, f32[768]{0:T(1024)S(1)} %copy-done.7, f32[1024]{0:T(1024)S(1)} %add_rsqrt_fusion, f32[1024]{0:T(1024)S(1)} %broadcast_multiply_fusion), kind=kOutput, calls=%fused_computation.21 | convolution fusion | flops 2419064832 | bytes 11808768
  49.5 1.1 multiply_reduce_fusion
  50.6 1.3 %fusion = f32[12,128]{1,0:T(8,128)S(1)} fusion(f32[12,128,1024]{2,1,0:T(8,128)S(1)} %get-tuple-element.44, f32[12,128]{1,0:T(8,128)S(1)} %get-tuple-element.43), kind=kLoop, calls=%fused_computation.5 | loop fusion | flops 4717056 | bytes 6303744 | tf_op jit(solution)/shard_map/reduce_sum | solution.py:167
  51.9 1.8 %fusion.24 = f32[128,12,64]{0,2,1:T(8,128)S(1)} fusion(f32[12,128,1024]{2,1,0:T(8,128)S(1)} %get-tuple-element.44, f32[12,128]{1,0:T(8,128)S(1)} %get-tuple-element.43, bf16[2,12,1024,64]{2,3,1,0:T(8,128)(2,1)S(1)} %convert_bitcast_fusion, f32[128,12]{0,1:T(8,128)S(1)} %bitcast.223), kind=kOutput, calls=%fused_computation.36 | convolution fusion | flops 206143488 | bytes 8273920 | tf_op jit(solution)/shard_map/hqk,hkd->qhd/dot_general | solution.py:168
  54.9 1.3 fusion.7
  57.9 1.0 fusion.51
  59.8 0.8 fusion.92
  60.6 16.1 %collective-permute-start.5 = (bf16[4,1,2048]{2,1,0:T(2,128)(2,1)S(1)}, bf16[4,1,2048]{2,1,0:T(2,128)(2,1)S(1)}, u32[]{:S(2)}, u32[]{:S(2)}) collective-permute-start(bf16[4,1,2048]{2,1,0:T(2,128)(2,1)S(1)} %slice.571), channel_id=1, source_target_pairs={{0,496},{16,0},{32,16},{48,32},{64,48},{80,64},{96,80},{112,96},{1... | collective-permute-start | bytes 49160 | tf_op jit(solution)/shard_map/ppermute | solution.py:54
  76.8 2.2 %collective-permute-start.4 = (bf16[1,4,2048]{2,1,0:T(4,128)(2,1)S(1)}, bf16[1,4,2048]{2,1,0:T(4,128)(2,1)S(1)}, u32[]{:S(2)}, u32[]{:S(2)}) collective-permute-start(bf16[1,4,2048]{2,1,0:T(4,128)(2,1)S(1)} %slice.569), channel_id=1, source_target_pairs={{0,15},{1,0},{2,1},{3,2},{4,3},{5,4},{6,5},{7,6},{8,7},{9,8},{10,9... | collective-permute-start | bytes 49160 | tf_op jit(solution)/shard_map/ppermute | solution.py:54
  80.8 1.4 %collective-permute-done.4 = bf16[1,4,2048]{2,1,0:T(4,128)(2,1)S(1)} collective-permute-done((bf16[1,4,2048]{2,1,0:T(4,128)(2,1)S(1)}, bf16[1,4,2048]{2,1,0:T(4,128)(2,1)S(1)}, u32[]{:S(2)}, u32[]{:S(2)}) %collective-permute-start.4) | collective-permute-done | bytes 16416 | tf_op jit(solution)/shard_map/ppermute | solution.py:54
  82.2 1.6 %fusion.90 = (f32[]{:T(128)}, f32[4,4,2048]{2,1,0:T(4,128)}, f32[4,4,2048]{2,1,0:T(4,128)}, f32[4,4,2048]{2,1,0:T(4,128)}) fusion(f32[4,4,2048]{2,1,0:T(4,128)S(1)} %get-tuple-element.8, f32[4,4,1]{2,1,0:T(4,128)S(1)} %slice.577, f32[4,4,2047]{2,1,0:T(4,128)S(1)} %slice.576, f32[4,4,1985]{2,1,0:T(4,128)S(1)} %bitcast.207, f32[4,4,63]{2,1,0:T(4,128)S(1)} %slice.574, ...), kind=kLoop, calls=%fused_computation.211 | loop fusion | flops 720895 | bytes 1198084 | tf_op jit(solution)/shard_map/reduce_sum | solution.py:222
  84.6 40.0 %all_to_all.6 = f32[512,1,2]{2,1,0:T(1,128)S(1)} all-to-all(f32[512,1,2]{2,1,0:T(1,128)S(1)} %broadcast_in_dim.74), channel_id=1, replica_groups=mesh['space'=32,'tm'=16] {'space','tm'}, dimensions={0} | all-to-all | bytes 8192 | tf_op jit(solution)/shard_map/all_to_all | solution.py:225
  (176 shorter events, 15.9 us)
Async XLA Ops:
  0.6 53.6 %copy-start = (bf16[768,512]{1,0:T(8,128)(2,1)S(1)}, bf16[768,512]{1,0:T(8,128)(2,1)}, u32[]{:S(2)}) copy-start(bf16[768,512]{1,0:T(8,128)(2,1)} %param.23) | copy-start | bytes 2359300
  3.0 13.9 %copy-start.13 = (s32[1,1,128]{2,1,0:T(1,128)S(1)}, s32[1,1,128]{2,1,0:T(1,128)}, u32[]{:S(2)}) copy-start(s32[1,1,128]{2,1,0:T(1,128)} %param.16) | copy-start | bytes 1540
  4.1 13.1 %copy-start.11 = (s32[128]{0:T(128)S(1)}, s32[128]{0:T(128)}, u32[]{:S(2)}) copy-start(s32[128]{0:T(128)} %constant.150) | copy-start | bytes 1540
  4.1 13.1 %copy-start.12 = (s32[128]{0:T(128)S(1)}, s32[128]{0:T(128)}, u32[]{:S(2)}) copy-start(s32[128]{0:T(128)} %constant.151) | copy-start | bytes 1540
  4.1 13.1 %copy-start.2 = (bf16[256,768]{1,0:T(8,128)(2,1)S(1)}, bf16[256,768]{1,0:T(8,128)(2,1)}, u32[]{:S(2)}) copy-start(bf16[256,768]{1,0:T(8,128)(2,1)} %param.18) | copy-start | bytes 1179652
  7.2 12.1 %copy-start.6 = (f32[768]{0:T(1024)S(1)}, f32[768]{0:T(1024)}, u32[]{:S(2)}) copy-start(f32[768]{0:T(1024)} %param.19) | copy-start | bytes 9220
  7.2 12.7 %collective-permute-start = (bf16[1,129,128]{2,1,0:T(8,128)(2,1)S(1)}, bf16[1,129,128]{2,1,0:T(8,128)(2,1)S(1)}, u32[]{:S(2)}, u32[]{:S(2)}) collective-permute-start(bf16[1,129,128]{2,1,0:T(8,128)(2,1)S(1)} %maximum_bitcast_fusion), channel_id=1, source_target_pairs={{0,8},{1,9},{2,10},{3,11},{4,12},{5,13},{6,14},{7,15},{8,0},{9,1},... | collective-permute-start | bytes 99080 | tf_op jit(solution)/shard_map/ppermute | solution.py:26
  17.2 2.5 %copy-start.9 = (s32[16,8]{0,1:T(8,128)S(1)}, s32[16,8]{0,1:T(8,128)}, u32[]{:S(2)}) copy-start(s32[16,8]{0,1:T(8,128)} %param.17) | copy-start | bytes 1540
  18.0 12.0 %copy-start.10 = (f32[512]{0:T(512)S(1)}, f32[512]{0:T(512)}, u32[]{:S(2)}) copy-start(f32[512]{0:T(512)} %param.24) | copy-start | bytes 6148
  18.0 12.3 %copy-start.1 = (s32[16]{0:T(128)S(1)}, s32[16]{0:T(128)}, u32[]{:S(2)}) copy-start(s32[16]{0:T(128)} %constant.145.clone) | copy-start | bytes 196
  18.1 22.3 %copy-start.7 = (f32[768]{0:T(1024)S(1)}, f32[768]{0:T(1024)}, u32[]{:S(2)}) copy-start(f32[768]{0:T(1024)} %param.20) | copy-start | bytes 9220
  19.9 6.6 %collective-permute-start.1 = (bf16[2,129,128]{2,1,0:T(8,128)(2,1)S(1)}, bf16[2,129,128]{2,1,0:T(8,128)(2,1)S(1)}, u32[]{:S(2)}, u32[]{:S(2)}) collective-permute-start(bf16[2,129,128]{2,1,0:T(8,128)(2,1)S(1)} %pad_maximum_fusion.4), channel_id=1, source_target_pairs={{0,4},{1,5},{2,6},{3,7},{4,0},{5,1},{6,2},{7,3},{8,12},{9,13},{10,... | collective-permute-start | bytes 198152 | tf_op jit(solution)/shard_map/ppermute | solution.py:26
  26.5 6.0 %collective-permute-start.2 = (bf16[4,129,128]{2,1,0:T(8,128)(2,1)S(1)}, bf16[4,129,128]{2,1,0:T(8,128)(2,1)S(1)}, u32[]{:S(2)}, u32[]{:S(2)}) collective-permute-start(bf16[4,129,128]{2,1,0:T(8,128)(2,1)S(1)} %pad_maximum_fusion.1), channel_id=1, source_target_pairs={{0,2},{1,3},{2,0},{3,1},{4,6},{5,7},{6,4},{7,5},{8,10},{9,11},{10,... | collective-permute-start | bytes 396296 | tf_op jit(solution)/shard_map/ppermute | solution.py:26
  32.5 9.8 %collective-permute-start.3 = (bf16[8,129,128]{2,1,0:T(8,128)(2,1)S(1)}, bf16[8,129,128]{2,1,0:T(8,128)(2,1)S(1)}, u32[]{:S(2)}, u32[]{:S(2)}) collective-permute-start(bf16[8,129,128]{2,1,0:T(8,128)(2,1)S(1)} %pad_maximum_fusion), channel_id=1, source_target_pairs={{0,1},{1,0},{2,3},{3,2},{4,5},{5,4},{6,7},{7,6},{8,9},{9,8},{10,11... | collective-permute-start | bytes 792584 | tf_op jit(solution)/shard_map/ppermute | solution.py:26
  43.9 2.0 %copy-start.5 = (bf16[768,2304]{1,0:T(8,128)(2,1)S(1)}, bf16[768,2304]{1,0:T(8,128)(2,1)}, u32[]{:S(2)}) copy-start(bf16[768,2304]{1,0:T(8,128)(2,1)} %param.21) | copy-start | bytes 10616836
  51.9 2.3 %copy-start.8 = (f32[768]{0:T(1024)S(1)}, f32[768]{0:T(1024)}, u32[]{:S(2)}) copy-start(f32[768]{0:T(1024)} %param.22) | copy-start | bytes 9220
  57.4 2.4 %copy-start.4 = (f32[4,4,2048]{2,1,0:T(4,128)S(1)}, f32[4,4,2048]{2,1,0:T(4,128)}, u32[]{:S(2)}) copy-start(f32[4,4,2048]{2,1,0:T(4,128)} %param.15) | copy-start | bytes 393220
  60.6 67.1 %copy-start.3 = (f32[4,4,2048]{2,1,0:T(4,128)}, f32[4,4,2048]{2,1,0:T(4,128)S(1)}, u32[]{:S(2)}) copy-start(f32[4,4,2048]{2,1,0:T(4,128)S(1)} %get-tuple-element.8) | copy-start | bytes 393220
  60.6 20.1 %collective-permute-start.5 = (bf16[4,1,2048]{2,1,0:T(2,128)(2,1)S(1)}, bf16[4,1,2048]{2,1,0:T(2,128)(2,1)S(1)}, u32[]{:S(2)}, u32[]{:S(2)}) collective-permute-start(bf16[4,1,2048]{2,1,0:T(2,128)(2,1)S(1)} %slice.571), channel_id=1, source_target_pairs={{0,496},{16,0},{32,16},{48,32},{64,48},{80,64},{96,80},{112,96},{1... | collective-permute-start | bytes 49160 | tf_op jit(solution)/shard_map/ppermute | solution.py:54
  76.8 5.4 %collective-permute-start.4 = (bf16[1,4,2048]{2,1,0:T(4,128)(2,1)S(1)}, bf16[1,4,2048]{2,1,0:T(4,128)(2,1)S(1)}, u32[]{:S(2)}, u32[]{:S(2)}) collective-permute-start(bf16[1,4,2048]{2,1,0:T(4,128)(2,1)S(1)} %slice.569), channel_id=1, source_target_pairs={{0,15},{1,0},{2,1},{3,2},{4,3},{5,4},{6,5},{7,6},{8,7},{9,8},{10,9... | collective-permute-start | bytes 49160 | tf_op jit(solution)/shard_map/ppermute | solution.py:54
